TPU v7x, 32 devices: a whole 2x2x4 slice. The times are simulated.
32 devices in a mesh: seq: 8 (over z, y), head: 4 (over x, core).
Axes of the slice: x: 2, y: 2, z: 4, core: 2. Of those that a mesh axis runs over, the one named last changes fastest.
Arguments:
- query: bfloat16 [12288, 3072], P(('seq', 'head')), may hold values from -40 to 40
- key: bfloat16 [12288, 3072], P(('seq', 'head')), may hold values from -4 to 4
- value: bfloat16 [12288, 3072], P(('seq', 'head')), may hold values from -6 to 6
- raster_to_tile: int32 [12288], P(('seq', 'head')), may hold values from 0 to 12287, as said below
- window_list: int32 [32, 4], P('seq'), may hold values from 0 to 31, as said below
- valid_count: int32 [32], replicated, may hold values from 96 to 384
Outputs:
- attended: bfloat16 [12288, 3072], P(('seq', 'head'))
Inputs may be any that keep to these rules, and one draw needn't show every extreme that they name: `raster_to_tile`: A permutation of the slots. Raster shard d (rows d * 1536 // 4 onward, d counting seq+head) holds exactly 48 slots of every owner o, where owner o holds slots o * 1536 to (o+1) * 1536 - 1. `window_list`: row t holds t first, then 4 - 1 distinct other tiles, each within 3 tiles of t.
All inputs are finite; a program needn't handle non-finite values.
Results may differ from a plain program's by a relative error of at most 0.0036.
Values may be sent and summed in bfloat16 or wider, within the bound.
No kernel may reach another device: no remote copies, remote signals or barrier semaphores. Data moves between devices by JAX's collectives and lax.ppermute only.
A program may use at most 128 MiB of HBM per device.

v0:
```python
import functools

import jax
import jax.numpy as jnp
from jax import lax
from jax.experimental import pallas as pl
from jax.experimental.pallas import tpu as pltpu
from jax.sharding import PartitionSpec as P

HEAD_DIM = 128


def attn_kernel(win, tile, scale, win_ref, vcw_ref, vco_ref, q_ref, *refs):
    k_refs = refs[:win]
    v_refs = refs[win : 2 * win]
    o_ref = refs[2 * win]
    s_scr = refs[2 * win + 1]
    i = pl.program_id(0)
    q = q_ref[...]
    col = lax.broadcasted_iota(jnp.int32, (tile, tile), 1)
    for w in range(win):
        s = lax.dot_general(
            q, k_refs[w][...], (((1,), (1,)), ((), ())), preferred_element_type=jnp.float32
        )
        s = s * scale
        s = jnp.where(col < vcw_ref[i * win + w], s, -jnp.inf)
        s_scr[:, w * tile : (w + 1) * tile] = s
    s = s_scr[...]
    m = jnp.max(s, axis=1, keepdims=True)
    p = jnp.exp(s - m)
    total = jnp.sum(p, axis=1, keepdims=True)
    pb = p.astype(jnp.bfloat16)
    acc = jnp.dot(pb[:, 0:tile], v_refs[0][...], preferred_element_type=jnp.float32)
    for w in range(1, win):
        acc = acc + jnp.dot(
            pb[:, w * tile : (w + 1) * tile], v_refs[w][...], preferred_element_type=jnp.float32
        )
    out = acc / total
    row = lax.broadcasted_iota(jnp.int32, (tile, 1), 0)
    out = jnp.where(row < vco_ref[i], out, 0.0)
    o_ref[...] = out.astype(o_ref.dtype)


def attention(q_tile, kv_ext, win_flat, vcw_flat, vc_own, tile, win, heads_here):
    tok_dev, pw = q_tile.shape
    tile_dev = tok_dev // tile
    scale = HEAD_DIM ** (-0.5)

    def q_map(i, j, w_ref, a_ref, b_ref):
        return (i, j)

    def k_map(w, i, j, w_ref, a_ref, b_ref):
        return (w_ref[i * win + w], j)

    def v_map(w, i, j, w_ref, a_ref, b_ref):
        return (w_ref[i * win + w], heads_here + j)

    blk = (tile, HEAD_DIM)
    in_specs = [pl.BlockSpec(blk, q_map)]
    in_specs += [pl.BlockSpec(blk, functools.partial(k_map, w)) for w in range(win)]
    in_specs += [pl.BlockSpec(blk, functools.partial(v_map, w)) for w in range(win)]
    steps = tile_dev * heads_here
    cost = pl.CostEstimate(
        flops=steps * 4 * tile * win * tile * HEAD_DIM,
        transcendentals=steps * tile * win * tile,
        bytes_accessed=steps * (2 * win + 2) * tile * HEAD_DIM * 2,
    )
    return pl.pallas_call(
        functools.partial(attn_kernel, win, tile, scale),
        out_shape=jax.ShapeDtypeStruct((tok_dev, pw), jnp.bfloat16),
        grid_spec=pltpu.PrefetchScalarGridSpec(
            num_scalar_prefetch=3,
            grid=(tile_dev, heads_here),
            in_specs=in_specs,
            out_specs=pl.BlockSpec(blk, q_map),
            scratch_shapes=[pltpu.VMEM((tile, win * tile), jnp.float32)],
        ),
        cost_estimate=cost,
    )(win_flat, vcw_flat, vc_own, q_tile, *([kv_ext] * (2 * win)))


def pack_kernel(head_count, part_width, chunk_width, c, q_ref, k_ref, v_ref, o_ref):
    for h in range(head_count):
        base = h * part_width + c * chunk_width
        for t, x_ref in enumerate((q_ref, k_ref, v_ref)):
            o_ref[h, :, t * chunk_width : (t + 1) * chunk_width] = x_ref[:, base : base + chunk_width]


def pack(xs, c, seq_count, head_count, share, chunk_width):
    rows_here, width = xs[0].shape
    part_width = width // head_count
    return pl.pallas_call(
        functools.partial(pack_kernel, head_count, part_width, chunk_width, c),
        out_shape=jax.ShapeDtypeStruct((seq_count * head_count, share, 3 * chunk_width), xs[0].dtype),
        grid=(seq_count,),
        in_specs=[pl.BlockSpec((share, width), lambda s: (s, 0))] * 3,
        out_specs=pl.BlockSpec((head_count, share, 3 * chunk_width), lambda s: (s, 0, 0)),
        cost_estimate=pl.CostEstimate(
            flops=0, transcendentals=0, bytes_accessed=2 * 3 * rows_here * head_count * chunk_width * 2
        ),
    )(*xs)


def body(pos_of_owner, query, key, value, raster_to_tile, window_list, valid_count):
    seq_count = lax.axis_size("seq")
    head_count = lax.axis_size("head")
    seq_pos = lax.axis_index("seq")
    rows_here, width = query.shape
    part_width = width // head_count
    tile_dev, win = window_list.shape
    tok_dev = rows_here * head_count
    tile = tok_dev // tile_dev
    share = rows_here // seq_count
    reach = win - 1
    rim = reach * tile
    ext_tiles = tile_dev + 2 * reach
    heads_here = part_width // HEAD_DIM
    all_tiles = valid_count.shape[0]
    chunks = 2 if heads_here % 2 == 0 else 1
    chunk_heads = heads_here // chunks
    chunk_width = chunk_heads * HEAD_DIM
    devices = seq_count * head_count

    owner_at = [0] * seq_count
    for o, d in enumerate(pos_of_owner):
        owner_at[d] = o
    order = jnp.argsort(raster_to_tile)
    send_order = order.reshape(seq_count, share)[jnp.array(owner_at, jnp.int32)].reshape(rows_here)
    slots_sorted = raster_to_tile[send_order].reshape(seq_count, share)
    slot_send = jnp.broadcast_to(slots_sorted[:, None, :], (seq_count, head_count, share))
    slot_in = lax.all_to_all(
        slot_send.reshape(devices, share), ("seq", "head"), split_axis=0, concat_axis=0, tiled=True
    ).reshape(tok_dev)
    my_owner = jnp.array(owner_at, jnp.int32)[seq_pos]
    local = slot_in - my_owner * tok_dev
    place = jnp.zeros((tok_dev,), jnp.int32).at[local].set(jnp.arange(tok_dev, dtype=jnp.int32))

    window_mine = lax.ppermute(
        window_list, "seq", [(o, pos_of_owner[o]) for o in range(seq_count)]
    )
    first_tile = my_owner * tile_dev - reach
    global_tiles = jnp.clip(first_tile + jnp.arange(ext_tiles, dtype=jnp.int32), 0, all_tiles - 1)
    vc_ext = valid_count[global_tiles]
    local_windows = (window_mine - first_tile).astype(jnp.int32)
    win_flat = local_windows.reshape(tile_dev * win)
    vcw_flat = vc_ext[local_windows].reshape(tile_dev * win)
    vc_own = vc_ext[reach : reach + tile_dev]

    to_right = [(pos_of_owner[o], pos_of_owner[o + 1]) for o in range(seq_count - 1)]
    to_left = [(pos_of_owner[o + 1], pos_of_owner[o]) for o in range(seq_count - 1)]

    packable = share % 16 == 0
    if packable:
        rows_flat = [x[send_order] for x in (query, key, value)]
    else:
        rows_sorted = [
            x[send_order].reshape(seq_count, share, head_count, chunks, chunk_width)
            for x in (query, key, value)
        ]
    arrived = []
    for c in range(chunks):
        if packable:
            send = pack(rows_flat, c, seq_count, head_count, share, chunk_width)
        else:
            send = jnp.concatenate([x[:, :, :, c, :] for x in rows_sorted], axis=3)
            send = jnp.swapaxes(send, 1, 2).reshape(devices, share, 3 * chunk_width)
        got = lax.all_to_all(send, ("seq", "head"), split_axis=0, concat_axis=0, tiled=True)
        got_tile = got.reshape(tok_dev, 3 * chunk_width)[place]
        q_tile = got_tile[:, :chunk_width]
        kv_tile = got_tile[:, chunk_width:]
        from_left = lax.ppermute(kv_tile[tok_dev - rim :], "seq", to_right)
        from_right = lax.ppermute(kv_tile[:rim], "seq", to_left)
        kv_ext = jnp.concatenate([from_left, kv_tile, from_right], axis=0)
        out_tile = attention(q_tile, kv_ext, win_flat, vcw_flat, vc_own, tile, win, chunk_heads)
        outgoing = out_tile[local].reshape(devices, share, chunk_width)
        back = lax.all_to_all(outgoing, ("seq", "head"), split_axis=0, concat_axis=0, tiled=True)
        arrived.append(back.reshape(seq_count, head_count, share, 1, chunk_width))
    arrived = jnp.concatenate(arrived, axis=3)
    sorted_rows = jnp.swapaxes(arrived, 1, 2).reshape(rows_here, width)
    inverse = (
        jnp.zeros((rows_here,), jnp.int32).at[send_order].set(jnp.arange(rows_here, dtype=jnp.int32))
    )
    return sorted_rows[inverse]


def snake(mesh):
    seq_count = mesh.shape["seq"]
    first = mesh.devices.reshape(seq_count, -1)[:, 0]
    try:
        spots = [tuple(d.coords) for d in first]
    except AttributeError:
        spots = [(0, d % 2, d // 2) for d in range(seq_count)]
    low_z = min(c[2] for c in spots)

    def rank(d):
        x, y, z = spots[d][:3]
        return (z, y if (z - low_z) % 2 == 0 else -y, x)

    return tuple(sorted(range(seq_count), key=rank))


def solution(mesh):
    placed = (
        P(("seq", "head"), None),
        P(("seq", "head"), None),
        P(("seq", "head"), None),
        P(("seq", "head")),
        P("seq", None),
        P(),
    )
    return jax.shard_map(
        functools.partial(body, snake(mesh)), mesh=mesh, in_specs=placed, out_specs=P(("seq", "head"), None), check_vma=False
    )
```

profile of v0, /device:TPU:0, one launch (start us, length us, event | category | flops | bytes accessed | tf_op | source)
XLA Modules:
  0.0 377.2 jit_solution(9777853040523437814)
XLA Ops:
  0.0 4.6 %sort.17 = (s32[384]{0:T(512)}, s32[384]{0:T(512)S(1)}) sort(s32[384]{0:T(512)} %param.11, s32[384]{0:T(512)S(1)} %iota.15), dimensions={0}, to_apply=%region_0.0 | sort | flops 3456 | bytes 6144 | tf_op jit(solution)/shard_map/jit(argsort)/sort | solution.py:127
  6.6 3.6 gather_fusion.6
  10.9 7.3 %all-to-all-start.1 = ((s32[32,1,48]{2,1,0:T(1,128)}), s32[32,1,48]{2,1,0:T(1,128)S(1)}, u32[]{:S(2)}, u32[]{:S(2)}) async-start(s32[32,1,48]{2,1,0:T(1,128)} %bitcast.3), calls=%async_computation.1 | async-start | bytes 32768 | tf_op jit(solution)/shard_map/all_to_all | solution.py:131
  18.2 3.6 gather_fusion.5
  21.8 8.9 %gather_fusion.4 = bf16[384,3072]{1,0:T(8,128)(2,1)} fusion(bf16[384,3072]{1,0:T(8,128)(2,1)} %param.9, s32[1024]{0:T(1024)S(1)} %pad_clamp_fusion.3), kind=kCustom, calls=%fused_computation.4 | custom fusion | bytes 4720128 | tf_op jit(solution)/shard_map/gather | solution.py:154
  30.7 3.6 gather_fusion.3
  34.3 7.0 %shard_map.82 = bf16[32,48,1152]{2,1,0:T(8,128)(2,1)} custom-call(bf16[384,3072]{1,0:T(8,128)(2,1)} %gather_fusion.3, bf16[384,3072]{1,0:T(8,128)(2,1)} %gather_fusion.4, bf16[384,3072]{1,0:T(8,128)(2,1)} %gather_fusion.5), custom_call_target="tpu_custom_call" | custom-call | bytes 7077888 | tf_op jit(solution)/shard_map/pallas_call | solution.py:92
  41.9 5.9 %all-to-all-start = ((bf16[32,48,1152]{2,1,0:T(8,128)(2,1)}), bf16[32,48,1152]{2,1,0:T(8,128)(2,1)}, u32[]{:S(2)}, u32[]{:S(2)}) async-start(bf16[32,48,1152]{2,1,0:T(8,128)(2,1)} %shard_map.82), calls=%async_computation | async-start | bytes 7077888 | tf_op jit(solution)/shard_map/all_to_all | solution.py:167
  47.8 7.0 %shard_map.84 = bf16[32,48,1152]{2,1,0:T(8,128)(2,1)} custom-call(bf16[384,3072]{1,0:T(8,128)(2,1)} %gather_fusion.3, bf16[384,3072]{1,0:T(8,128)(2,1)} %gather_fusion.4, bf16[384,3072]{1,0:T(8,128)(2,1)} %gather_fusion.5), custom_call_target="tpu_custom_call" | custom-call | bytes 7077888 | tf_op jit(solution)/shard_map/pallas_call | solution.py:92
  54.8 72.7 %all-to-all-done = bf16[32,48,1152]{2,1,0:T(8,128)(2,1)} async-done(((bf16[32,48,1152]{2,1,0:T(8,128)(2,1)}), bf16[32,48,1152]{2,1,0:T(8,128)(2,1)}, u32[]{:S(2)}, u32[]{:S(2)}) %all-to-all-start) | async-done | bytes 3538976 | tf_op jit(solution)/shard_map/all_to_all | solution.py:167
  127.6 4.1 %all-to-all-start.3 = ((bf16[32,48,1152]{2,1,0:T(8,128)(2,1)}), bf16[32,48,1152]{2,1,0:T(8,128)(2,1)S(1)}, u32[]{:S(2)}, u32[]{:S(2)}) async-start(bf16[32,48,1152]{2,1,0:T(8,128)(2,1)} %shard_map.84), calls=%async_computation.3 | async-start | bytes 7077888 | tf_op jit(solution)/shard_map/all_to_all | solution.py:167
  135.6 6.3 %scatter_custom_fusion = s32[1536]{0:T(1024)S(1)} fusion(s32[1536]{0:T(1024)S(1)} %fusion, s32[1536]{0:T(1024)} %iota.16, s32[]{:T(128)} %constant.15.clone.1), kind=kCustom, calls=%fused_computation.31 | custom fusion | bytes 6656 | tf_op jit(solution)/shard_map/scatter | solution.py:136
  142.6 10.9 %gather_fusion.7 = bf16[1536,1152]{1,0:T(8,128)(2,1)} fusion(bf16[1536,1152]{1,0:T(8,128)(2,1)} %bitcast.2, s32[2048]{0:T(1024)S(1)} %pad_clamp_fusion.1), kind=kCustom, calls=%fused_computation.7 | custom fusion | bytes 7084032 | tf_op jit(solution)/shard_map/gather | solution.py:168
  153.5 4.0 %fusion.7 = (bf16[1152,768]{1,0:T(8,128)(2,1)}, bf16[1152,768]{1,0:T(8,128)(2,1)}) fusion(bf16[1536,1152]{1,0:T(8,128)(2,1)} %gather_fusion.7), kind=kLoop, calls=%fused_computation.39 | loop fusion | bytes 7077888 | tf_op jit(solution)/shard_map/slice | solution.py:171
  157.5 4.9 %collective-permute-start.1 = (bf16[1152,768]{1,0:T(8,128)(2,1)}, bf16[1152,768]{1,0:T(8,128)(2,1)}, u32[]{:S(2)}, u32[]{:S(2)}) collective-permute-start(bf16[1152,768]{1,0:T(8,128)(2,1)} %get-tuple-element.9), channel_id=1, source_target_pairs={{0,4},{4,12},{12,8},{8,16},{16,20},{20,28},{28,24},{1,5},{5,13},{1... | collective-permute-start | bytes 5308424 | tf_op jit(solution)/shard_map/ppermute | solution.py:171
  172.0 40.0 %all-to-all-done.3 = bf16[32,48,1152]{2,1,0:T(8,128)(2,1)S(1)} async-done(((bf16[32,48,1152]{2,1,0:T(8,128)(2,1)}), bf16[32,48,1152]{2,1,0:T(8,128)(2,1)S(1)}, u32[]{:S(2)}, u32[]{:S(2)}) %all-to-all-start.3) | async-done | bytes 3538976 | tf_op jit(solution)/shard_map/all_to_all | solution.py:167
  212.0 6.0 %gather_fusion.9 = bf16[1536,1152]{1,0:T(8,128)(2,1)} fusion(bf16[1536,1152]{1,0:T(8,128)(2,1)S(1)} %bitcast.15, s32[2048]{0:T(1024)S(1)} %copy-done.6), kind=kCustom, calls=%fused_computation.9 | custom fusion | bytes 7084032 | tf_op jit(solution)/shard_map/gather | solution.py:168
  218.1 4.2 %fusion.8 = (bf16[1152,768]{1,0:T(8,128)(2,1)}, bf16[1152,768]{1,0:T(8,128)(2,1)}) fusion(bf16[1536,1152]{1,0:T(8,128)(2,1)} %gather_fusion.9), kind=kLoop, calls=%fused_computation.40 | loop fusion | bytes 7077888 | tf_op jit(solution)/shard_map/slice | solution.py:171
  222.2 3.9 %collective-permute-start.3 = (bf16[1152,768]{1,0:T(8,128)(2,1)}, bf16[1152,768]{1,0:T(8,128)(2,1)}, u32[]{:S(2)}, u32[]{:S(2)}) collective-permute-start(bf16[1152,768]{1,0:T(8,128)(2,1)} %get-tuple-element.11), channel_id=1, source_target_pairs={{0,4},{4,12},{12,8},{8,16},{16,20},{20,28},{28,24},{1,5},{5,13},{1... | collective-permute-start | bytes 5308424 | tf_op jit(solution)/shard_map/ppermute | solution.py:171
  227.5 5.1 %pad_maximum_fusion.refs_0_.refs_1_.refs_2_.refs_3_.refs_4_.refs_5_.refs_6_.refs_7_ = bf16[3840,768]{1,0:T(8,128)(2,1)} fusion(bf16[1152,768]{1,0:T(8,128)(2,1)} %collective-permute-done.2, bf16[1536,768]{1,0:T(8,128)(2,1)S(1)} %slice-done, bf16[1152,768]{1,0:T(8,128)(2,1)} %collective-permute-done.1), kind=kLoop, calls=%fused_computation.14 | loop fusion | flops 17694720 | bytes 11796480 | tf_op jit(solution)/shard_map/concatenate | solution.py:173
  232.6 20.2 %shard_map.83 = bf16[1536,384]{1,0:T(8,128)(2,1)} custom-call(s32[16]{0:T(128)} %reshape.114.win_ref, s32[16]{0:T(128)} %gather_fusion.1, s32[4]{0:T(128)} %slice.31.vco_ref, bf16[1536,384]{1,0:T(8,128)(2,1)} %slice.64.q_ref, bf16[3840,768]{1,0:T(8,128)(2,1)} %pad_maximum_fusion.refs_0_.refs_1_.refs_2_.refs_3_.refs_4_.refs_5_.refs_6_.refs_7_, ...), custom_call_target="tpu_custom_call" | custom-call | flops 3623878656 | bytes 11796480 | tf_op jit(solution)/shard_map/pallas_call | solution.py:68
  252.9 6.6 %gather_fusion.8 = bf16[1536,384]{1,0:T(8,128)(2,1)} fusion(bf16[1536,384]{1,0:T(8,128)(2,1)} %shard_map.83, s32[2048]{0:T(1024)S(1)} %pad_clamp_fusion), kind=kCustom, calls=%fused_computation.8 | custom fusion | bytes 2365440 | tf_op jit(solution)/shard_map/gather | solution.py:175
  259.5 24.4 %all-to-all-start.2 = ((bf16[32,48,384]{2,1,0:T(8,128)(2,1)}), bf16[32,48,384]{2,1,0:T(8,128)(2,1)}, u32[]{:S(2)}, u32[]{:S(2)}) async-start(bf16[32,48,384]{2,1,0:T(8,128)(2,1)} %bitcast.16), calls=%async_computation.2 | async-start | bytes 2359296 | tf_op jit(solution)/shard_map/all_to_all | solution.py:176
  286.7 5.1 %pad_maximum_fusion.1.refs_0_.refs_1_.refs_2_.refs_3_.refs_4_.refs_5_.refs_6_.refs_7_ = bf16[3840,768]{1,0:T(8,128)(2,1)} fusion(bf16[1152,768]{1,0:T(8,128)(2,1)} %collective-permute-done.4, bf16[1536,768]{1,0:T(8,128)(2,1)S(1)} %slice-done.1, bf16[1152,768]{1,0:T(8,128)(2,1)} %collective-permute-done.3), kind=kLoop, calls=%fused_computation.15 | loop fusion | flops 17694720 | bytes 11796480 | tf_op jit(solution)/shard_map/concatenate | solution.py:173
  291.8 20.2 %shard_map.85 = bf16[1536,384]{1,0:T(8,128)(2,1)} custom-call(s32[16]{0:T(128)} %reshape.114.win_ref, s32[16]{0:T(128)} %gather_fusion.1, s32[4]{0:T(128)} %slice.31.vco_ref, bf16[1536,384]{1,0:T(8,128)(2,1)} %slice.68.q_ref, bf16[3840,768]{1,0:T(8,128)(2,1)} %pad_maximum_fusion.1.refs_0_.refs_1_.refs_2_.refs_3_.refs_4_.refs_5_.refs_6_.refs_7_, ...), custom_call_target="tpu_custom_call" | custom-call | flops 3623878656 | bytes 11796480 | tf_op jit(solution)/shard_map/pallas_call | solution.py:68
  312.0 6.5 %gather_fusion.10 = bf16[1536,384]{1,0:T(8,128)(2,1)} fusion(bf16[1536,384]{1,0:T(8,128)(2,1)} %shard_map.85, s32[2048]{0:T(1024)S(1)} %pad_clamp_fusion), kind=kCustom, calls=%fused_computation.10 | custom fusion | bytes 2365440 | tf_op jit(solution)/shard_map/gather | solution.py:175
  318.5 5.8 %all-to-all-start.4 = ((bf16[32,48,384]{2,1,0:T(8,128)(2,1)}), bf16[32,48,384]{2,1,0:T(8,128)(2,1)S(1)}, u32[]{:S(2)}, u32[]{:S(2)}) async-start(bf16[32,48,384]{2,1,0:T(8,128)(2,1)} %bitcast.8), calls=%async_computation.4 | async-start | bytes 2359296 | tf_op jit(solution)/shard_map/all_to_all | solution.py:176
  324.3 3.3 scatter_custom_fusion.1
  330.9 22.5 %all-to-all-done.4 = bf16[32,48,384]{2,1,0:T(8,128)(2,1)S(1)} async-done(((bf16[32,48,384]{2,1,0:T(8,128)(2,1)}), bf16[32,48,384]{2,1,0:T(8,128)(2,1)S(1)}, u32[]{:S(2)}, u32[]{:S(2)}) %all-to-all-start.4) | async-done | bytes 1179680 | tf_op jit(solution)/shard_map/all_to_all | solution.py:176
  355.3 6.7 %maximum_bitcast_fusion = bf16[8,48,4,2,384]{4,3,2,1,0:T(2,128)(2,1)} fusion(bf16[8,4,48,1,384]{4,3,1,2,0:T(2,128)(2,1)S(1)} %copy.14, bf16[8,4,48,1,384]{4,3,1,2,0:T(2,128)(2,1)S(1)} %copy.13), kind=kLoop, calls=%fused_computation.16 | loop fusion | flops 4718592 | bytes 4718592 | tf_op jit(solution)/shard_map/transpose | solution.py:179
  362.1 6.3 %reshape.124 = bf16[384,3072]{1,0:T(8,128)(2,1)} reshape(bf16[8,48,4,2,384]{4,3,2,1,0:T(2,128)(2,1)} %maximum_bitcast_fusion) | data formatting | bytes 4718592 | tf_op jit(solution)/shard_map/reshape | solution.py:179
  368.3 8.9 %gather_fusion.11 = bf16[384,3072]{1,0:T(8,128)(2,1)} fusion(bf16[384,3072]{1,0:T(8,128)(2,1)} %reshape.124, s32[1024]{0:T(1024)S(1)} %pad_clamp_fusion.2), kind=kCustom, calls=%fused_computation.11 | custom fusion | bytes 4720128 | tf_op jit(solution)/shard_map/gather | solution.py:183
  (69 shorter events, 25.6 us)
Async XLA Ops:
  0.0 18.2 %copy-start = (bf16[384,3072]{1,0:T(8,128)(2,1)S(1)}, bf16[384,3072]{1,0:T(8,128)(2,1)}, u32[]{:S(2)}) copy-start(bf16[384,3072]{1,0:T(8,128)(2,1)} %param.10) | copy-start | bytes 7077892
  6.0 0.6 copy-start.9
  10.9 30.4 %all-to-all-start.1 = ((s32[32,1,48]{2,1,0:T(1,128)}), s32[32,1,48]{2,1,0:T(1,128)S(1)}, u32[]{:S(2)}, u32[]{:S(2)}) async-start(s32[32,1,48]{2,1,0:T(1,128)} %bitcast.3), calls=%async_computation.1 | async-start | bytes 32768 | tf_op jit(solution)/shard_map/all_to_all | solution.py:131
  21.8 8.9 %copy-start.3 = (bf16[384,3072]{1,0:T(8,128)(2,1)S(1)}, bf16[384,3072]{1,0:T(8,128)(2,1)}, u32[]{:S(2)}) copy-start(bf16[384,3072]{1,0:T(8,128)(2,1)} %param.8) | copy-start | bytes 7077892
  41.3 0.6 copy-start.7
  41.9 85.7 %all-to-all-start = ((bf16[32,48,1152]{2,1,0:T(8,128)(2,1)}), bf16[32,48,1152]{2,1,0:T(8,128)(2,1)}, u32[]{:S(2)}, u32[]{:S(2)}) async-start(bf16[32,48,1152]{2,1,0:T(8,128)(2,1)} %shard_map.82), calls=%async_computation | async-start | bytes 7077888 | tf_op jit(solution)/shard_map/all_to_all | solution.py:167
  54.8 76.8 %copy-start.10 = (s32[8]{0:T(128)S(1)}, s32[8]{0:T(128)}, u32[]{:S(2)}) copy-start(s32[8]{0:T(128)} %constant.38.clone) | copy-start | bytes 100
  127.6 84.5 %all-to-all-start.3 = ((bf16[32,48,1152]{2,1,0:T(8,128)(2,1)}), bf16[32,48,1152]{2,1,0:T(8,128)(2,1)S(1)}, u32[]{:S(2)}, u32[]{:S(2)}) async-start(bf16[32,48,1152]{2,1,0:T(8,128)(2,1)} %shard_map.84), calls=%async_computation.3 | async-start | bytes 7077888 | tf_op jit(solution)/shard_map/all_to_all | solution.py:167
  135.0 7.0 %copy-start.8 = (s32[1536]{0:T(1024)}, s32[1536]{0:T(1024)S(1)}, u32[]{:S(2)}) copy-start(s32[1536]{0:T(1024)S(1)} %fusion) | copy-start | bytes 18436
  142.0 0.6 copy-start.5
  153.5 12.1 %copy-start.2 = (s32[32]{0:T(128)S(1)}, s32[32]{0:T(128)}, u32[]{:S(2)}) copy-start(s32[32]{0:T(128)} %param.13) | copy-start | bytes 388
  157.5 70.0 %collective-permute-start.1 = (bf16[1152,768]{1,0:T(8,128)(2,1)}, bf16[1152,768]{1,0:T(8,128)(2,1)}, u32[]{:S(2)}, u32[]{:S(2)}) collective-permute-start(bf16[1152,768]{1,0:T(8,128)(2,1)} %get-tuple-element.9), channel_id=1, source_target_pairs={{0,4},{4,12},{12,8},{8,16},{16,20},{20,28},{28,24},{1,5},{5,13},{1... | collective-permute-start | bytes 5308424 | tf_op jit(solution)/shard_map/ppermute | solution.py:171
  162.4 65.1 %collective-permute-start.2 = (bf16[1152,768]{1,0:T(8,128)(2,1)}, bf16[1152,768]{1,0:T(8,128)(2,1)}, u32[]{:S(2)}, u32[]{:S(2)}) collective-permute-start(bf16[1152,768]{1,0:T(8,128)(2,1)} %get-tuple-element.10), channel_id=1, source_target_pairs={{4,0},{12,4},{8,12},{16,8},{20,16},{28,20},{24,28},{5,1},{13,5},{9... | collective-permute-start | bytes 5308424 | tf_op jit(solution)/shard_map/ppermute | solution.py:172
  163.7 3.2 collective-permute-start
  172.0 40.0 %copy-start.6 = (s32[2048]{0:T(1024)S(1)}, s32[2048]{0:T(1024)}, u32[]{:S(2)}) copy-start(s32[2048]{0:T(1024)} %copy-done.5) | copy-start | bytes 24580
  218.1 9.5 %slice-start = ((bf16[1536,1152]{1,0:T(8,128)(2,1)}), bf16[1536,768]{1,0:T(8,128)(2,1)S(1)}, s32[]{:S(2)}) async-start(bf16[1536,1152]{1,0:T(8,128)(2,1)} %gather_fusion.7), calls=%async_computation.5 | async-start | bytes 4718592 | tf_op jit(solution)/shard_map/slice | solution.py:170
  222.2 62.8 %collective-permute-start.3 = (bf16[1152,768]{1,0:T(8,128)(2,1)}, bf16[1152,768]{1,0:T(8,128)(2,1)}, u32[]{:S(2)}, u32[]{:S(2)}) collective-permute-start(bf16[1152,768]{1,0:T(8,128)(2,1)} %get-tuple-element.11), channel_id=1, source_target_pairs={{0,4},{4,12},{12,8},{8,16},{16,20},{20,28},{28,24},{1,5},{5,13},{1... | collective-permute-start | bytes 5308424 | tf_op jit(solution)/shard_map/ppermute | solution.py:171
  226.2 58.9 %collective-permute-start.4 = (bf16[1152,768]{1,0:T(8,128)(2,1)}, bf16[1152,768]{1,0:T(8,128)(2,1)}, u32[]{:S(2)}, u32[]{:S(2)}) collective-permute-start(bf16[1152,768]{1,0:T(8,128)(2,1)} %get-tuple-element.12), channel_id=1, source_target_pairs={{4,0},{12,4},{8,12},{16,8},{20,16},{28,20},{24,28},{5,1},{13,5},{9... | collective-permute-start | bytes 5308424 | tf_op jit(solution)/shard_map/ppermute | solution.py:172
  252.9 31.0 %copy-start.4 = (bf16[1536,1152]{1,0:T(8,128)(2,1)S(1)}, bf16[1536,1152]{1,0:T(8,128)(2,1)}, u32[]{:S(2)}) copy-start(bf16[1536,1152]{1,0:T(8,128)(2,1)} %gather_fusion.9) | copy-start | bytes 10616836
  259.5 59.1 %all-to-all-start.2 = ((bf16[32,48,384]{2,1,0:T(8,128)(2,1)}), bf16[32,48,384]{2,1,0:T(8,128)(2,1)}, u32[]{:S(2)}, u32[]{:S(2)}) async-start(bf16[32,48,384]{2,1,0:T(8,128)(2,1)} %bitcast.16), calls=%async_computation.2 | async-start | bytes 2359296 | tf_op jit(solution)/shard_map/all_to_all | solution.py:176
  285.1 1.7 slice-start.1
  318.5 34.8 %all-to-all-start.4 = ((bf16[32,48,384]{2,1,0:T(8,128)(2,1)}), bf16[32,48,384]{2,1,0:T(8,128)(2,1)S(1)}, u32[]{:S(2)}, u32[]{:S(2)}) async-start(bf16[32,48,384]{2,1,0:T(8,128)(2,1)} %bitcast.8), calls=%async_computation.4 | async-start | bytes 2359296 | tf_op jit(solution)/shard_map/all_to_all | solution.py:176
  368.3 8.9 %copy-start.1 = (bf16[384,3072]{1,0:T(8,128)(2,1)S(1)}, bf16[384,3072]{1,0:T(8,128)(2,1)}, u32[]{:S(2)}) copy-start(bf16[384,3072]{1,0:T(8,128)(2,1)} %param.10) | copy-start | bytes 7077892
where the time goes:
time: 379 us; the launch traced here: 377 us
  waiting for transfers between devices  135 us (36%)
  local copies, waits for them, and re-layouts  101 us (27%)
  starting transfers between devices  60.3 us (16%)
  Pallas kernels  54.4 us (14%)
  other arithmetic  24.4 us (6%)
    all_to_all x2, waiting for transfers between devices, body(): lax.all_to_all(send, ('seq', 'head'), split_axis=0, concat_axis=0, tiled=...  113 us
    pallas_call x2, Pallas kernels, attention(): pl.pallas_call(functools.partial(attn_kernel, win, tile, scale), out_shap...  40.4 us
    all_to_all x2, starting transfers between devices, body(): lax.all_to_all(outgoing, ('seq', 'head'), split_axis=0, concat_axis=0, ti...  30.2 us
    all_to_all x2, waiting for transfers between devices, body(): lax.all_to_all(outgoing, ('seq', 'head'), split_axis=0, concat_axis=0, ti...  22.5 us
    gather x2, local copies, waits for them, and re-layouts, body(): got_tile = got.reshape(tok_dev, 3 * chunk_width)[place]  16.9 us
    gather x3, local copies, waits for them, and re-layouts, body(): rows_flat = [x[send_order] for x in (query, key, value)]  16 us
    pallas_call x2, Pallas kernels, pack(): pl.pallas_call(functools.partial(pack_kernel, head_count, part_width, chu...  14 us
    gather x2, local copies, waits for them, and re-layouts, body(): outgoing = out_tile[local].reshape(devices, share, chunk_width)  13.1 us
  transfers between devices with their start and end apart: 10, of which 3 were waited for; matrix products, arithmetic and copies ran while one was open for 23% of the time, Pallas kernels for 14%

commit v1 on v0

--- a/solution.py
+++ b/solution.py
@@ -101,6 +101,29 @@
     )(*xs)
 
 
+def unpack_kernel(head_count, part_width, chunk_width, *refs):
+    o_ref = refs[-1]
+    for c, b_ref in enumerate(refs[:-1]):
+        for h in range(head_count):
+            base = h * part_width + c * chunk_width
+            o_ref[:, base : base + chunk_width] = b_ref[h]
+
+
+def unpack(backs, seq_count, head_count, share, width):
+    devices, _, chunk_width = backs[0].shape
+    part_width = width // head_count
+    return pl.pallas_call(
+        functools.partial(unpack_kernel, head_count, part_width, chunk_width),
+        out_shape=jax.ShapeDtypeStruct((seq_count * share, width), backs[0].dtype),
+        grid=(seq_count,),
+        in_specs=[pl.BlockSpec((head_count, share, chunk_width), lambda s: (s, 0, 0))] * len(backs),
+        out_specs=pl.BlockSpec((share, width), lambda s: (s, 0)),
+        cost_estimate=pl.CostEstimate(
+            flops=0, transcendentals=0, bytes_accessed=2 * seq_count * share * width * 2
+        ),
+    )(*backs)
+
+
 def body(pos_of_owner, query, key, value, raster_to_tile, window_list, valid_count):
     seq_count = lax.axis_size("seq")
     head_count = lax.axis_size("head")
@@ -116,7 +139,7 @@
     ext_tiles = tile_dev + 2 * reach
     heads_here = part_width // HEAD_DIM
     all_tiles = valid_count.shape[0]
-    chunks = 2 if heads_here % 2 == 0 else 1
+    chunks = 3 if heads_here % 3 == 0 else (2 if heads_here % 2 == 0 else 1)
     chunk_heads = heads_here // chunks
     chunk_width = chunk_heads * HEAD_DIM
     devices = seq_count * head_count
@@ -174,9 +197,13 @@
         out_tile = attention(q_tile, kv_ext, win_flat, vcw_flat, vc_own, tile, win, chunk_heads)
         outgoing = out_tile[local].reshape(devices, share, chunk_width)
         back = lax.all_to_all(outgoing, ("seq", "head"), split_axis=0, concat_axis=0, tiled=True)
-        arrived.append(back.reshape(seq_count, head_count, share, 1, chunk_width))
-    arrived = jnp.concatenate(arrived, axis=3)
-    sorted_rows = jnp.swapaxes(arrived, 1, 2).reshape(rows_here, width)
+        arrived.append(back)
+    if packable:
+        sorted_rows = unpack(arrived, seq_count, head_count, share, width)
+    else:
+        arrived = [b.reshape(seq_count, head_count, share, 1, chunk_width) for b in arrived]
+        arrived = jnp.concatenate(arrived, axis=3)
+        sorted_rows = jnp.swapaxes(arrived, 1, 2).reshape(rows_here, width)
     inverse = (
         jnp.zeros((rows_here,), jnp.int32).at[send_order].set(jnp.arange(rows_here, dtype=jnp.int32))
     )

time: 379 us -> 388 us (1.024)
  waiting for transfers between devices: 135 us -> 119 us
  Pallas kernels: 54.4 us -> 68.7 us
  starting transfers between devices: 60.3 us -> 73 us
  other arithmetic: 24.4 us -> 18.3 us
  local copies, waits for them, and re-layouts: 101 us -> 105 us
    all_to_all x2 -> x3, waiting for transfers between devices: 113 us -> 95.5 us  [body(): lax.all_to_all(send, ('seq', 'head'), split_axis=0, concat_axis=0, tiled=...]
    reshape x3 -> x0, local copies, waits for them, and re-layouts: 11.5 us -> none  [the longest x1 6.28 us: body(): sorted_rows = jnp.swapaxes(arrived, 1, 2).reshape(rows_here, width)]
    transpose x1 -> x0, other arithmetic: 6.75 us -> none  [body(): sorted_rows = jnp.swapaxes(arrived, 1, 2).reshape(rows_here, width)]
    gather x2 -> x3, local copies, waits for them, and re-layouts: 16.9 us -> 22.9 us  [body(): got_tile = got.reshape(tok_dev, 3 * chunk_width)[place]]
    pallas_call x2 -> x3, Pallas kernels: 14 us -> 19.9 us  [pack(): pl.pallas_call(functools.partial(pack_kernel, head_count, part_width, chu...]
    pallas_call x0 -> x1, Pallas kernels: none -> 5.92 us  [unpack(): pl.pallas_call(functools.partial(unpack_kernel, head_count, part_width, c...]
    ppermute x2 -> x3, starting transfers between devices: 8.85 us -> 14.1 us  [body(): from_left = lax.ppermute(kv_tile[tok_dev - rim:], 'seq', to_right)]
    all_to_all x2 -> x3, waiting for transfers between devices: 22.5 us -> 17.3 us  [body(): lax.all_to_all(outgoing, ('seq', 'head'), split_axis=0, concat_axis=0, ti...]
  transfers between devices with their start and end apart: 10 -> 14, of which waited for: 3 -> 5; matrix products, arithmetic and copies ran while one was open for 23% -> 26% of each run, Pallas kernels for 14% -> 16%
where the time goes in v1:
time: 388 us; the launch traced here: 386 us
  waiting for transfers between devices  119 us (31%)
  local copies, waits for them, and re-layouts  105 us (27%)
  starting transfers between devices  73 us (19%)
  Pallas kernels  68.7 us (18%)
  other arithmetic  18.3 us (5%)
    all_to_all x3, waiting for transfers between devices, body(): lax.all_to_all(send, ('seq', 'head'), split_axis=0, concat_axis=0, tiled=...  95.5 us
    pallas_call x3, Pallas kernels, attention(): pl.pallas_call(functools.partial(attn_kernel, win, tile, scale), out_shap...  42.9 us
    all_to_all x3, starting transfers between devices, body(): lax.all_to_all(outgoing, ('seq', 'head'), split_axis=0, concat_axis=0, ti...  31.6 us
    gather x3, local copies, waits for them, and re-layouts, body(): got_tile = got.reshape(tok_dev, 3 * chunk_width)[place]  22.9 us
    pallas_call x3, Pallas kernels, pack(): pl.pallas_call(functools.partial(pack_kernel, head_count, part_width, chu...  19.9 us
    gather x3, local copies, waits for them, and re-layouts, body(): outgoing = out_tile[local].reshape(devices, share, chunk_width)  17.4 us
    all_to_all x3, waiting for transfers between devices, body(): lax.all_to_all(outgoing, ('seq', 'head'), split_axis=0, concat_axis=0, ti...  17.3 us
    gather x3, local copies, waits for them, and re-layouts, body(): rows_flat = [x[send_order] for x in (query, key, value)]  16 us
  transfers between devices with their start and end apart: 14, of which 5 were waited for; matrix products, arithmetic and copies ran while one was open for 26% of the time, Pallas kernels for 16%

profile of v1, /device:TPU:0, one launch (start us, length us, event | category | flops | bytes accessed | tf_op | source)
XLA Modules:
  0.0 385.8 jit_solution(15476097116600939639)
XLA Ops:
  0.0 4.6 %sort.17 = (s32[384]{0:T(512)}, s32[384]{0:T(512)S(1)}) sort(s32[384]{0:T(512)} %param.11, s32[384]{0:T(512)S(1)} %iota.15), dimensions={0}, to_apply=%region_0.0 | sort | flops 3456 | bytes 6144 | tf_op jit(solution)/shard_map/jit(argsort)/sort | solution.py:150
  6.6 3.6 gather_fusion.6
  10.9 7.3 %all-to-all-start.1 = ((s32[32,1,48]{2,1,0:T(1,128)}), s32[32,1,48]{2,1,0:T(1,128)S(1)}, u32[]{:S(2)}, u32[]{:S(2)}) async-start(s32[32,1,48]{2,1,0:T(1,128)} %bitcast.3), calls=%async_computation.1 | async-start | bytes 32768 | tf_op jit(solution)/shard_map/all_to_all | solution.py:154
  21.8 8.9 %gather_fusion.4 = bf16[384,3072]{1,0:T(8,128)(2,1)} fusion(bf16[384,3072]{1,0:T(8,128)(2,1)} %param.9, s32[1024]{0:T(1024)S(1)} %pad_clamp_fusion.3), kind=kCustom, calls=%fused_computation.4 | custom fusion | bytes 4720128 | tf_op jit(solution)/shard_map/gather | solution.py:177
  34.2 6.6 %shard_map.84 = bf16[32,48,768]{2,1,0:T(8,128)(2,1)} custom-call(bf16[384,3072]{1,0:T(8,128)(2,1)} %gather_fusion.3, bf16[384,3072]{1,0:T(8,128)(2,1)} %gather_fusion.4, bf16[384,3072]{1,0:T(8,128)(2,1)} %gather_fusion.5), custom_call_target="tpu_custom_call" | custom-call | bytes 4718592 | tf_op jit(solution)/shard_map/pallas_call | solution.py:92
  40.9 5.8 %all-to-all-start.3 = ((bf16[32,48,768]{2,1,0:T(8,128)(2,1)}), bf16[32,48,768]{2,1,0:T(8,128)(2,1)S(1)}, u32[]{:S(2)}, u32[]{:S(2)}) async-start(bf16[32,48,768]{2,1,0:T(8,128)(2,1)} %shard_map.84), calls=%async_computation.3 | async-start | bytes 4718592 | tf_op jit(solution)/shard_map/all_to_all | solution.py:190
  46.7 6.6 %shard_map.82 = bf16[32,48,768]{2,1,0:T(8,128)(2,1)} custom-call(bf16[384,3072]{1,0:T(8,128)(2,1)} %gather_fusion.3, bf16[384,3072]{1,0:T(8,128)(2,1)} %gather_fusion.4, bf16[384,3072]{1,0:T(8,128)(2,1)} %gather_fusion.5), custom_call_target="tpu_custom_call" | custom-call | bytes 4718592 | tf_op jit(solution)/shard_map/pallas_call | solution.py:92
  53.3 47.8 %all-to-all-done.3 = bf16[32,48,768]{2,1,0:T(8,128)(2,1)S(1)} async-done(((bf16[32,48,768]{2,1,0:T(8,128)(2,1)}), bf16[32,48,768]{2,1,0:T(8,128)(2,1)S(1)}, u32[]{:S(2)}, u32[]{:S(2)}) %all-to-all-start.3) | async-done | bytes 2359328 | tf_op jit(solution)/shard_map/all_to_all | solution.py:190
  102.6 4.1 %all-to-all-start = ((bf16[32,48,768]{2,1,0:T(8,128)(2,1)}), bf16[32,48,768]{2,1,0:T(8,128)(2,1)S(1)}, u32[]{:S(2)}, u32[]{:S(2)}) async-start(bf16[32,48,768]{2,1,0:T(8,128)(2,1)} %shard_map.82), calls=%async_computation | async-start | bytes 4718592 | tf_op jit(solution)/shard_map/all_to_all | solution.py:190
  106.7 6.6 %shard_map.86 = bf16[32,48,768]{2,1,0:T(8,128)(2,1)} custom-call(bf16[384,3072]{1,0:T(8,128)(2,1)} %gather_fusion.3, bf16[384,3072]{1,0:T(8,128)(2,1)} %gather_fusion.4, bf16[384,3072]{1,0:T(8,128)(2,1)} %gather_fusion.5), custom_call_target="tpu_custom_call" | custom-call | bytes 4718592 | tf_op jit(solution)/shard_map/pallas_call | solution.py:92
  113.3 47.8 %all-to-all-done = bf16[32,48,768]{2,1,0:T(8,128)(2,1)S(1)} async-done(((bf16[32,48,768]{2,1,0:T(8,128)(2,1)}), bf16[32,48,768]{2,1,0:T(8,128)(2,1)S(1)}, u32[]{:S(2)}, u32[]{:S(2)}) %all-to-all-start) | async-done | bytes 2359328 | tf_op jit(solution)/shard_map/all_to_all | solution.py:190
  162.5 4.1 %all-to-all-start.5 = ((bf16[32,48,768]{2,1,0:T(8,128)(2,1)}), bf16[32,48,768]{2,1,0:T(8,128)(2,1)S(1)}, u32[]{:S(2)}, u32[]{:S(2)}) async-start(bf16[32,48,768]{2,1,0:T(8,128)(2,1)} %shard_map.86), calls=%async_computation.5 | async-start | bytes 4718592 | tf_op jit(solution)/shard_map/all_to_all | solution.py:190
  170.4 6.2 %scatter_custom_fusion = s32[1536]{0:T(1024)S(1)} fusion(s32[1536]{0:T(1024)S(1)} %fusion, s32[1536]{0:T(1024)S(1)} %iota.16, s32[]{:T(128)} %constant.15.clone.1), kind=kCustom, calls=%fused_computation.33 | custom fusion | bytes 6148 | tf_op jit(solution)/shard_map/scatter | solution.py:159
  176.7 8.7 %gather_fusion.9 = bf16[1536,768]{1,0:T(8,128)(2,1)} fusion(bf16[1536,768]{1,0:T(8,128)(2,1)} %bitcast.15, s32[2048]{0:T(1024)S(1)} %pad_clamp_fusion.1), kind=kCustom, calls=%fused_computation.9 | custom fusion | bytes 4724736 | tf_op jit(solution)/shard_map/gather | solution.py:191
  188.6 3.7 collective-permute-start.3
  203.7 8.7 %gather_fusion.7 = bf16[1536,768]{1,0:T(8,128)(2,1)} fusion(bf16[1536,768]{1,0:T(8,128)(2,1)} %bitcast.14, s32[2048]{0:T(1024)S(1)} %pad_clamp_fusion.1), kind=kCustom, calls=%fused_computation.7 | custom fusion | bytes 4724736 | tf_op jit(solution)/shard_map/gather | solution.py:191
  215.6 5.6 %collective-permute-start.1 = (bf16[1152,512]{1,0:T(8,128)(2,1)}, bf16[1152,512]{1,0:T(8,128)(2,1)}, u32[]{:S(2)}, u32[]{:S(2)}) collective-permute-start(bf16[1152,512]{1,0:T(8,128)(2,1)} %get-tuple-element.13), channel_id=1, source_target_pairs={{0,4},{4,12},{12,8},{8,16},{16,20},{20,28},{28,24},{1,5},{5,13},{1... | collective-permute-start | bytes 3538952 | tf_op jit(solution)/shard_map/ppermute | solution.py:194
  222.5 3.8 collective-permute-done.3
  232.2 14.2 %shard_map.85 = bf16[1536,256]{1,0:T(8,128)(2,1)} custom-call(s32[16]{0:T(128)} %reshape.111.win_ref, s32[16]{0:T(128)} %gather_fusion.1, s32[4]{0:T(128)} %slice.45.vco_ref, bf16[1536,256]{1,0:T(8,128)(2,1)} %slice.90.q_ref, bf16[3840,512]{1,0:T(8,128)(2,1)} %pad_maximum_fusion.1.refs_0_.refs_1_.refs_2_.refs_3_.refs_4_.refs_5_.refs_6_.refs_7_, ...), custom_call_target="tpu_custom_call" | custom-call | flops 2415919104 | bytes 7864320 | tf_op jit(solution)/shard_map/pallas_call | solution.py:68
  246.4 5.7 %gather_fusion.10 = bf16[1536,256]{1,0:T(8,128)(2,1)} fusion(bf16[1536,256]{1,0:T(8,128)(2,1)} %shard_map.85, s32[2048]{0:T(1024)S(1)} %pad_clamp_fusion), kind=kCustom, calls=%fused_computation.10 | custom fusion | bytes 1579008 | tf_op jit(solution)/shard_map/gather | solution.py:198
  252.2 20.0 %all-to-all-start.4 = ((bf16[32,48,256]{2,1,0:T(8,128)(2,1)}), bf16[32,48,256]{2,1,0:T(8,128)(2,1)S(1)}, u32[]{:S(2)}, u32[]{:S(2)}) async-start(bf16[32,48,256]{2,1,0:T(8,128)(2,1)} %bitcast.16), calls=%async_computation.4 | async-start | bytes 1572864 | tf_op jit(solution)/shard_map/all_to_all | solution.py:199
  274.2 5.6 %gather_fusion.11 = bf16[1536,768]{1,0:T(8,128)(2,1)} fusion(bf16[1536,768]{1,0:T(8,128)(2,1)S(1)} %bitcast.13, s32[2048]{0:T(1024)S(1)} %pad_clamp_fusion.1), kind=kCustom, calls=%fused_computation.11 | custom fusion | bytes 4724736 | tf_op jit(solution)/shard_map/gather | solution.py:191
  283.2 4.7 %collective-permute-start.5 = (bf16[1152,512]{1,0:T(8,128)(2,1)}, bf16[1152,512]{1,0:T(8,128)(2,1)}, u32[]{:S(2)}, u32[]{:S(2)}) collective-permute-start(bf16[1152,512]{1,0:T(8,128)(2,1)} %get-tuple-element.9), channel_id=1, source_target_pairs={{0,4},{4,12},{12,8},{8,16},{16,20},{20,28},{28,24},{1,5},{5,13},{1... | collective-permute-start | bytes 3538952 | tf_op jit(solution)/shard_map/ppermute | solution.py:194
  292.5 14.4 %shard_map.83 = bf16[1536,256]{1,0:T(8,128)(2,1)} custom-call(s32[16]{0:T(128)} %reshape.111.win_ref, s32[16]{0:T(128)} %gather_fusion.1, s32[4]{0:T(128)} %slice.45.vco_ref, bf16[1536,256]{1,0:T(8,128)(2,1)} %slice.86.q_ref, bf16[3840,512]{1,0:T(8,128)(2,1)} %pad_maximum_fusion.refs_0_.refs_1_.refs_2_.refs_3_.refs_4_.refs_5_.refs_6_.refs_7_, ...), custom_call_target="tpu_custom_call" | custom-call | flops 2415919104 | bytes 7864320 | tf_op jit(solution)/shard_map/pallas_call | solution.py:68
  306.9 6.0 %gather_fusion.8 = bf16[1536,256]{1,0:T(8,128)(2,1)} fusion(bf16[1536,256]{1,0:T(8,128)(2,1)} %shard_map.83, s32[2048]{0:T(1024)S(1)} %copy-done.10), kind=kCustom, calls=%fused_computation.8 | custom fusion | bytes 1579008 | tf_op jit(solution)/shard_map/gather | solution.py:198
  312.9 5.9 %all-to-all-start.2 = ((bf16[32,48,256]{2,1,0:T(8,128)(2,1)}), bf16[32,48,256]{2,1,0:T(8,128)(2,1)}, u32[]{:S(2)}, u32[]{:S(2)}) async-start(bf16[32,48,256]{2,1,0:T(8,128)(2,1)} %bitcast.17), calls=%async_computation.2 | async-start | bytes 1572864 | tf_op jit(solution)/shard_map/all_to_all | solution.py:199
  323.8 14.3 %shard_map.87 = bf16[1536,256]{1,0:T(8,128)(2,1)} custom-call(s32[16]{0:T(128)} %reshape.111.win_ref, s32[16]{0:T(128)} %gather_fusion.1, s32[4]{0:T(128)} %slice.45.vco_ref, bf16[1536,256]{1,0:T(8,128)(2,1)} %slice.94.q_ref, bf16[3840,512]{1,0:T(8,128)(2,1)} %pad_maximum_fusion.2.refs_0_.refs_1_.refs_2_.refs_3_.refs_4_.refs_5_.refs_6_.refs_7_, ...), custom_call_target="tpu_custom_call" | custom-call | flops 2415919104 | bytes 7864320 | tf_op jit(solution)/shard_map/pallas_call | solution.py:68
  338.0 5.7 %gather_fusion.12 = bf16[1536,256]{1,0:T(8,128)(2,1)} fusion(bf16[1536,256]{1,0:T(8,128)(2,1)} %shard_map.87, s32[2048]{0:T(1024)S(1)} %copy-done.10), kind=kCustom, calls=%fused_computation.12 | custom fusion | bytes 1579008 | tf_op jit(solution)/shard_map/gather | solution.py:198
  343.8 5.8 %all-to-all-start.6 = ((bf16[32,48,256]{2,1,0:T(8,128)(2,1)}), bf16[32,48,256]{2,1,0:T(8,128)(2,1)S(1)}, u32[]{:S(2)}, u32[]{:S(2)}) async-start(bf16[32,48,256]{2,1,0:T(8,128)(2,1)} %bitcast.9), calls=%async_computation.6 | async-start | bytes 1572864 | tf_op jit(solution)/shard_map/all_to_all | solution.py:199
  352.9 17.3 %all-to-all-done.6.refs_2_ = bf16[32,48,256]{2,1,0:T(8,128)(2,1)S(1)} async-done(((bf16[32,48,256]{2,1,0:T(8,128)(2,1)}), bf16[32,48,256]{2,1,0:T(8,128)(2,1)S(1)}, u32[]{:S(2)}, u32[]{:S(2)}) %all-to-all-start.6) | async-done | bytes 786464 | tf_op jit(solution)/shard_map/all_to_all | solution.py:199
  371.0 5.9 %shard_map.88 = bf16[384,3072]{1,0:T(8,128)(2,1)} custom-call(bf16[32,48,256]{2,1,0:T(8,128)(2,1)} %all-to-all-done.2.refs_0_, bf16[32,48,256]{2,1,0:T(8,128)(2,1)} %copy-done.7, bf16[32,48,256]{2,1,0:T(8,128)(2,1)} %copy-done.8), custom_call_target="tpu_custom_call" | custom-call | bytes 4718592 | tf_op jit(solution)/shard_map/pallas_call | solution.py:115
  376.9 8.9 %gather_fusion.13 = bf16[384,3072]{1,0:T(8,128)(2,1)} fusion(bf16[384,3072]{1,0:T(8,128)(2,1)} %shard_map.88, s32[1024]{0:T(1024)S(1)} %pad_clamp_fusion.2), kind=kCustom, calls=%fused_computation.13 | custom fusion | bytes 4720128 | tf_op jit(solution)/shard_map/gather | solution.py:210
  (89 shorter events, 59.5 us)
Async XLA Ops:
  0.0 18.2 %copy-start = (bf16[384,3072]{1,0:T(8,128)(2,1)S(1)}, bf16[384,3072]{1,0:T(8,128)(2,1)}, u32[]{:S(2)}) copy-start(bf16[384,3072]{1,0:T(8,128)(2,1)} %param.10) | copy-start | bytes 7077892
  6.0 0.6 copy-start.12
  10.9 30.0 %all-to-all-start.1 = ((s32[32,1,48]{2,1,0:T(1,128)}), s32[32,1,48]{2,1,0:T(1,128)S(1)}, u32[]{:S(2)}, u32[]{:S(2)}) async-start(s32[32,1,48]{2,1,0:T(1,128)} %bitcast.3), calls=%async_computation.1 | async-start | bytes 32768 | tf_op jit(solution)/shard_map/all_to_all | solution.py:154
  21.8 8.9 %copy-start.5 = (bf16[384,3072]{1,0:T(8,128)(2,1)S(1)}, bf16[384,3072]{1,0:T(8,128)(2,1)}, u32[]{:S(2)}) copy-start(bf16[384,3072]{1,0:T(8,128)(2,1)} %param.8) | copy-start | bytes 7077892
  40.9 60.2 %all-to-all-start.3 = ((bf16[32,48,768]{2,1,0:T(8,128)(2,1)}), bf16[32,48,768]{2,1,0:T(8,128)(2,1)S(1)}, u32[]{:S(2)}, u32[]{:S(2)}) async-start(bf16[32,48,768]{2,1,0:T(8,128)(2,1)} %shard_map.84), calls=%async_computation.3 | async-start | bytes 4718592 | tf_op jit(solution)/shard_map/all_to_all | solution.py:190
  101.1 1.5 copy-start.4
  102.6 58.5 %all-to-all-start = ((bf16[32,48,768]{2,1,0:T(8,128)(2,1)}), bf16[32,48,768]{2,1,0:T(8,128)(2,1)S(1)}, u32[]{:S(2)}, u32[]{:S(2)}) async-start(bf16[32,48,768]{2,1,0:T(8,128)(2,1)} %shard_map.82), calls=%async_computation | async-start | bytes 4718592 | tf_op jit(solution)/shard_map/all_to_all | solution.py:190
  113.3 55.2 %copy-start.13 = (s32[8]{0:T(128)S(1)}, s32[8]{0:T(128)}, u32[]{:S(2)}) copy-start(s32[8]{0:T(128)} %constant.38.clone) | copy-start | bytes 100
  161.1 1.4 copy-start.3
  162.5 89.7 %all-to-all-start.5 = ((bf16[32,48,768]{2,1,0:T(8,128)(2,1)}), bf16[32,48,768]{2,1,0:T(8,128)(2,1)S(1)}, u32[]{:S(2)}, u32[]{:S(2)}) async-start(bf16[32,48,768]{2,1,0:T(8,128)(2,1)} %shard_map.86), calls=%async_computation.5 | async-start | bytes 4718592 | tf_op jit(solution)/shard_map/all_to_all | solution.py:190
  166.6 29.2 %collective-permute-start = (s32[4,4]{1,0:T(4,128)}, s32[4,4]{1,0:T(4,128)}, u32[]{:S(2)}, u32[]{:S(2)}) collective-permute-start(s32[4,4]{1,0:T(4,128)} %param.12), channel_id=1, source_target_pairs={{0,0},{4,4},{8,12},{12,8},{16,16},{20,20},{24,28},{28,24},{1,1},{5... | collective-permute-start | bytes 200 | tf_op jit(solution)/shard_map/ppermute | solution.py:161
  170.4 6.2 %copy-start.11 = (s32[1536]{0:T(1024)}, s32[1536]{0:T(1024)S(1)}, u32[]{:S(2)}) copy-start(s32[1536]{0:T(1024)S(1)} %fusion) | copy-start | bytes 18436
  185.3 9.1 %copy-start.2 = (s32[32]{0:T(128)S(1)}, s32[32]{0:T(128)}, u32[]{:S(2)}) copy-start(s32[32]{0:T(128)} %param.13) | copy-start | bytes 388
  188.6 37.7 %collective-permute-start.3 = (bf16[1152,512]{1,0:T(8,128)(2,1)}, bf16[1152,512]{1,0:T(8,128)(2,1)S(1)}, u32[]{:S(2)}, u32[]{:S(2)}) collective-permute-start(bf16[1152,512]{1,0:T(8,128)(2,1)} %get-tuple-element.11), channel_id=1, source_target_pairs={{0,4},{4,12},{12,8},{8,16},{16,20},{20,28},{28,24},{1,5},{5,13},{1... | collective-permute-start | bytes 3538952 | tf_op jit(solution)/shard_map/ppermute | solution.py:194
  192.3 36.8 %collective-permute-start.4 = (bf16[1152,512]{1,0:T(8,128)(2,1)}, bf16[1152,512]{1,0:T(8,128)(2,1)}, u32[]{:S(2)}, u32[]{:S(2)}) collective-permute-start(bf16[1152,512]{1,0:T(8,128)(2,1)} %get-tuple-element.12), channel_id=1, source_target_pairs={{4,0},{12,4},{8,12},{16,8},{20,16},{28,20},{24,28},{5,1},{13,5},{9... | collective-permute-start | bytes 3538952 | tf_op jit(solution)/shard_map/ppermute | solution.py:195
  201.6 44.8 %copy-start.9 = (s32[2048]{0:T(1024)}, s32[2048]{0:T(1024)S(1)}, u32[]{:S(2)}) copy-start(s32[2048]{0:T(1024)S(1)} %pad_clamp_fusion) | copy-start | bytes 24580
  212.3 16.7 %slice-start.2 = ((bf16[1536,768]{1,0:T(8,128)(2,1)}), bf16[1536,512]{1,0:T(8,128)(2,1)S(1)}, s32[]{:S(2)}) async-start(bf16[1536,768]{1,0:T(8,128)(2,1)} %gather_fusion.9), calls=%async_computation.9 | async-start | bytes 3145728 | tf_op jit(solution)/shard_map/slice | solution.py:193
  215.6 73.5 %collective-permute-start.1 = (bf16[1152,512]{1,0:T(8,128)(2,1)}, bf16[1152,512]{1,0:T(8,128)(2,1)}, u32[]{:S(2)}, u32[]{:S(2)}) collective-permute-start(bf16[1152,512]{1,0:T(8,128)(2,1)} %get-tuple-element.13), channel_id=1, source_target_pairs={{0,4},{4,12},{12,8},{8,16},{16,20},{20,28},{28,24},{1,5},{5,13},{1... | collective-permute-start | bytes 3538952 | tf_op jit(solution)/shard_map/ppermute | solution.py:194
  221.2 67.9 %collective-permute-start.2 = (bf16[1152,512]{1,0:T(8,128)(2,1)}, bf16[1152,512]{1,0:T(8,128)(2,1)}, u32[]{:S(2)}, u32[]{:S(2)}) collective-permute-start(bf16[1152,512]{1,0:T(8,128)(2,1)} %get-tuple-element.14), channel_id=1, source_target_pairs={{4,0},{12,4},{8,12},{16,8},{20,16},{28,20},{24,28},{5,1},{13,5},{9... | collective-permute-start | bytes 3538952 | tf_op jit(solution)/shard_map/ppermute | solution.py:195
  252.2 60.7 %all-to-all-start.4 = ((bf16[32,48,256]{2,1,0:T(8,128)(2,1)}), bf16[32,48,256]{2,1,0:T(8,128)(2,1)S(1)}, u32[]{:S(2)}, u32[]{:S(2)}) async-start(bf16[32,48,256]{2,1,0:T(8,128)(2,1)} %bitcast.16), calls=%async_computation.4 | async-start | bytes 1572864 | tf_op jit(solution)/shard_map/all_to_all | solution.py:199
  279.8 9.4 %slice-start.1 = ((bf16[1536,768]{1,0:T(8,128)(2,1)}), bf16[1536,512]{1,0:T(8,128)(2,1)S(1)}, s32[]{:S(2)}) async-start(bf16[1536,768]{1,0:T(8,128)(2,1)} %gather_fusion.7), calls=%async_computation.8 | async-start | bytes 3145728 | tf_op jit(solution)/shard_map/slice | solution.py:193
  283.2 36.6 %collective-permute-start.5 = (bf16[1152,512]{1,0:T(8,128)(2,1)}, bf16[1152,512]{1,0:T(8,128)(2,1)}, u32[]{:S(2)}, u32[]{:S(2)}) collective-permute-start(bf16[1152,512]{1,0:T(8,128)(2,1)} %get-tuple-element.9), channel_id=1, source_target_pairs={{0,4},{4,12},{12,8},{8,16},{16,20},{20,28},{28,24},{1,5},{5,13},{1... | collective-permute-start | bytes 3538952 | tf_op jit(solution)/shard_map/ppermute | solution.py:194
  287.9 31.9 %collective-permute-start.6 = (bf16[1152,512]{1,0:T(8,128)(2,1)}, bf16[1152,512]{1,0:T(8,128)(2,1)}, u32[]{:S(2)}, u32[]{:S(2)}) collective-permute-start(bf16[1152,512]{1,0:T(8,128)(2,1)} %get-tuple-element.10), channel_id=1, source_target_pairs={{4,0},{12,4},{8,12},{16,8},{20,16},{28,20},{24,28},{5,1},{13,5},{9... | collective-permute-start | bytes 3538952 | tf_op jit(solution)/shard_map/ppermute | solution.py:195
  292.5 14.4 %copy-start.10 = (s32[2048]{0:T(1024)S(1)}, s32[2048]{0:T(1024)}, u32[]{:S(2)}) copy-start(s32[2048]{0:T(1024)} %copy-done.9) | copy-start | bytes 24580
  306.9 11.8 %copy-start.6 = (bf16[1536,768]{1,0:T(8,128)(2,1)S(1)}, bf16[1536,768]{1,0:T(8,128)(2,1)}, u32[]{:S(2)}) copy-start(bf16[1536,768]{1,0:T(8,128)(2,1)} %gather_fusion.11) | copy-start | bytes 7077892
  312.9 6.8 %copy-start.7 = (bf16[32,48,256]{2,1,0:T(8,128)(2,1)}, bf16[32,48,256]{2,1,0:T(8,128)(2,1)S(1)}, u32[]{:S(2)}) copy-start(bf16[32,48,256]{2,1,0:T(8,128)(2,1)S(1)} %all-to-all-done.4.refs_1_) | copy-start | bytes 2359300
  312.9 30.9 %all-to-all-start.2 = ((bf16[32,48,256]{2,1,0:T(8,128)(2,1)}), bf16[32,48,256]{2,1,0:T(8,128)(2,1)}, u32[]{:S(2)}, u32[]{:S(2)}) async-start(bf16[32,48,256]{2,1,0:T(8,128)(2,1)} %bitcast.17), calls=%async_computation.2 | async-start | bytes 1572864 | tf_op jit(solution)/shard_map/all_to_all | solution.py:199
  318.8 1.7 slice-start
  343.8 26.4 %all-to-all-start.6 = ((bf16[32,48,256]{2,1,0:T(8,128)(2,1)}), bf16[32,48,256]{2,1,0:T(8,128)(2,1)S(1)}, u32[]{:S(2)}, u32[]{:S(2)}) async-start(bf16[32,48,256]{2,1,0:T(8,128)(2,1)} %bitcast.9), calls=%async_computation.6 | async-start | bytes 1572864 | tf_op jit(solution)/shard_map/all_to_all | solution.py:199
  370.1 0.9 copy-start.8
  376.9 8.9 %copy-start.1 = (bf16[384,3072]{1,0:T(8,128)(2,1)S(1)}, bf16[384,3072]{1,0:T(8,128)(2,1)}, u32[]{:S(2)}) copy-start(bf16[384,3072]{1,0:T(8,128)(2,1)} %param.10) | copy-start | bytes 7077892

commit v2 on v1

--- a/solution.py
+++ b/solution.py
@@ -139,7 +139,7 @@
     ext_tiles = tile_dev + 2 * reach
     heads_here = part_width // HEAD_DIM
     all_tiles = valid_count.shape[0]
-    chunks = 3 if heads_here % 3 == 0 else (2 if heads_here % 2 == 0 else 1)
+    chunks = 2 if heads_here % 2 == 0 else 1
     chunk_heads = heads_here // chunks
     chunk_width = chunk_heads * HEAD_DIM
     devices = seq_count * head_count

time: 388 us -> 370 us (0.954)
  waiting for transfers between devices: 119 us -> 138 us
  local copies, waits for them, and re-layouts: 105 us -> 90.8 us
  starting transfers between devices: 73 us -> 60.1 us
  Pallas kernels: 68.7 us -> 60.3 us
    all_to_all x3 -> x2, waiting for transfers between devices: 95.5 us -> 113 us  [body(): lax.all_to_all(send, ('seq', 'head'), split_axis=0, concat_axis=0, tiled=...]
    all_to_all x3 -> x2, waiting for transfers between devices: 17.3 us -> 25.9 us  [body(): lax.all_to_all(outgoing, ('seq', 'head'), split_axis=0, concat_axis=0, ti...]
    gather x3 -> x2, local copies, waits for them, and re-layouts: 22.9 us -> 16.9 us  [body(): got_tile = got.reshape(tok_dev, 3 * chunk_width)[place]]
    pallas_call x3 -> x2, Pallas kernels: 19.9 us -> 14 us  [pack(): pl.pallas_call(functools.partial(pack_kernel, head_count, part_width, chu...]
    ppermute x3 -> x2, starting transfers between devices: 14.1 us -> 8.88 us  [body(): from_left = lax.ppermute(kv_tile[tok_dev - rim:], 'seq', to_right)]
    gather x3 -> x2, local copies, waits for them, and re-layouts: 17.4 us -> 13 us  [body(): outgoing = out_tile[local].reshape(devices, share, chunk_width)]
    all_to_all x3 -> x2, starting transfers between devices: 14.1 us -> 10 us  [body(): lax.all_to_all(send, ('seq', 'head'), split_axis=0, concat_axis=0, tiled=...]
    pallas_call x3 -> x2, Pallas kernels: 42.9 us -> 40.4 us  [attention(): pl.pallas_call(functools.partial(attn_kernel, win, tile, scale), out_shap...]
  transfers between devices with their start and end apart: 14 -> 10, of which waited for: 5 -> 3; matrix products, arithmetic and copies ran while one was open for 26% -> 23% of each run, Pallas kernels for 16% -> 15%
where the time goes in v2:
time: 370 us; the launch traced here: 369 us
  waiting for transfers between devices  138 us (37%)
  local copies, waits for them, and re-layouts  90.8 us (25%)
  Pallas kernels  60.3 us (16%)
  starting transfers between devices  60.1 us (16%)
  other arithmetic  17.6 us (5%)
    all_to_all x2, waiting for transfers between devices, body(): lax.all_to_all(send, ('seq', 'head'), split_axis=0, concat_axis=0, tiled=...  113 us
    pallas_call x2, Pallas kernels, attention(): pl.pallas_call(functools.partial(attn_kernel, win, tile, scale), out_shap...  40.4 us
    all_to_all x2, starting transfers between devices, body(): lax.all_to_all(outgoing, ('seq', 'head'), split_axis=0, concat_axis=0, ti...  30 us
    all_to_all x2, waiting for transfers between devices, body(): lax.all_to_all(outgoing, ('seq', 'head'), split_axis=0, concat_axis=0, ti...  25.9 us
    gather x2, local copies, waits for them, and re-layouts, body(): got_tile = got.reshape(tok_dev, 3 * chunk_width)[place]  16.9 us
    gather x3, local copies, waits for them, and re-layouts, body(): rows_flat = [x[send_order] for x in (query, key, value)]  16 us
    pallas_call x2, Pallas kernels, pack(): pl.pallas_call(functools.partial(pack_kernel, head_count, part_width, chu...  14 us
    gather x2, local copies, waits for them, and re-layouts, body(): outgoing = out_tile[local].reshape(devices, share, chunk_width)  13 us
  transfers between devices with their start and end apart: 10, of which 3 were waited for; matrix products, arithmetic and copies ran while one was open for 23% of the time, Pallas kernels for 15%

profile of v2, /device:TPU:0, one launch (start us, length us, event | category | flops | bytes accessed | tf_op | source)
XLA Modules:
  0.0 368.8 jit_solution(7142387691130047417)
XLA Ops:
  0.0 4.6 %sort.17 = (s32[384]{0:T(512)}, s32[384]{0:T(512)S(1)}) sort(s32[384]{0:T(512)} %param.11, s32[384]{0:T(512)S(1)} %iota.15), dimensions={0}, to_apply=%region_0.0 | sort | flops 3456 | bytes 6144 | tf_op jit(solution)/shard_map/jit(argsort)/sort | solution.py:150
  6.6 3.6 gather_fusion.6
  10.9 7.3 %all-to-all-start.1 = ((s32[32,1,48]{2,1,0:T(1,128)}), s32[32,1,48]{2,1,0:T(1,128)S(1)}, u32[]{:S(2)}, u32[]{:S(2)}) async-start(s32[32,1,48]{2,1,0:T(1,128)} %bitcast.3), calls=%async_computation.1 | async-start | bytes 32768 | tf_op jit(solution)/shard_map/all_to_all | solution.py:154
  18.2 3.6 gather_fusion.5
  21.8 8.9 %gather_fusion.4 = bf16[384,3072]{1,0:T(8,128)(2,1)} fusion(bf16[384,3072]{1,0:T(8,128)(2,1)} %param.9, s32[1024]{0:T(1024)S(1)} %pad_clamp_fusion.3), kind=kCustom, calls=%fused_computation.4 | custom fusion | bytes 4720128 | tf_op jit(solution)/shard_map/gather | solution.py:177
  30.7 3.6 gather_fusion.3
  34.3 7.0 %shard_map.82 = bf16[32,48,1152]{2,1,0:T(8,128)(2,1)} custom-call(bf16[384,3072]{1,0:T(8,128)(2,1)} %gather_fusion.3, bf16[384,3072]{1,0:T(8,128)(2,1)} %gather_fusion.4, bf16[384,3072]{1,0:T(8,128)(2,1)} %gather_fusion.5), custom_call_target="tpu_custom_call" | custom-call | bytes 7077888 | tf_op jit(solution)/shard_map/pallas_call | solution.py:92
  41.9 5.9 %all-to-all-start = ((bf16[32,48,1152]{2,1,0:T(8,128)(2,1)}), bf16[32,48,1152]{2,1,0:T(8,128)(2,1)}, u32[]{:S(2)}, u32[]{:S(2)}) async-start(bf16[32,48,1152]{2,1,0:T(8,128)(2,1)} %shard_map.82), calls=%async_computation | async-start | bytes 7077888 | tf_op jit(solution)/shard_map/all_to_all | solution.py:190
  47.8 7.0 %shard_map.84 = bf16[32,48,1152]{2,1,0:T(8,128)(2,1)} custom-call(bf16[384,3072]{1,0:T(8,128)(2,1)} %gather_fusion.3, bf16[384,3072]{1,0:T(8,128)(2,1)} %gather_fusion.4, bf16[384,3072]{1,0:T(8,128)(2,1)} %gather_fusion.5), custom_call_target="tpu_custom_call" | custom-call | bytes 7077888 | tf_op jit(solution)/shard_map/pallas_call | solution.py:92
  54.8 72.7 %all-to-all-done = bf16[32,48,1152]{2,1,0:T(8,128)(2,1)} async-done(((bf16[32,48,1152]{2,1,0:T(8,128)(2,1)}), bf16[32,48,1152]{2,1,0:T(8,128)(2,1)}, u32[]{:S(2)}, u32[]{:S(2)}) %all-to-all-start) | async-done | bytes 3538976 | tf_op jit(solution)/shard_map/all_to_all | solution.py:190
  127.5 4.1 %all-to-all-start.3 = ((bf16[32,48,1152]{2,1,0:T(8,128)(2,1)}), bf16[32,48,1152]{2,1,0:T(8,128)(2,1)S(1)}, u32[]{:S(2)}, u32[]{:S(2)}) async-start(bf16[32,48,1152]{2,1,0:T(8,128)(2,1)} %shard_map.84), calls=%async_computation.3 | async-start | bytes 7077888 | tf_op jit(solution)/shard_map/all_to_all | solution.py:190
  135.7 6.3 %scatter_custom_fusion = s32[1536]{0:T(1024)S(1)} fusion(s32[1536]{0:T(1024)S(1)} %fusion, s32[1536]{0:T(1024)} %iota.16, s32[]{:T(128)} %constant.15.clone.1), kind=kCustom, calls=%fused_computation.30 | custom fusion | bytes 6656 | tf_op jit(solution)/shard_map/scatter | solution.py:159
  142.7 10.9 %gather_fusion.7 = bf16[1536,1152]{1,0:T(8,128)(2,1)} fusion(bf16[1536,1152]{1,0:T(8,128)(2,1)} %bitcast.2, s32[2048]{0:T(1024)S(1)} %pad_clamp_fusion.1), kind=kCustom, calls=%fused_computation.7 | custom fusion | bytes 7084032 | tf_op jit(solution)/shard_map/gather | solution.py:191
  153.6 4.1 %fusion.8 = (bf16[1152,768]{1,0:T(8,128)(2,1)}, bf16[1152,768]{1,0:T(8,128)(2,1)}) fusion(bf16[1536,1152]{1,0:T(8,128)(2,1)} %gather_fusion.7), kind=kLoop, calls=%fused_computation.39 | loop fusion | bytes 7077888 | tf_op jit(solution)/shard_map/slice | solution.py:194
  157.7 4.9 %collective-permute-start.1 = (bf16[1152,768]{1,0:T(8,128)(2,1)}, bf16[1152,768]{1,0:T(8,128)(2,1)}, u32[]{:S(2)}, u32[]{:S(2)}) collective-permute-start(bf16[1152,768]{1,0:T(8,128)(2,1)} %get-tuple-element.11), channel_id=1, source_target_pairs={{0,4},{4,12},{12,8},{8,16},{16,20},{20,28},{28,24},{1,5},{5,13},{1... | collective-permute-start | bytes 5308424 | tf_op jit(solution)/shard_map/ppermute | solution.py:194
  169.8 2.4 slice.64.q_ref
  172.2 39.8 %all-to-all-done.3 = bf16[32,48,1152]{2,1,0:T(8,128)(2,1)S(1)} async-done(((bf16[32,48,1152]{2,1,0:T(8,128)(2,1)}), bf16[32,48,1152]{2,1,0:T(8,128)(2,1)S(1)}, u32[]{:S(2)}, u32[]{:S(2)}) %all-to-all-start.3) | async-done | bytes 3538976 | tf_op jit(solution)/shard_map/all_to_all | solution.py:190
  212.0 6.1 %gather_fusion.9 = bf16[1536,1152]{1,0:T(8,128)(2,1)} fusion(bf16[1536,1152]{1,0:T(8,128)(2,1)S(1)} %bitcast.11, s32[2048]{0:T(1024)S(1)} %copy-done.7), kind=kCustom, calls=%fused_computation.9 | custom fusion | bytes 7084032 | tf_op jit(solution)/shard_map/gather | solution.py:191
  218.1 4.2 %fusion.7 = (bf16[1152,768]{1,0:T(8,128)(2,1)}, bf16[1152,768]{1,0:T(8,128)(2,1)}) fusion(bf16[1536,1152]{1,0:T(8,128)(2,1)} %gather_fusion.9), kind=kLoop, calls=%fused_computation.38 | loop fusion | bytes 7077888 | tf_op jit(solution)/shard_map/slice | solution.py:194
  222.3 4.0 %collective-permute-start.3 = (bf16[1152,768]{1,0:T(8,128)(2,1)}, bf16[1152,768]{1,0:T(8,128)(2,1)}, u32[]{:S(2)}, u32[]{:S(2)}) collective-permute-start(bf16[1152,768]{1,0:T(8,128)(2,1)} %get-tuple-element.9), channel_id=1, source_target_pairs={{0,4},{4,12},{12,8},{8,16},{16,20},{20,28},{28,24},{1,5},{5,13},{1... | collective-permute-start | bytes 5308424 | tf_op jit(solution)/shard_map/ppermute | solution.py:194
  227.6 5.1 %pad_maximum_fusion.refs_0_.refs_1_.refs_2_.refs_3_.refs_4_.refs_5_.refs_6_.refs_7_ = bf16[3840,768]{1,0:T(8,128)(2,1)} fusion(bf16[1152,768]{1,0:T(8,128)(2,1)} %collective-permute-done.2, bf16[1536,768]{1,0:T(8,128)(2,1)S(1)} %slice-done, bf16[1152,768]{1,0:T(8,128)(2,1)} %collective-permute-done.1), kind=kLoop, calls=%fused_computation.14 | loop fusion | flops 17694720 | bytes 11796480 | tf_op jit(solution)/shard_map/concatenate | solution.py:196
  232.7 20.2 %shard_map.83 = bf16[1536,384]{1,0:T(8,128)(2,1)} custom-call(s32[16]{0:T(128)} %reshape.105.win_ref, s32[16]{0:T(128)} %gather_fusion.1, s32[4]{0:T(128)} %slice.31.vco_ref, bf16[1536,384]{1,0:T(8,128)(2,1)} %slice.64.q_ref, bf16[3840,768]{1,0:T(8,128)(2,1)} %pad_maximum_fusion.refs_0_.refs_1_.refs_2_.refs_3_.refs_4_.refs_5_.refs_6_.refs_7_, ...), custom_call_target="tpu_custom_call" | custom-call | flops 3623878656 | bytes 11796480 | tf_op jit(solution)/shard_map/pallas_call | solution.py:68
  252.9 6.6 %gather_fusion.8 = bf16[1536,384]{1,0:T(8,128)(2,1)} fusion(bf16[1536,384]{1,0:T(8,128)(2,1)} %shard_map.83, s32[2048]{0:T(1024)S(1)} %pad_clamp_fusion), kind=kCustom, calls=%fused_computation.8 | custom fusion | bytes 2365440 | tf_op jit(solution)/shard_map/gather | solution.py:198
  259.5 24.3 %all-to-all-start.2 = ((bf16[32,48,384]{2,1,0:T(8,128)(2,1)}), bf16[32,48,384]{2,1,0:T(8,128)(2,1)}, u32[]{:S(2)}, u32[]{:S(2)}) async-start(bf16[32,48,384]{2,1,0:T(8,128)(2,1)} %bitcast.12), calls=%async_computation.2 | async-start | bytes 2359296 | tf_op jit(solution)/shard_map/all_to_all | solution.py:199
  286.6 5.1 %pad_maximum_fusion.1.refs_0_.refs_1_.refs_2_.refs_3_.refs_4_.refs_5_.refs_6_.refs_7_ = bf16[3840,768]{1,0:T(8,128)(2,1)} fusion(bf16[1152,768]{1,0:T(8,128)(2,1)} %collective-permute-done.4, bf16[1536,768]{1,0:T(8,128)(2,1)S(1)} %slice-done.1, bf16[1152,768]{1,0:T(8,128)(2,1)} %collective-permute-done.3), kind=kLoop, calls=%fused_computation.15 | loop fusion | flops 17694720 | bytes 11796480 | tf_op jit(solution)/shard_map/concatenate | solution.py:196
  291.7 20.2 %shard_map.85 = bf16[1536,384]{1,0:T(8,128)(2,1)} custom-call(s32[16]{0:T(128)} %reshape.105.win_ref, s32[16]{0:T(128)} %gather_fusion.1, s32[4]{0:T(128)} %slice.31.vco_ref, bf16[1536,384]{1,0:T(8,128)(2,1)} %slice.68.q_ref, bf16[3840,768]{1,0:T(8,128)(2,1)} %pad_maximum_fusion.1.refs_0_.refs_1_.refs_2_.refs_3_.refs_4_.refs_5_.refs_6_.refs_7_, ...), custom_call_target="tpu_custom_call" | custom-call | flops 3623878656 | bytes 11796480 | tf_op jit(solution)/shard_map/pallas_call | solution.py:68
  311.9 6.4 %gather_fusion.10 = bf16[1536,384]{1,0:T(8,128)(2,1)} fusion(bf16[1536,384]{1,0:T(8,128)(2,1)} %shard_map.85, s32[2048]{0:T(1024)S(1)} %pad_clamp_fusion), kind=kCustom, calls=%fused_computation.10 | custom fusion | bytes 2365440 | tf_op jit(solution)/shard_map/gather | solution.py:198
  318.3 5.7 %all-to-all-start.4 = ((bf16[32,48,384]{2,1,0:T(8,128)(2,1)}), bf16[32,48,384]{2,1,0:T(8,128)(2,1)S(1)}, u32[]{:S(2)}, u32[]{:S(2)}) async-start(bf16[32,48,384]{2,1,0:T(8,128)(2,1)} %bitcast.7), calls=%async_computation.4 | async-start | bytes 2359296 | tf_op jit(solution)/shard_map/all_to_all | solution.py:199
  324.0 3.0 scatter_custom_fusion.1
  327.1 25.9 %all-to-all-done.4.refs_1_ = bf16[32,48,384]{2,1,0:T(8,128)(2,1)S(1)} async-done(((bf16[32,48,384]{2,1,0:T(8,128)(2,1)}), bf16[32,48,384]{2,1,0:T(8,128)(2,1)S(1)}, u32[]{:S(2)}, u32[]{:S(2)}) %all-to-all-start.4) | async-done | bytes 1179680 | tf_op jit(solution)/shard_map/all_to_all | solution.py:199
  354.0 5.9 %shard_map.86 = bf16[384,3072]{1,0:T(8,128)(2,1)} custom-call(bf16[32,48,384]{2,1,0:T(8,128)(2,1)} %all-to-all-done.2.refs_0_, bf16[32,48,384]{2,1,0:T(8,128)(2,1)} %copy-done.5), custom_call_target="tpu_custom_call" | custom-call | bytes 4718592 | tf_op jit(solution)/shard_map/pallas_call | solution.py:115
  359.9 8.9 %gather_fusion.11 = bf16[384,3072]{1,0:T(8,128)(2,1)} fusion(bf16[384,3072]{1,0:T(8,128)(2,1)} %shard_map.86, s32[1024]{0:T(1024)S(1)} %pad_clamp_fusion.2), kind=kCustom, calls=%fused_computation.11 | custom fusion | bytes 4720128 | tf_op jit(solution)/shard_map/gather | solution.py:210
  (68 shorter events, 19.0 us)
Async XLA Ops:
  0.0 18.2 %copy-start = (bf16[384,3072]{1,0:T(8,128)(2,1)S(1)}, bf16[384,3072]{1,0:T(8,128)(2,1)}, u32[]{:S(2)}) copy-start(bf16[384,3072]{1,0:T(8,128)(2,1)} %param.10) | copy-start | bytes 7077892
  6.0 0.6 copy-start.10
  10.9 30.4 %all-to-all-start.1 = ((s32[32,1,48]{2,1,0:T(1,128)}), s32[32,1,48]{2,1,0:T(1,128)S(1)}, u32[]{:S(2)}, u32[]{:S(2)}) async-start(s32[32,1,48]{2,1,0:T(1,128)} %bitcast.3), calls=%async_computation.1 | async-start | bytes 32768 | tf_op jit(solution)/shard_map/all_to_all | solution.py:154
  21.8 8.9 %copy-start.3 = (bf16[384,3072]{1,0:T(8,128)(2,1)S(1)}, bf16[384,3072]{1,0:T(8,128)(2,1)}, u32[]{:S(2)}) copy-start(bf16[384,3072]{1,0:T(8,128)(2,1)} %param.8) | copy-start | bytes 7077892
  41.3 0.6 copy-start.8
  41.9 85.7 %all-to-all-start = ((bf16[32,48,1152]{2,1,0:T(8,128)(2,1)}), bf16[32,48,1152]{2,1,0:T(8,128)(2,1)}, u32[]{:S(2)}, u32[]{:S(2)}) async-start(bf16[32,48,1152]{2,1,0:T(8,128)(2,1)} %shard_map.82), calls=%async_computation | async-start | bytes 7077888 | tf_op jit(solution)/shard_map/all_to_all | solution.py:190
  54.8 76.8 %copy-start.11 = (s32[8]{0:T(128)S(1)}, s32[8]{0:T(128)}, u32[]{:S(2)}) copy-start(s32[8]{0:T(128)} %constant.38.clone) | copy-start | bytes 100
  127.5 84.5 %all-to-all-start.3 = ((bf16[32,48,1152]{2,1,0:T(8,128)(2,1)}), bf16[32,48,1152]{2,1,0:T(8,128)(2,1)S(1)}, u32[]{:S(2)}, u32[]{:S(2)}) async-start(bf16[32,48,1152]{2,1,0:T(8,128)(2,1)} %shard_map.84), calls=%async_computation.3 | async-start | bytes 7077888 | tf_op jit(solution)/shard_map/all_to_all | solution.py:190
  135.1 7.0 %copy-start.9 = (s32[1536]{0:T(1024)}, s32[1536]{0:T(1024)S(1)}, u32[]{:S(2)}) copy-start(s32[1536]{0:T(1024)S(1)} %fusion) | copy-start | bytes 18436
  142.1 0.6 copy-start.6
  153.6 12.3 %copy-start.2 = (s32[32]{0:T(128)S(1)}, s32[32]{0:T(128)}, u32[]{:S(2)}) copy-start(s32[32]{0:T(128)} %param.13) | copy-start | bytes 388
  157.7 69.9 %collective-permute-start.1 = (bf16[1152,768]{1,0:T(8,128)(2,1)}, bf16[1152,768]{1,0:T(8,128)(2,1)}, u32[]{:S(2)}, u32[]{:S(2)}) collective-permute-start(bf16[1152,768]{1,0:T(8,128)(2,1)} %get-tuple-element.11), channel_id=1, source_target_pairs={{0,4},{4,12},{12,8},{8,16},{16,20},{20,28},{28,24},{1,5},{5,13},{1... | collective-permute-start | bytes 5308424 | tf_op jit(solution)/shard_map/ppermute | solution.py:194
  162.6 65.0 %collective-permute-start.2 = (bf16[1152,768]{1,0:T(8,128)(2,1)}, bf16[1152,768]{1,0:T(8,128)(2,1)}, u32[]{:S(2)}, u32[]{:S(2)}) collective-permute-start(bf16[1152,768]{1,0:T(8,128)(2,1)} %get-tuple-element.12), channel_id=1, source_target_pairs={{4,0},{12,4},{8,12},{16,8},{20,16},{28,20},{24,28},{5,1},{13,5},{9... | collective-permute-start | bytes 5308424 | tf_op jit(solution)/shard_map/ppermute | solution.py:195
  163.8 3.3 collective-permute-start
  172.2 39.8 %copy-start.7 = (s32[2048]{0:T(1024)S(1)}, s32[2048]{0:T(1024)}, u32[]{:S(2)}) copy-start(s32[2048]{0:T(1024)} %copy-done.6) | copy-start | bytes 24580
  218.1 9.5 %slice-start = ((bf16[1536,1152]{1,0:T(8,128)(2,1)}), bf16[1536,768]{1,0:T(8,128)(2,1)S(1)}, s32[]{:S(2)}) async-start(bf16[1536,1152]{1,0:T(8,128)(2,1)} %gather_fusion.7), calls=%async_computation.5 | async-start | bytes 4718592 | tf_op jit(solution)/shard_map/slice | solution.py:193
  222.3 62.6 %collective-permute-start.3 = (bf16[1152,768]{1,0:T(8,128)(2,1)}, bf16[1152,768]{1,0:T(8,128)(2,1)}, u32[]{:S(2)}, u32[]{:S(2)}) collective-permute-start(bf16[1152,768]{1,0:T(8,128)(2,1)} %get-tuple-element.9), channel_id=1, source_target_pairs={{0,4},{4,12},{12,8},{8,16},{16,20},{20,28},{28,24},{1,5},{5,13},{1... | collective-permute-start | bytes 5308424 | tf_op jit(solution)/shard_map/ppermute | solution.py:194
  226.3 58.7 %collective-permute-start.4 = (bf16[1152,768]{1,0:T(8,128)(2,1)}, bf16[1152,768]{1,0:T(8,128)(2,1)}, u32[]{:S(2)}, u32[]{:S(2)}) collective-permute-start(bf16[1152,768]{1,0:T(8,128)(2,1)} %get-tuple-element.10), channel_id=1, source_target_pairs={{4,0},{12,4},{8,12},{16,8},{20,16},{28,20},{24,28},{5,1},{13,5},{9... | collective-permute-start | bytes 5308424 | tf_op jit(solution)/shard_map/ppermute | solution.py:195
  252.9 30.9 %copy-start.4 = (bf16[1536,1152]{1,0:T(8,128)(2,1)S(1)}, bf16[1536,1152]{1,0:T(8,128)(2,1)}, u32[]{:S(2)}) copy-start(bf16[1536,1152]{1,0:T(8,128)(2,1)} %gather_fusion.9) | copy-start | bytes 10616836
  259.5 58.9 %all-to-all-start.2 = ((bf16[32,48,384]{2,1,0:T(8,128)(2,1)}), bf16[32,48,384]{2,1,0:T(8,128)(2,1)}, u32[]{:S(2)}, u32[]{:S(2)}) async-start(bf16[32,48,384]{2,1,0:T(8,128)(2,1)} %bitcast.12), calls=%async_computation.2 | async-start | bytes 2359296 | tf_op jit(solution)/shard_map/all_to_all | solution.py:199
  284.9 1.7 slice-start.1
  318.3 34.7 %all-to-all-start.4 = ((bf16[32,48,384]{2,1,0:T(8,128)(2,1)}), bf16[32,48,384]{2,1,0:T(8,128)(2,1)S(1)}, u32[]{:S(2)}, u32[]{:S(2)}) async-start(bf16[32,48,384]{2,1,0:T(8,128)(2,1)} %bitcast.7), calls=%async_computation.4 | async-start | bytes 2359296 | tf_op jit(solution)/shard_map/all_to_all | solution.py:199
  353.0 1.0 copy-start.5
  359.9 8.9 %copy-start.1 = (bf16[384,3072]{1,0:T(8,128)(2,1)S(1)}, bf16[384,3072]{1,0:T(8,128)(2,1)}, u32[]{:S(2)}) copy-start(bf16[384,3072]{1,0:T(8,128)(2,1)} %param.10) | copy-start | bytes 7077892

commit v3 on v2

--- a/solution.py
+++ b/solution.py
@@ -79,18 +79,18 @@
     )(win_flat, vcw_flat, vc_own, q_tile, *([kv_ext] * (2 * win)))
 
 
-def pack_kernel(head_count, part_width, chunk_width, c, q_ref, k_ref, v_ref, o_ref):
+def pack_kernel(head_count, part_width, chunk_width, col0, q_ref, k_ref, v_ref, o_ref):
     for h in range(head_count):
-        base = h * part_width + c * chunk_width
+        base = h * part_width + col0
         for t, x_ref in enumerate((q_ref, k_ref, v_ref)):
             o_ref[h, :, t * chunk_width : (t + 1) * chunk_width] = x_ref[:, base : base + chunk_width]
 
 
-def pack(xs, c, seq_count, head_count, share, chunk_width):
+def pack(xs, col0, seq_count, head_count, share, chunk_width):
     rows_here, width = xs[0].shape
     part_width = width // head_count
     return pl.pallas_call(
-        functools.partial(pack_kernel, head_count, part_width, chunk_width, c),
+        functools.partial(pack_kernel, head_count, part_width, chunk_width, col0),
         out_shape=jax.ShapeDtypeStruct((seq_count * head_count, share, 3 * chunk_width), xs[0].dtype),
         grid=(seq_count,),
         in_specs=[pl.BlockSpec((share, width), lambda s: (s, 0))] * 3,
@@ -101,22 +101,28 @@
     )(*xs)
 
 
-def unpack_kernel(head_count, part_width, chunk_width, *refs):
+def unpack_kernel(head_count, part_width, spans, *refs):
     o_ref = refs[-1]
-    for c, b_ref in enumerate(refs[:-1]):
+    for (col0, chunk_width), b_ref in zip(spans, refs[:-1]):
         for h in range(head_count):
-            base = h * part_width + c * chunk_width
+            base = h * part_width + col0
             o_ref[:, base : base + chunk_width] = b_ref[h]
 
 
 def unpack(backs, seq_count, head_count, share, width):
-    devices, _, chunk_width = backs[0].shape
     part_width = width // head_count
+    spans = []
+    col0 = 0
+    for b in backs:
+        spans.append((col0, b.shape[2]))
+        col0 += b.shape[2]
     return pl.pallas_call(
-        functools.partial(unpack_kernel, head_count, part_width, chunk_width),
+        functools.partial(unpack_kernel, head_count, part_width, tuple(spans)),
         out_shape=jax.ShapeDtypeStruct((seq_count * share, width), backs[0].dtype),
         grid=(seq_count,),
-        in_specs=[pl.BlockSpec((head_count, share, chunk_width), lambda s: (s, 0, 0))] * len(backs),
+        in_specs=[
+            pl.BlockSpec((head_count, share, b.shape[2]), lambda s: (s, 0, 0)) for b in backs
+        ],
         out_specs=pl.BlockSpec((share, width), lambda s: (s, 0)),
         cost_estimate=pl.CostEstimate(
             flops=0, transcendentals=0, bytes_accessed=2 * seq_count * share * width * 2
@@ -139,9 +145,8 @@
     ext_tiles = tile_dev + 2 * reach
     heads_here = part_width // HEAD_DIM
     all_tiles = valid_count.shape[0]
-    chunks = 2 if heads_here % 2 == 0 else 1
-    chunk_heads = heads_here // chunks
-    chunk_width = chunk_heads * HEAD_DIM
+    later = heads_here // 3
+    head_split = [heads_here - later, later] if later > 0 else [heads_here]
     devices = seq_count * head_count
 
     owner_at = [0] * seq_count
@@ -177,16 +182,21 @@
         rows_flat = [x[send_order] for x in (query, key, value)]
     else:
         rows_sorted = [
-            x[send_order].reshape(seq_count, share, head_count, chunks, chunk_width)
+            x[send_order].reshape(seq_count, share, head_count, part_width)
             for x in (query, key, value)
         ]
     arrived = []
-    for c in range(chunks):
+    col0 = 0
+    for chunk_heads in head_split:
+        chunk_width = chunk_heads * HEAD_DIM
         if packable:
-            send = pack(rows_flat, c, seq_count, head_count, share, chunk_width)
+            send = pack(rows_flat, col0, seq_count, head_count, share, chunk_width)
         else:
-            send = jnp.concatenate([x[:, :, :, c, :] for x in rows_sorted], axis=3)
+            send = jnp.concatenate(
+                [x[:, :, :, col0 : col0 + chunk_width] for x in rows_sorted], axis=3
+            )
             send = jnp.swapaxes(send, 1, 2).reshape(devices, share, 3 * chunk_width)
+        col0 += chunk_width
         got = lax.all_to_all(send, ("seq", "head"), split_axis=0, concat_axis=0, tiled=True)
         got_tile = got.reshape(tok_dev, 3 * chunk_width)[place]
         q_tile = got_tile[:, :chunk_width]
@@ -201,7 +211,7 @@
     if packable:
         sorted_rows = unpack(arrived, seq_count, head_count, share, width)
     else:
-        arrived = [b.reshape(seq_count, head_count, share, 1, chunk_width) for b in arrived]
+        arrived = [b.reshape(seq_count, head_count, share, b.shape[2]) for b in arrived]
         arrived = jnp.concatenate(arrived, axis=3)
         sorted_rows = jnp.swapaxes(arrived, 1, 2).reshape(rows_here, width)
     inverse = (

time: 370 us -> 423 us (1.14)
  waiting for transfers between devices: 138 us -> 166 us
  starting transfers between devices: 60.1 us -> 87.3 us
    all_to_all x2, starting transfers between devices: 30 us -> 58.8 us  [body(): lax.all_to_all(outgoing, ('seq', 'head'), split_axis=0, concat_axis=0, ti...]
    all_to_all x2, waiting for transfers between devices: 113 us -> 131 us  [body(): lax.all_to_all(send, ('seq', 'head'), split_axis=0, concat_axis=0, tiled=...]
    all_to_all x2, waiting for transfers between devices: 25.9 us -> 34.3 us  [body(): lax.all_to_all(outgoing, ('seq', 'head'), split_axis=0, concat_axis=0, ti...]
  transfers between devices with their start and end apart: 10 -> 10, of which waited for: 3 -> 3; matrix products, arithmetic and copies ran while one was open for 23% -> 20% of each run, Pallas kernels for 15% -> 13%
where the time goes in v3:
time: 423 us; the launch traced here: 421 us
  waiting for transfers between devices  166 us (39%)
  local copies, waits for them, and re-layouts  91.9 us (22%)
  starting transfers between devices  87.3 us (21%)
  Pallas kernels  60.3 us (14%)
  other arithmetic  14.6 us (3%)
    all_to_all x2, waiting for transfers between devices, body(): lax.all_to_all(send, ('seq', 'head'), split_axis=0, concat_axis=0, tiled=...  131 us
    all_to_all x2, starting transfers between devices, body(): lax.all_to_all(outgoing, ('seq', 'head'), split_axis=0, concat_axis=0, ti...  58.8 us
    pallas_call x2, Pallas kernels, attention(): pl.pallas_call(functools.partial(attn_kernel, win, tile, scale), out_shap...  40.4 us
    all_to_all x2, waiting for transfers between devices, body(): lax.all_to_all(outgoing, ('seq', 'head'), split_axis=0, concat_axis=0, ti...  34.3 us
    gather x2, local copies, waits for them, and re-layouts, body(): got_tile = got.reshape(tok_dev, 3 * chunk_width)[place]  19 us
    gather x3, local copies, waits for them, and re-layouts, body(): rows_flat = [x[send_order] for x in (query, key, value)]  16.1 us
    pallas_call x2, Pallas kernels, pack(): pl.pallas_call(functools.partial(pack_kernel, head_count, part_width, chu...  14.1 us
    gather x2, local copies, waits for them, and re-layouts, body(): outgoing = out_tile[local].reshape(devices, share, chunk_width)  12.9 us
  transfers between devices with their start and end apart: 10, of which 3 were waited for; matrix products, arithmetic and copies ran while one was open for 20% of the time, Pallas kernels for 13%

profile of v3, /device:TPU:0, one launch (start us, length us, event | category | flops | bytes accessed | tf_op | source)
XLA Modules:
  0.0 421.1 jit_solution(13828702900304929625)
XLA Ops:
  0.0 4.6 %sort.17 = (s32[384]{0:T(512)}, s32[384]{0:T(512)S(1)}) sort(s32[384]{0:T(512)} %param.11, s32[384]{0:T(512)S(1)} %iota.15), dimensions={0}, to_apply=%region_0.0 | sort | flops 3456 | bytes 6144 | tf_op jit(solution)/shard_map/jit(argsort)/sort | solution.py:155
  6.6 3.6 gather_fusion.6
  10.9 7.3 %all-to-all-start.1 = ((s32[32,1,48]{2,1,0:T(1,128)}), s32[32,1,48]{2,1,0:T(1,128)S(1)}, u32[]{:S(2)}, u32[]{:S(2)}) async-start(s32[32,1,48]{2,1,0:T(1,128)} %bitcast.3), calls=%async_computation.1 | async-start | bytes 32768 | tf_op jit(solution)/shard_map/all_to_all | solution.py:159
  18.3 3.7 gather_fusion.5
  21.9 8.9 %gather_fusion.4 = bf16[384,3072]{1,0:T(8,128)(2,1)} fusion(bf16[384,3072]{1,0:T(8,128)(2,1)} %param.9, s32[1024]{0:T(1024)S(1)} %pad_clamp_fusion.3), kind=kCustom, calls=%fused_computation.4 | custom fusion | bytes 4720128 | tf_op jit(solution)/shard_map/gather | solution.py:182
  30.9 3.6 gather_fusion.3
  34.4 6.6 %shard_map.84 = bf16[32,48,768]{2,1,0:T(8,128)(2,1)} custom-call(bf16[384,3072]{1,0:T(8,128)(2,1)} %gather_fusion.3, bf16[384,3072]{1,0:T(8,128)(2,1)} %gather_fusion.4, bf16[384,3072]{1,0:T(8,128)(2,1)} %gather_fusion.5), custom_call_target="tpu_custom_call" | custom-call | bytes 4718592 | tf_op jit(solution)/shard_map/pallas_call | solution.py:92
  41.0 5.8 %all-to-all-start.3 = ((bf16[32,48,768]{2,1,0:T(8,128)(2,1)}), bf16[32,48,768]{2,1,0:T(8,128)(2,1)S(1)}, u32[]{:S(2)}, u32[]{:S(2)}) async-start(bf16[32,48,768]{2,1,0:T(8,128)(2,1)} %shard_map.84), calls=%async_computation.3 | async-start | bytes 4718592 | tf_op jit(solution)/shard_map/all_to_all | solution.py:200
  46.9 7.5 %shard_map.82 = bf16[32,48,1536]{2,1,0:T(8,128)(2,1)} custom-call(bf16[384,3072]{1,0:T(8,128)(2,1)} %gather_fusion.3, bf16[384,3072]{1,0:T(8,128)(2,1)} %gather_fusion.4, bf16[384,3072]{1,0:T(8,128)(2,1)} %gather_fusion.5), custom_call_target="tpu_custom_call" | custom-call | bytes 9437184 | tf_op jit(solution)/shard_map/pallas_call | solution.py:92
  54.3 46.9 %all-to-all-done.3 = bf16[32,48,768]{2,1,0:T(8,128)(2,1)S(1)} async-done(((bf16[32,48,768]{2,1,0:T(8,128)(2,1)}), bf16[32,48,768]{2,1,0:T(8,128)(2,1)S(1)}, u32[]{:S(2)}, u32[]{:S(2)}) %all-to-all-start.3) | async-done | bytes 2359328 | tf_op jit(solution)/shard_map/all_to_all | solution.py:200
  101.3 4.2 %all-to-all-start = ((bf16[32,48,1536]{2,1,0:T(8,128)(2,1)}), bf16[32,48,1536]{2,1,0:T(8,128)(2,1)}, u32[]{:S(2)}, u32[]{:S(2)}) async-start(bf16[32,48,1536]{2,1,0:T(8,128)(2,1)} %shard_map.82), calls=%async_computation | async-start | bytes 9437184 | tf_op jit(solution)/shard_map/all_to_all | solution.py:200
  106.8 6.2 %scatter_custom_fusion = s32[1536]{0:T(1024)S(1)} fusion(s32[1536]{0:T(1024)S(1)} %fusion, s32[1536]{0:T(1024)S(1)} %iota.16, s32[]{:T(128)} %constant.15.clone.1), kind=kCustom, calls=%fused_computation.30 | custom fusion | bytes 6148 | tf_op jit(solution)/shard_map/scatter | solution.py:164
  113.0 5.6 %gather_fusion.9 = bf16[1536,768]{1,0:T(8,128)(2,1)} fusion(bf16[1536,768]{1,0:T(8,128)(2,1)S(1)} %bitcast.11, s32[2048]{0:T(1024)S(1)} %pad_clamp_fusion.1), kind=kCustom, calls=%fused_computation.9 | custom fusion | bytes 4724736 | tf_op jit(solution)/shard_map/gather | solution.py:201
  118.7 3.2 fusion.8
  121.9 3.7 collective-permute-start.3
  127.0 84.2 %all-to-all-done = bf16[32,48,1536]{2,1,0:T(8,128)(2,1)} async-done(((bf16[32,48,1536]{2,1,0:T(8,128)(2,1)}), bf16[32,48,1536]{2,1,0:T(8,128)(2,1)}, u32[]{:S(2)}, u32[]{:S(2)}) %all-to-all-start) | async-done | bytes 4718624 | tf_op jit(solution)/shard_map/all_to_all | solution.py:200
  211.2 13.3 %gather_fusion.7 = bf16[1536,1536]{1,0:T(8,128)(2,1)} fusion(bf16[1536,1536]{1,0:T(8,128)(2,1)} %bitcast.2, s32[2048]{0:T(1024)S(1)} %pad_clamp_fusion.1), kind=kCustom, calls=%fused_computation.7 | custom fusion | bytes 9443328 | tf_op jit(solution)/shard_map/gather | solution.py:201
  224.6 5.1 %fusion.7 = (bf16[1152,1024]{1,0:T(8,128)(2,1)}, bf16[1152,1024]{1,0:T(8,128)(2,1)}) fusion(bf16[1536,1536]{1,0:T(8,128)(2,1)} %gather_fusion.7), kind=kLoop, calls=%fused_computation.38 | loop fusion | bytes 9437184 | tf_op jit(solution)/shard_map/slice | solution.py:204
  229.6 4.1 collective-permute-start.1
  241.7 3.1 pad_maximum_fusion.1.refs_0_.refs_1_.refs_2_.refs_3_.refs_4_.refs_5_.refs_6_.refs_7_
  244.9 14.2 %shard_map.85 = bf16[1536,256]{1,0:T(8,128)(2,1)} custom-call(s32[16]{0:T(128)} %reshape.105.win_ref, s32[16]{0:T(128)} %gather_fusion.1, s32[4]{0:T(128)} %slice.31.vco_ref, bf16[1536,256]{1,0:T(8,128)(2,1)} %slice.68.q_ref, bf16[3840,512]{1,0:T(8,128)(2,1)} %pad_maximum_fusion.1.refs_0_.refs_1_.refs_2_.refs_3_.refs_4_.refs_5_.refs_6_.refs_7_, ...), custom_call_target="tpu_custom_call" | custom-call | flops 2415919104 | bytes 7864320 | tf_op jit(solution)/shard_map/pallas_call | solution.py:68
  259.1 5.8 %gather_fusion.10 = bf16[1536,256]{1,0:T(8,128)(2,1)} fusion(bf16[1536,256]{1,0:T(8,128)(2,1)} %shard_map.85, s32[2048]{0:T(1024)S(1)} %pad_clamp_fusion), kind=kCustom, calls=%fused_computation.10 | custom fusion | bytes 1579008 | tf_op jit(solution)/shard_map/gather | solution.py:208
  264.9 52.9 %all-to-all-start.4 = ((bf16[32,48,256]{2,1,0:T(8,128)(2,1)}), bf16[32,48,256]{2,1,0:T(8,128)(2,1)S(1)}, u32[]{:S(2)}, u32[]{:S(2)}) async-start(bf16[32,48,256]{2,1,0:T(8,128)(2,1)} %bitcast.7), calls=%async_computation.4 | async-start | bytes 1572864 | tf_op jit(solution)/shard_map/all_to_all | solution.py:209
  317.8 2.7 slice.64.q_ref
  322.4 6.1 %pad_maximum_fusion.refs_0_.refs_1_.refs_2_.refs_3_.refs_4_.refs_5_.refs_6_.refs_7_ = bf16[3840,1024]{1,0:T(8,128)(2,1)} fusion(bf16[1152,1024]{1,0:T(8,128)(2,1)} %collective-permute-done.2, bf16[1536,1024]{1,0:T(8,128)(2,1)S(1)} %slice-done, bf16[1152,1024]{1,0:T(8,128)(2,1)} %collective-permute-done.1), kind=kLoop, calls=%fused_computation.14 | loop fusion | flops 23592960 | bytes 15728640 | tf_op jit(solution)/shard_map/concatenate | solution.py:206
  328.4 26.2 %shard_map.83 = bf16[1536,512]{1,0:T(8,128)(2,1)} custom-call(s32[16]{0:T(128)} %reshape.105.win_ref, s32[16]{0:T(128)} %gather_fusion.1, s32[4]{0:T(128)} %slice.31.vco_ref, bf16[1536,512]{1,0:T(8,128)(2,1)} %slice.64.q_ref, bf16[3840,1024]{1,0:T(8,128)(2,1)} %pad_maximum_fusion.refs_0_.refs_1_.refs_2_.refs_3_.refs_4_.refs_5_.refs_6_.refs_7_, ...), custom_call_target="tpu_custom_call" | custom-call | flops 4831838208 | bytes 15728640 | tf_op jit(solution)/shard_map/pallas_call | solution.py:68
  354.6 7.1 %gather_fusion.8 = bf16[1536,512]{1,0:T(8,128)(2,1)} fusion(bf16[1536,512]{1,0:T(8,128)(2,1)} %shard_map.83, s32[2048]{0:T(1024)S(1)} %pad_clamp_fusion), kind=kCustom, calls=%fused_computation.8 | custom fusion | bytes 3151872 | tf_op jit(solution)/shard_map/gather | solution.py:208
  361.7 5.8 %all-to-all-start.2 = ((bf16[32,48,512]{2,1,0:T(8,128)(2,1)}), bf16[32,48,512]{2,1,0:T(8,128)(2,1)S(1)}, u32[]{:S(2)}, u32[]{:S(2)}) async-start(bf16[32,48,512]{2,1,0:T(8,128)(2,1)} %bitcast.5), calls=%async_computation.2 | async-start | bytes 3145728 | tf_op jit(solution)/shard_map/all_to_all | solution.py:209
  367.5 3.3 scatter_custom_fusion.1
  370.8 34.3 %all-to-all-done.2.refs_0_ = bf16[32,48,512]{2,1,0:T(8,128)(2,1)S(1)} async-done(((bf16[32,48,512]{2,1,0:T(8,128)(2,1)}), bf16[32,48,512]{2,1,0:T(8,128)(2,1)S(1)}, u32[]{:S(2)}, u32[]{:S(2)}) %all-to-all-start.2) | async-done | bytes 1572896 | tf_op jit(solution)/shard_map/all_to_all | solution.py:209
  406.3 5.9 %shard_map.86 = bf16[384,3072]{1,0:T(8,128)(2,1)} custom-call(bf16[32,48,512]{2,1,0:T(8,128)(2,1)} %copy-done.4, bf16[32,48,256]{2,1,0:T(8,128)(2,1)} %copy-done.5), custom_call_target="tpu_custom_call" | custom-call | bytes 4718592 | tf_op jit(solution)/shard_map/pallas_call | solution.py:119
  412.2 8.9 %gather_fusion.11 = bf16[384,3072]{1,0:T(8,128)(2,1)} fusion(bf16[384,3072]{1,0:T(8,128)(2,1)} %shard_map.86, s32[1024]{0:T(1024)S(1)} %pad_clamp_fusion.2), kind=kCustom, calls=%fused_computation.11 | custom fusion | bytes 4720128 | tf_op jit(solution)/shard_map/gather | solution.py:220
  (62 shorter events, 15.4 us)
Async XLA Ops:
  0.0 18.3 %copy-start = (bf16[384,3072]{1,0:T(8,128)(2,1)S(1)}, bf16[384,3072]{1,0:T(8,128)(2,1)}, u32[]{:S(2)}) copy-start(bf16[384,3072]{1,0:T(8,128)(2,1)} %param.10) | copy-start | bytes 7077892
  6.0 0.6 copy-start.6
  10.9 30.1 %all-to-all-start.1 = ((s32[32,1,48]{2,1,0:T(1,128)}), s32[32,1,48]{2,1,0:T(1,128)S(1)}, u32[]{:S(2)}, u32[]{:S(2)}) async-start(s32[32,1,48]{2,1,0:T(1,128)} %bitcast.3), calls=%async_computation.1 | async-start | bytes 32768 | tf_op jit(solution)/shard_map/all_to_all | solution.py:159
  21.9 8.9 %copy-start.3 = (bf16[384,3072]{1,0:T(8,128)(2,1)S(1)}, bf16[384,3072]{1,0:T(8,128)(2,1)}, u32[]{:S(2)}) copy-start(bf16[384,3072]{1,0:T(8,128)(2,1)} %param.8) | copy-start | bytes 7077892
  41.0 60.2 %all-to-all-start.3 = ((bf16[32,48,768]{2,1,0:T(8,128)(2,1)}), bf16[32,48,768]{2,1,0:T(8,128)(2,1)S(1)}, u32[]{:S(2)}, u32[]{:S(2)}) async-start(bf16[32,48,768]{2,1,0:T(8,128)(2,1)} %shard_map.84), calls=%async_computation.3 | async-start | bytes 4718592 | tf_op jit(solution)/shard_map/all_to_all | solution.py:200
  54.3 51.2 %copy-start.7 = (s32[8]{0:T(128)S(1)}, s32[8]{0:T(128)}, u32[]{:S(2)}) copy-start(s32[8]{0:T(128)} %constant.38.clone) | copy-start | bytes 100
  101.3 110.0 %all-to-all-start = ((bf16[32,48,1536]{2,1,0:T(8,128)(2,1)}), bf16[32,48,1536]{2,1,0:T(8,128)(2,1)}, u32[]{:S(2)}, u32[]{:S(2)}) async-start(bf16[32,48,1536]{2,1,0:T(8,128)(2,1)} %shard_map.82), calls=%async_computation | async-start | bytes 9437184 | tf_op jit(solution)/shard_map/all_to_all | solution.py:200
  121.9 119.8 %collective-permute-start.3 = (bf16[1152,512]{1,0:T(8,128)(2,1)}, bf16[1152,512]{1,0:T(8,128)(2,1)S(1)}, u32[]{:S(2)}, u32[]{:S(2)}) collective-permute-start(bf16[1152,512]{1,0:T(8,128)(2,1)} %get-tuple-element.11), channel_id=1, source_target_pairs={{0,4},{4,12},{12,8},{8,16},{16,20},{20,28},{28,24},{1,5},{5,13},{1... | collective-permute-start | bytes 3538952 | tf_op jit(solution)/shard_map/ppermute | solution.py:204
  125.6 116.2 %collective-permute-start.4 = (bf16[1152,512]{1,0:T(8,128)(2,1)}, bf16[1152,512]{1,0:T(8,128)(2,1)}, u32[]{:S(2)}, u32[]{:S(2)}) collective-permute-start(bf16[1152,512]{1,0:T(8,128)(2,1)} %get-tuple-element.12), channel_id=1, source_target_pairs={{4,0},{12,4},{8,12},{16,8},{20,16},{28,20},{24,28},{5,1},{13,5},{9... | collective-permute-start | bytes 3538952 | tf_op jit(solution)/shard_map/ppermute | solution.py:205
  224.6 10.4 %copy-start.8 = (s32[4,4]{1,0:T(4,128)S(1)}, s32[4,4]{1,0:T(4,128)}, u32[]{:S(2)}) copy-start(s32[4,4]{1,0:T(4,128)} %param.12) | copy-start | bytes 196
  224.6 11.7 %copy-start.2 = (s32[32]{0:T(128)S(1)}, s32[32]{0:T(128)}, u32[]{:S(2)}) copy-start(s32[32]{0:T(128)} %param.13) | copy-start | bytes 388
  229.6 90.8 %collective-permute-start.1 = (bf16[1152,1024]{1,0:T(8,128)(2,1)}, bf16[1152,1024]{1,0:T(8,128)(2,1)}, u32[]{:S(2)}, u32[]{:S(2)}) collective-permute-start(bf16[1152,1024]{1,0:T(8,128)(2,1)} %get-tuple-element.9), channel_id=1, source_target_pairs={{0,4},{4,12},{12,8},{8,16},{16,20},{20,28},{28,24},{1,5},{5,13},{1... | collective-permute-start | bytes 7077896 | tf_op jit(solution)/shard_map/ppermute | solution.py:204
  233.7 86.8 %collective-permute-start.2 = (bf16[1152,1024]{1,0:T(8,128)(2,1)}, bf16[1152,1024]{1,0:T(8,128)(2,1)}, u32[]{:S(2)}, u32[]{:S(2)}) collective-permute-start(bf16[1152,1024]{1,0:T(8,128)(2,1)} %get-tuple-element.10), channel_id=1, source_target_pairs={{4,0},{12,4},{8,12},{16,8},{20,16},{28,20},{24,28},{5,1},{13,5},{9... | collective-permute-start | bytes 7077896 | tf_op jit(solution)/shard_map/ppermute | solution.py:205
  235.0 2.5 collective-permute-start
  239.5 2.2 slice-start.1
  264.9 96.8 %all-to-all-start.4 = ((bf16[32,48,256]{2,1,0:T(8,128)(2,1)}), bf16[32,48,256]{2,1,0:T(8,128)(2,1)S(1)}, u32[]{:S(2)}, u32[]{:S(2)}) async-start(bf16[32,48,256]{2,1,0:T(8,128)(2,1)} %bitcast.7), calls=%async_computation.4 | async-start | bytes 1572864 | tf_op jit(solution)/shard_map/all_to_all | solution.py:209
  320.5 1.9 slice-start
  361.7 43.5 %copy-start.5 = (bf16[32,48,256]{2,1,0:T(8,128)(2,1)}, bf16[32,48,256]{2,1,0:T(8,128)(2,1)S(1)}, u32[]{:S(2)}) copy-start(bf16[32,48,256]{2,1,0:T(8,128)(2,1)S(1)} %all-to-all-done.4.refs_1_) | copy-start | bytes 2359300
  361.7 43.5 %all-to-all-start.2 = ((bf16[32,48,512]{2,1,0:T(8,128)(2,1)}), bf16[32,48,512]{2,1,0:T(8,128)(2,1)S(1)}, u32[]{:S(2)}, u32[]{:S(2)}) async-start(bf16[32,48,512]{2,1,0:T(8,128)(2,1)} %bitcast.5), calls=%async_computation.2 | async-start | bytes 3145728 | tf_op jit(solution)/shard_map/all_to_all | solution.py:209
  405.2 1.1 copy-start.4
  412.2 8.9 %copy-start.1 = (bf16[384,3072]{1,0:T(8,128)(2,1)S(1)}, bf16[384,3072]{1,0:T(8,128)(2,1)}, u32[]{:S(2)}) copy-start(bf16[384,3072]{1,0:T(8,128)(2,1)} %param.10) | copy-start | bytes 7077892

commit v4 on v2

--- a/solution.py
+++ b/solution.py
@@ -14,27 +14,28 @@
     k_refs = refs[:win]
     v_refs = refs[win : 2 * win]
     o_ref = refs[2 * win]
-    s_scr = refs[2 * win + 1]
     i = pl.program_id(0)
     q = q_ref[...]
-    col = lax.broadcasted_iota(jnp.int32, (tile, tile), 1)
+    col = lax.broadcasted_iota(jnp.int32, (1, tile), 1)
+    scores = []
+    top = None
     for w in range(win):
         s = lax.dot_general(
             q, k_refs[w][...], (((1,), (1,)), ((), ())), preferred_element_type=jnp.float32
         )
         s = s * scale
         s = jnp.where(col < vcw_ref[i * win + w], s, -jnp.inf)
-        s_scr[:, w * tile : (w + 1) * tile] = s
-    s = s_scr[...]
-    m = jnp.max(s, axis=1, keepdims=True)
-    p = jnp.exp(s - m)
-    total = jnp.sum(p, axis=1, keepdims=True)
-    pb = p.astype(jnp.bfloat16)
-    acc = jnp.dot(pb[:, 0:tile], v_refs[0][...], preferred_element_type=jnp.float32)
-    for w in range(1, win):
-        acc = acc + jnp.dot(
-            pb[:, w * tile : (w + 1) * tile], v_refs[w][...], preferred_element_type=jnp.float32
-        )
+        scores.append(s)
+        m = jnp.max(s, axis=1, keepdims=True)
+        top = m if top is None else jnp.maximum(top, m)
+    total = None
+    acc = None
+    for w in range(win):
+        p = jnp.exp(scores[w] - top)
+        part = jnp.sum(p, axis=1, keepdims=True)
+        mix = jnp.dot(p.astype(jnp.bfloat16), v_refs[w][...], preferred_element_type=jnp.float32)
+        total = part if total is None else total + part
+        acc = mix if acc is None else acc + mix
     out = acc / total
     row = lax.broadcasted_iota(jnp.int32, (tile, 1), 0)
     out = jnp.where(row < vco_ref[i], out, 0.0)
@@ -73,7 +74,6 @@
             grid=(tile_dev, heads_here),
             in_specs=in_specs,
             out_specs=pl.BlockSpec(blk, q_map),
-            scratch_shapes=[pltpu.VMEM((tile, win * tile), jnp.float32)],
         ),
         cost_estimate=cost,
     )(win_flat, vcw_flat, vc_own, q_tile, *([kv_ext] * (2 * win)))

time: 370 us -> 371 us (level)
  starting transfers between devices: 60.1 us -> 65 us
  Pallas kernels: 60.3 us -> 55.6 us
    all_to_all x2, starting transfers between devices: 30 us -> 34.9 us  [body(): lax.all_to_all(outgoing, ('seq', 'head'), split_axis=0, concat_axis=0, ti...]
    pallas_call x2, Pallas kernels: 40.4 us -> 35.8 us  [attention(): pl.pallas_call(functools.partial(attn_kernel, win, tile, scale), out_shap...]
  transfers between devices with their start and end apart: 10 -> 10, of which waited for: 3 -> 3; matrix products, arithmetic and copies ran while one was open for 23% -> 23% of each run, Pallas kernels for 15% -> 13%
where the time goes in v4:
time: 371 us; the launch traced here: 369 us
  waiting for transfers between devices  138 us (37%)
  local copies, waits for them, and re-layouts  90.8 us (24%)
  starting transfers between devices  65 us (18%)
  Pallas kernels  55.6 us (15%)
  other arithmetic  17.6 us (5%)
    all_to_all x2, waiting for transfers between devices, body(): lax.all_to_all(send, ('seq', 'head'), split_axis=0, concat_axis=0, tiled=...  113 us
    pallas_call x2, Pallas kernels, attention(): pl.pallas_call(functools.partial(attn_kernel, win, tile, scale), out_shap...  35.8 us
    all_to_all x2, starting transfers between devices, body(): lax.all_to_all(outgoing, ('seq', 'head'), split_axis=0, concat_axis=0, ti...  34.9 us
    all_to_all x2, waiting for transfers between devices, body(): lax.all_to_all(outgoing, ('seq', 'head'), split_axis=0, concat_axis=0, ti...  25.9 us
    gather x2, local copies, waits for them, and re-layouts, body(): got_tile = got.reshape(tok_dev, 3 * chunk_width)[place]  17 us
    gather x3, local copies, waits for them, and re-layouts, body(): rows_flat = [x[send_order] for x in (query, key, value)]  16 us
    pallas_call x2, Pallas kernels, pack(): pl.pallas_call(functools.partial(pack_kernel, head_count, part_width, chu...  14 us
    gather x2, local copies, waits for them, and re-layouts, body(): outgoing = out_tile[local].reshape(devices, share, chunk_width)  13 us
  transfers between devices with their start and end apart: 10, of which 3 were waited for; matrix products, arithmetic and copies ran while one was open for 23% of the time, Pallas kernels for 13%

profile of v4, /device:TPU:0, one launch (start us, length us, event | category | flops | bytes accessed | tf_op | source)
XLA Modules:
  0.0 369.0 jit_solution(1538469088833460304)
XLA Ops:
  0.0 4.6 %sort.17 = (s32[384]{0:T(512)}, s32[384]{0:T(512)S(1)}) sort(s32[384]{0:T(512)} %param.11, s32[384]{0:T(512)S(1)} %iota.15), dimensions={0}, to_apply=%region_0.0 | sort | flops 3456 | bytes 6144 | tf_op jit(solution)/shard_map/jit(argsort)/sort | solution.py:150
  6.6 3.6 gather_fusion.6
  10.9 7.3 %all-to-all-start.1 = ((s32[32,1,48]{2,1,0:T(1,128)}), s32[32,1,48]{2,1,0:T(1,128)S(1)}, u32[]{:S(2)}, u32[]{:S(2)}) async-start(s32[32,1,48]{2,1,0:T(1,128)} %bitcast.3), calls=%async_computation.1 | async-start | bytes 32768 | tf_op jit(solution)/shard_map/all_to_all | solution.py:154
  18.2 3.6 gather_fusion.5
  21.8 8.9 %gather_fusion.4 = bf16[384,3072]{1,0:T(8,128)(2,1)} fusion(bf16[384,3072]{1,0:T(8,128)(2,1)} %param.9, s32[1024]{0:T(1024)S(1)} %pad_clamp_fusion.3), kind=kCustom, calls=%fused_computation.4 | custom fusion | bytes 4720128 | tf_op jit(solution)/shard_map/gather | solution.py:177
  30.7 3.6 gather_fusion.3
  34.3 7.0 %shard_map.82 = bf16[32,48,1152]{2,1,0:T(8,128)(2,1)} custom-call(bf16[384,3072]{1,0:T(8,128)(2,1)} %gather_fusion.3, bf16[384,3072]{1,0:T(8,128)(2,1)} %gather_fusion.4, bf16[384,3072]{1,0:T(8,128)(2,1)} %gather_fusion.5), custom_call_target="tpu_custom_call" | custom-call | bytes 7077888 | tf_op jit(solution)/shard_map/pallas_call | solution.py:92
  41.9 5.9 %all-to-all-start = ((bf16[32,48,1152]{2,1,0:T(8,128)(2,1)}), bf16[32,48,1152]{2,1,0:T(8,128)(2,1)}, u32[]{:S(2)}, u32[]{:S(2)}) async-start(bf16[32,48,1152]{2,1,0:T(8,128)(2,1)} %shard_map.82), calls=%async_computation | async-start | bytes 7077888 | tf_op jit(solution)/shard_map/all_to_all | solution.py:190
  47.8 7.0 %shard_map.84 = bf16[32,48,1152]{2,1,0:T(8,128)(2,1)} custom-call(bf16[384,3072]{1,0:T(8,128)(2,1)} %gather_fusion.3, bf16[384,3072]{1,0:T(8,128)(2,1)} %gather_fusion.4, bf16[384,3072]{1,0:T(8,128)(2,1)} %gather_fusion.5), custom_call_target="tpu_custom_call" | custom-call | bytes 7077888 | tf_op jit(solution)/shard_map/pallas_call | solution.py:92
  54.8 72.7 %all-to-all-done = bf16[32,48,1152]{2,1,0:T(8,128)(2,1)} async-done(((bf16[32,48,1152]{2,1,0:T(8,128)(2,1)}), bf16[32,48,1152]{2,1,0:T(8,128)(2,1)}, u32[]{:S(2)}, u32[]{:S(2)}) %all-to-all-start) | async-done | bytes 3538976 | tf_op jit(solution)/shard_map/all_to_all | solution.py:190
  127.5 4.1 %all-to-all-start.3 = ((bf16[32,48,1152]{2,1,0:T(8,128)(2,1)}), bf16[32,48,1152]{2,1,0:T(8,128)(2,1)S(1)}, u32[]{:S(2)}, u32[]{:S(2)}) async-start(bf16[32,48,1152]{2,1,0:T(8,128)(2,1)} %shard_map.84), calls=%async_computation.3 | async-start | bytes 7077888 | tf_op jit(solution)/shard_map/all_to_all | solution.py:190
  135.7 6.3 %scatter_custom_fusion = s32[1536]{0:T(1024)S(1)} fusion(s32[1536]{0:T(1024)S(1)} %fusion, s32[1536]{0:T(1024)} %iota.16, s32[]{:T(128)} %constant.15.clone.1), kind=kCustom, calls=%fused_computation.30 | custom fusion | bytes 6656 | tf_op jit(solution)/shard_map/scatter | solution.py:159
  142.7 10.9 %gather_fusion.7 = bf16[1536,1152]{1,0:T(8,128)(2,1)} fusion(bf16[1536,1152]{1,0:T(8,128)(2,1)} %bitcast.2, s32[2048]{0:T(1024)S(1)} %pad_clamp_fusion.1), kind=kCustom, calls=%fused_computation.7 | custom fusion | bytes 7084032 | tf_op jit(solution)/shard_map/gather | solution.py:191
  153.6 4.1 %fusion.8 = (bf16[1152,768]{1,0:T(8,128)(2,1)}, bf16[1152,768]{1,0:T(8,128)(2,1)}) fusion(bf16[1536,1152]{1,0:T(8,128)(2,1)} %gather_fusion.7), kind=kLoop, calls=%fused_computation.39 | loop fusion | bytes 7077888 | tf_op jit(solution)/shard_map/slice | solution.py:194
  157.7 4.9 %collective-permute-start.1 = (bf16[1152,768]{1,0:T(8,128)(2,1)}, bf16[1152,768]{1,0:T(8,128)(2,1)}, u32[]{:S(2)}, u32[]{:S(2)}) collective-permute-start(bf16[1152,768]{1,0:T(8,128)(2,1)} %get-tuple-element.11), channel_id=1, source_target_pairs={{0,4},{4,12},{12,8},{8,16},{16,20},{20,28},{28,24},{1,5},{5,13},{1... | collective-permute-start | bytes 5308424 | tf_op jit(solution)/shard_map/ppermute | solution.py:194
  169.8 2.4 slice.64.q_ref
  172.2 39.8 %all-to-all-done.3 = bf16[32,48,1152]{2,1,0:T(8,128)(2,1)S(1)} async-done(((bf16[32,48,1152]{2,1,0:T(8,128)(2,1)}), bf16[32,48,1152]{2,1,0:T(8,128)(2,1)S(1)}, u32[]{:S(2)}, u32[]{:S(2)}) %all-to-all-start.3) | async-done | bytes 3538976 | tf_op jit(solution)/shard_map/all_to_all | solution.py:190
  212.0 6.1 %gather_fusion.9 = bf16[1536,1152]{1,0:T(8,128)(2,1)} fusion(bf16[1536,1152]{1,0:T(8,128)(2,1)S(1)} %bitcast.11, s32[2048]{0:T(1024)S(1)} %copy-done.7), kind=kCustom, calls=%fused_computation.9 | custom fusion | bytes 7084032 | tf_op jit(solution)/shard_map/gather | solution.py:191
  218.1 4.2 %fusion.7 = (bf16[1152,768]{1,0:T(8,128)(2,1)}, bf16[1152,768]{1,0:T(8,128)(2,1)}) fusion(bf16[1536,1152]{1,0:T(8,128)(2,1)} %gather_fusion.9), kind=kLoop, calls=%fused_computation.38 | loop fusion | bytes 7077888 | tf_op jit(solution)/shard_map/slice | solution.py:194
  222.3 4.0 %collective-permute-start.3 = (bf16[1152,768]{1,0:T(8,128)(2,1)}, bf16[1152,768]{1,0:T(8,128)(2,1)}, u32[]{:S(2)}, u32[]{:S(2)}) collective-permute-start(bf16[1152,768]{1,0:T(8,128)(2,1)} %get-tuple-element.9), channel_id=1, source_target_pairs={{0,4},{4,12},{12,8},{8,16},{16,20},{20,28},{28,24},{1,5},{5,13},{1... | collective-permute-start | bytes 5308424 | tf_op jit(solution)/shard_map/ppermute | solution.py:194
  227.6 5.1 %pad_maximum_fusion.refs_0_.refs_1_.refs_2_.refs_3_.refs_4_.refs_5_.refs_6_.refs_7_ = bf16[3840,768]{1,0:T(8,128)(2,1)} fusion(bf16[1152,768]{1,0:T(8,128)(2,1)} %collective-permute-done.2, bf16[1536,768]{1,0:T(8,128)(2,1)S(1)} %slice-done, bf16[1152,768]{1,0:T(8,128)(2,1)} %collective-permute-done.1), kind=kLoop, calls=%fused_computation.14 | loop fusion | flops 17694720 | bytes 11796480 | tf_op jit(solution)/shard_map/concatenate | solution.py:196
  232.7 17.9 %shard_map.83 = bf16[1536,384]{1,0:T(8,128)(2,1)} custom-call(s32[16]{0:T(128)} %reshape.105.win_ref, s32[16]{0:T(128)} %gather_fusion.1, s32[4]{0:T(128)} %slice.31.vco_ref, bf16[1536,384]{1,0:T(8,128)(2,1)} %slice.64.q_ref, bf16[3840,768]{1,0:T(8,128)(2,1)} %pad_maximum_fusion.refs_0_.refs_1_.refs_2_.refs_3_.refs_4_.refs_5_.refs_6_.refs_7_, ...), custom_call_target="tpu_custom_call" | custom-call | flops 3623878656 | bytes 11796480 | tf_op jit(solution)/shard_map/pallas_call | solution.py:69
  250.6 6.6 %gather_fusion.8 = bf16[1536,384]{1,0:T(8,128)(2,1)} fusion(bf16[1536,384]{1,0:T(8,128)(2,1)} %shard_map.83, s32[2048]{0:T(1024)S(1)} %pad_clamp_fusion), kind=kCustom, calls=%fused_computation.8 | custom fusion | bytes 2365440 | tf_op jit(solution)/shard_map/gather | solution.py:198
  257.1 24.4 %all-to-all-start.2 = ((bf16[32,48,384]{2,1,0:T(8,128)(2,1)}), bf16[32,48,384]{2,1,0:T(8,128)(2,1)}, u32[]{:S(2)}, u32[]{:S(2)}) async-start(bf16[32,48,384]{2,1,0:T(8,128)(2,1)} %bitcast.12), calls=%async_computation.2 | async-start | bytes 2359296 | tf_op jit(solution)/shard_map/all_to_all | solution.py:199
  284.3 5.1 %pad_maximum_fusion.1.refs_0_.refs_1_.refs_2_.refs_3_.refs_4_.refs_5_.refs_6_.refs_7_ = bf16[3840,768]{1,0:T(8,128)(2,1)} fusion(bf16[1152,768]{1,0:T(8,128)(2,1)} %collective-permute-done.4, bf16[1536,768]{1,0:T(8,128)(2,1)S(1)} %slice-done.1, bf16[1152,768]{1,0:T(8,128)(2,1)} %collective-permute-done.3), kind=kLoop, calls=%fused_computation.15 | loop fusion | flops 17694720 | bytes 11796480 | tf_op jit(solution)/shard_map/concatenate | solution.py:196
  289.4 17.9 %shard_map.85 = bf16[1536,384]{1,0:T(8,128)(2,1)} custom-call(s32[16]{0:T(128)} %reshape.105.win_ref, s32[16]{0:T(128)} %gather_fusion.1, s32[4]{0:T(128)} %slice.31.vco_ref, bf16[1536,384]{1,0:T(8,128)(2,1)} %slice.68.q_ref, bf16[3840,768]{1,0:T(8,128)(2,1)} %pad_maximum_fusion.1.refs_0_.refs_1_.refs_2_.refs_3_.refs_4_.refs_5_.refs_6_.refs_7_, ...), custom_call_target="tpu_custom_call" | custom-call | flops 3623878656 | bytes 11796480 | tf_op jit(solution)/shard_map/pallas_call | solution.py:69
  307.3 6.4 %gather_fusion.10 = bf16[1536,384]{1,0:T(8,128)(2,1)} fusion(bf16[1536,384]{1,0:T(8,128)(2,1)} %shard_map.85, s32[2048]{0:T(1024)S(1)} %pad_clamp_fusion), kind=kCustom, calls=%fused_computation.10 | custom fusion | bytes 2365440 | tf_op jit(solution)/shard_map/gather | solution.py:198
  313.7 10.5 %all-to-all-start.4 = ((bf16[32,48,384]{2,1,0:T(8,128)(2,1)}), bf16[32,48,384]{2,1,0:T(8,128)(2,1)S(1)}, u32[]{:S(2)}, u32[]{:S(2)}) async-start(bf16[32,48,384]{2,1,0:T(8,128)(2,1)} %bitcast.7), calls=%async_computation.4 | async-start | bytes 2359296 | tf_op jit(solution)/shard_map/all_to_all | solution.py:199
  324.3 3.0 scatter_custom_fusion.1
  327.3 25.9 %all-to-all-done.4.refs_1_ = bf16[32,48,384]{2,1,0:T(8,128)(2,1)S(1)} async-done(((bf16[32,48,384]{2,1,0:T(8,128)(2,1)}), bf16[32,48,384]{2,1,0:T(8,128)(2,1)S(1)}, u32[]{:S(2)}, u32[]{:S(2)}) %all-to-all-start.4) | async-done | bytes 1179680 | tf_op jit(solution)/shard_map/all_to_all | solution.py:199
  354.3 5.9 %shard_map.86 = bf16[384,3072]{1,0:T(8,128)(2,1)} custom-call(bf16[32,48,384]{2,1,0:T(8,128)(2,1)} %all-to-all-done.2.refs_0_, bf16[32,48,384]{2,1,0:T(8,128)(2,1)} %copy-done.5), custom_call_target="tpu_custom_call" | custom-call | bytes 4718592 | tf_op jit(solution)/shard_map/pallas_call | solution.py:115
  360.2 8.9 %gather_fusion.11 = bf16[384,3072]{1,0:T(8,128)(2,1)} fusion(bf16[384,3072]{1,0:T(8,128)(2,1)} %shard_map.86, s32[1024]{0:T(1024)S(1)} %pad_clamp_fusion.2), kind=kCustom, calls=%fused_computation.11 | custom fusion | bytes 4720128 | tf_op jit(solution)/shard_map/gather | solution.py:210
  (68 shorter events, 19.0 us)
Async XLA Ops:
  0.0 18.2 %copy-start = (bf16[384,3072]{1,0:T(8,128)(2,1)S(1)}, bf16[384,3072]{1,0:T(8,128)(2,1)}, u32[]{:S(2)}) copy-start(bf16[384,3072]{1,0:T(8,128)(2,1)} %param.10) | copy-start | bytes 7077892
  6.0 0.6 copy-start.10
  10.9 30.4 %all-to-all-start.1 = ((s32[32,1,48]{2,1,0:T(1,128)}), s32[32,1,48]{2,1,0:T(1,128)S(1)}, u32[]{:S(2)}, u32[]{:S(2)}) async-start(s32[32,1,48]{2,1,0:T(1,128)} %bitcast.3), calls=%async_computation.1 | async-start | bytes 32768 | tf_op jit(solution)/shard_map/all_to_all | solution.py:154
  21.8 8.9 %copy-start.3 = (bf16[384,3072]{1,0:T(8,128)(2,1)S(1)}, bf16[384,3072]{1,0:T(8,128)(2,1)}, u32[]{:S(2)}) copy-start(bf16[384,3072]{1,0:T(8,128)(2,1)} %param.8) | copy-start | bytes 7077892
  41.3 0.6 copy-start.8
  41.9 85.7 %all-to-all-start = ((bf16[32,48,1152]{2,1,0:T(8,128)(2,1)}), bf16[32,48,1152]{2,1,0:T(8,128)(2,1)}, u32[]{:S(2)}, u32[]{:S(2)}) async-start(bf16[32,48,1152]{2,1,0:T(8,128)(2,1)} %shard_map.82), calls=%async_computation | async-start | bytes 7077888 | tf_op jit(solution)/shard_map/all_to_all | solution.py:190
  54.8 76.8 %copy-start.11 = (s32[8]{0:T(128)S(1)}, s32[8]{0:T(128)}, u32[]{:S(2)}) copy-start(s32[8]{0:T(128)} %constant.38.clone) | copy-start | bytes 100
  127.5 84.5 %all-to-all-start.3 = ((bf16[32,48,1152]{2,1,0:T(8,128)(2,1)}), bf16[32,48,1152]{2,1,0:T(8,128)(2,1)S(1)}, u32[]{:S(2)}, u32[]{:S(2)}) async-start(bf16[32,48,1152]{2,1,0:T(8,128)(2,1)} %shard_map.84), calls=%async_computation.3 | async-start | bytes 7077888 | tf_op jit(solution)/shard_map/all_to_all | solution.py:190
  135.1 7.0 %copy-start.9 = (s32[1536]{0:T(1024)}, s32[1536]{0:T(1024)S(1)}, u32[]{:S(2)}) copy-start(s32[1536]{0:T(1024)S(1)} %fusion) | copy-start | bytes 18436
  142.1 0.6 copy-start.6
  153.6 12.3 %copy-start.2 = (s32[32]{0:T(128)S(1)}, s32[32]{0:T(128)}, u32[]{:S(2)}) copy-start(s32[32]{0:T(128)} %param.13) | copy-start | bytes 388
  157.7 69.9 %collective-permute-start.1 = (bf16[1152,768]{1,0:T(8,128)(2,1)}, bf16[1152,768]{1,0:T(8,128)(2,1)}, u32[]{:S(2)}, u32[]{:S(2)}) collective-permute-start(bf16[1152,768]{1,0:T(8,128)(2,1)} %get-tuple-element.11), channel_id=1, source_target_pairs={{0,4},{4,12},{12,8},{8,16},{16,20},{20,28},{28,24},{1,5},{5,13},{1... | collective-permute-start | bytes 5308424 | tf_op jit(solution)/shard_map/ppermute | solution.py:194
  162.6 65.0 %collective-permute-start.2 = (bf16[1152,768]{1,0:T(8,128)(2,1)}, bf16[1152,768]{1,0:T(8,128)(2,1)}, u32[]{:S(2)}, u32[]{:S(2)}) collective-permute-start(bf16[1152,768]{1,0:T(8,128)(2,1)} %get-tuple-element.12), channel_id=1, source_target_pairs={{4,0},{12,4},{8,12},{16,8},{20,16},{28,20},{24,28},{5,1},{13,5},{9... | collective-permute-start | bytes 5308424 | tf_op jit(solution)/shard_map/ppermute | solution.py:195
  163.8 3.3 collective-permute-start
  172.2 39.8 %copy-start.7 = (s32[2048]{0:T(1024)S(1)}, s32[2048]{0:T(1024)}, u32[]{:S(2)}) copy-start(s32[2048]{0:T(1024)} %copy-done.6) | copy-start | bytes 24580
  218.1 9.5 %slice-start = ((bf16[1536,1152]{1,0:T(8,128)(2,1)}), bf16[1536,768]{1,0:T(8,128)(2,1)S(1)}, s32[]{:S(2)}) async-start(bf16[1536,1152]{1,0:T(8,128)(2,1)} %gather_fusion.7), calls=%async_computation.5 | async-start | bytes 4718592 | tf_op jit(solution)/shard_map/slice | solution.py:193
  222.3 60.4 %collective-permute-start.3 = (bf16[1152,768]{1,0:T(8,128)(2,1)}, bf16[1152,768]{1,0:T(8,128)(2,1)}, u32[]{:S(2)}, u32[]{:S(2)}) collective-permute-start(bf16[1152,768]{1,0:T(8,128)(2,1)} %get-tuple-element.9), channel_id=1, source_target_pairs={{0,4},{4,12},{12,8},{8,16},{16,20},{20,28},{28,24},{1,5},{5,13},{1... | collective-permute-start | bytes 5308424 | tf_op jit(solution)/shard_map/ppermute | solution.py:194
  226.3 56.4 %collective-permute-start.4 = (bf16[1152,768]{1,0:T(8,128)(2,1)}, bf16[1152,768]{1,0:T(8,128)(2,1)}, u32[]{:S(2)}, u32[]{:S(2)}) collective-permute-start(bf16[1152,768]{1,0:T(8,128)(2,1)} %get-tuple-element.10), channel_id=1, source_target_pairs={{4,0},{12,4},{8,12},{16,8},{20,16},{28,20},{24,28},{5,1},{13,5},{9... | collective-permute-start | bytes 5308424 | tf_op jit(solution)/shard_map/ppermute | solution.py:195
  250.6 31.0 %copy-start.4 = (bf16[1536,1152]{1,0:T(8,128)(2,1)S(1)}, bf16[1536,1152]{1,0:T(8,128)(2,1)}, u32[]{:S(2)}) copy-start(bf16[1536,1152]{1,0:T(8,128)(2,1)} %gather_fusion.9) | copy-start | bytes 10616836
  257.1 56.6 %all-to-all-start.2 = ((bf16[32,48,384]{2,1,0:T(8,128)(2,1)}), bf16[32,48,384]{2,1,0:T(8,128)(2,1)}, u32[]{:S(2)}, u32[]{:S(2)}) async-start(bf16[32,48,384]{2,1,0:T(8,128)(2,1)} %bitcast.12), calls=%async_computation.2 | async-start | bytes 2359296 | tf_op jit(solution)/shard_map/all_to_all | solution.py:199
  282.7 1.7 slice-start.1
  313.7 39.5 %all-to-all-start.4 = ((bf16[32,48,384]{2,1,0:T(8,128)(2,1)}), bf16[32,48,384]{2,1,0:T(8,128)(2,1)S(1)}, u32[]{:S(2)}, u32[]{:S(2)}) async-start(bf16[32,48,384]{2,1,0:T(8,128)(2,1)} %bitcast.7), calls=%async_computation.4 | async-start | bytes 2359296 | tf_op jit(solution)/shard_map/all_to_all | solution.py:199
  353.3 1.0 copy-start.5
  360.1 8.9 %copy-start.1 = (bf16[384,3072]{1,0:T(8,128)(2,1)S(1)}, bf16[384,3072]{1,0:T(8,128)(2,1)}, u32[]{:S(2)}) copy-start(bf16[384,3072]{1,0:T(8,128)(2,1)} %param.10) | copy-start | bytes 7077892

commit v5 on v4

--- a/solution.py
+++ b/solution.py
@@ -124,10 +124,11 @@
     )(*backs)
 
 
-def body(pos_of_owner, query, key, value, raster_to_tile, window_list, valid_count):
+def body(placements, query, key, value, raster_to_tile, window_list, valid_count):
     seq_count = lax.axis_size("seq")
     head_count = lax.axis_size("head")
     seq_pos = lax.axis_index("seq")
+    head_pos = lax.axis_index("head")
     rows_here, width = query.shape
     part_width = width // head_count
     tile_dev, win = window_list.shape
@@ -144,22 +145,31 @@
     chunk_width = chunk_heads * HEAD_DIM
     devices = seq_count * head_count
 
-    owner_at = [0] * seq_count
-    for o, d in enumerate(pos_of_owner):
-        owner_at[d] = o
-    order = jnp.argsort(raster_to_tile)
-    send_order = order.reshape(seq_count, share)[jnp.array(owner_at, jnp.int32)].reshape(rows_here)
+    owner_at = [[0] * seq_count for _ in range(head_count)]
+    for h in range(head_count):
+        for o, d in enumerate(placements[h % len(placements)]):
+            owner_at[h][d] = o
+    pos_of = [placements[h % len(placements)] for h in range(head_count)]
+    send_blocks = [owner_at[h][d] * head_count + h for d in range(seq_count) for h in range(head_count)]
+    back_blocks = [pos_of[h][o] * head_count + h for o in range(seq_count) for h in range(head_count)]
+    send_blocks = jnp.array(send_blocks, jnp.int32)
+    back_blocks = jnp.array(back_blocks, jnp.int32)
+    send_order = jnp.argsort(raster_to_tile)
     slots_sorted = raster_to_tile[send_order].reshape(seq_count, share)
     slot_send = jnp.broadcast_to(slots_sorted[:, None, :], (seq_count, head_count, share))
+    slot_send = slot_send.reshape(devices, share)[send_blocks]
     slot_in = lax.all_to_all(
-        slot_send.reshape(devices, share), ("seq", "head"), split_axis=0, concat_axis=0, tiled=True
+        slot_send, ("seq", "head"), split_axis=0, concat_axis=0, tiled=True
     ).reshape(tok_dev)
-    my_owner = jnp.array(owner_at, jnp.int32)[seq_pos]
+    my_owner = jnp.array(owner_at, jnp.int32)[head_pos, seq_pos]
     local = slot_in - my_owner * tok_dev
     place = jnp.zeros((tok_dev,), jnp.int32).at[local].set(jnp.arange(tok_dev, dtype=jnp.int32))
 
+    both = ("seq", "head")
     window_mine = lax.ppermute(
-        window_list, "seq", [(o, pos_of_owner[o]) for o in range(seq_count)]
+        window_list,
+        both,
+        [(o * head_count + h, pos_of[h][o] * head_count + h) for o in range(seq_count) for h in range(head_count)],
     )
     first_tile = my_owner * tile_dev - reach
     global_tiles = jnp.clip(first_tile + jnp.arange(ext_tiles, dtype=jnp.int32), 0, all_tiles - 1)
@@ -169,8 +179,12 @@
     vcw_flat = vc_ext[local_windows].reshape(tile_dev * win)
     vc_own = vc_ext[reach : reach + tile_dev]
 
-    to_right = [(pos_of_owner[o], pos_of_owner[o + 1]) for o in range(seq_count - 1)]
-    to_left = [(pos_of_owner[o + 1], pos_of_owner[o]) for o in range(seq_count - 1)]
+    to_right = [
+        (pos_of[h][o] * head_count + h, pos_of[h][o + 1] * head_count + h)
+        for o in range(seq_count - 1)
+        for h in range(head_count)
+    ]
+    to_left = [(b, a) for a, b in to_right]
 
     packable = share % 16 == 0
     if packable:
@@ -187,17 +201,17 @@
         else:
             send = jnp.concatenate([x[:, :, :, c, :] for x in rows_sorted], axis=3)
             send = jnp.swapaxes(send, 1, 2).reshape(devices, share, 3 * chunk_width)
-        got = lax.all_to_all(send, ("seq", "head"), split_axis=0, concat_axis=0, tiled=True)
+        got = lax.all_to_all(send[send_blocks], both, split_axis=0, concat_axis=0, tiled=True)
         got_tile = got.reshape(tok_dev, 3 * chunk_width)[place]
         q_tile = got_tile[:, :chunk_width]
         kv_tile = got_tile[:, chunk_width:]
-        from_left = lax.ppermute(kv_tile[tok_dev - rim :], "seq", to_right)
-        from_right = lax.ppermute(kv_tile[:rim], "seq", to_left)
+        from_left = lax.ppermute(kv_tile[tok_dev - rim :], both, to_right)
+        from_right = lax.ppermute(kv_tile[:rim], both, to_left)
         kv_ext = jnp.concatenate([from_left, kv_tile, from_right], axis=0)
         out_tile = attention(q_tile, kv_ext, win_flat, vcw_flat, vc_own, tile, win, chunk_heads)
         outgoing = out_tile[local].reshape(devices, share, chunk_width)
         back = lax.all_to_all(outgoing, ("seq", "head"), split_axis=0, concat_axis=0, tiled=True)
-        arrived.append(back)
+        arrived.append(back[back_blocks])
     if packable:
         sorted_rows = unpack(arrived, seq_count, head_count, share, width)
     else:
@@ -210,7 +224,7 @@
     return sorted_rows[inverse]
 
 
-def snake(mesh):
+def snake(mesh, mirror):
     seq_count = mesh.shape["seq"]
     first = mesh.devices.reshape(seq_count, -1)[:, 0]
     try:
@@ -218,9 +232,12 @@
     except AttributeError:
         spots = [(0, d % 2, d // 2) for d in range(seq_count)]
     low_z = min(c[2] for c in spots)
+    high_y = max(c[1] for c in spots)
 
     def rank(d):
         x, y, z = spots[d][:3]
+        if mirror:
+            y = high_y - y
         return (z, y if (z - low_z) % 2 == 0 else -y, x)
 
     return tuple(sorted(range(seq_count), key=rank))
@@ -236,5 +253,5 @@
         P(),
     )
     return jax.shard_map(
-        functools.partial(body, snake(mesh)), mesh=mesh, in_specs=placed, out_specs=P(("seq", "head"), None), check_vma=False
-    )
+        functools.partial(body, (snake(mesh, False), snake(mesh, True))), mesh=mesh, in_specs=placed, out_specs=P(("seq", "head"), None), check_vma=False
+    )

time: 371 us -> 364 us (0.981)
  local copies, waits for them, and re-layouts: 90.8 us -> 104 us
  starting transfers between devices: 65 us -> 54.3 us
  waiting for transfers between devices: 138 us -> 129 us
    gather x1 -> x5, local copies, waits for them, and re-layouts: 0.55 us -> 15.5 us  [the longest x2 9.39 us: body(): send[send_blocks]]
    all_to_all x2, starting transfers between devices: 34.9 us -> 23.1 us  [body(): lax.all_to_all(outgoing, ('seq', 'head'), split_axis=0, concat_axis=0, ti...]
    all_to_all x3, waiting for transfers between devices: 113 us -> 106 us  [the longest x2 106 us: body(): lax.all_to_all(send[send_blocks], both, split_axis=0, concat_axis=0, tile...]
  transfers between devices with their start and end apart: 10 -> 10, of which waited for: 3 -> 3; matrix products, arithmetic and copies ran while one was open for 23% -> 27% of each run, Pallas kernels for 13% -> 14%
where the time goes in v5:
time: 364 us; the launch traced here: 363 us
  waiting for transfers between devices  129 us (35%)
  local copies, waits for them, and re-layouts  104 us (29%)
  Pallas kernels  55.6 us (15%)
  starting transfers between devices  54.3 us (15%)
  other arithmetic  17.7 us (5%)
    all_to_all x2, waiting for transfers between devices, body(): lax.all_to_all(send[send_blocks], both, split_axis=0, concat_axis=0, tile...  106 us
    pallas_call x2, Pallas kernels, attention(): pl.pallas_call(functools.partial(attn_kernel, win, tile, scale), out_shap...  35.8 us
    all_to_all x2, starting transfers between devices, body(): lax.all_to_all(outgoing, ('seq', 'head'), split_axis=0, concat_axis=0, ti...  23.1 us
    all_to_all x2, waiting for transfers between devices, body(): lax.all_to_all(outgoing, ('seq', 'head'), split_axis=0, concat_axis=0, ti...  22.8 us
    gather x2, local copies, waits for them, and re-layouts, body(): got_tile = got.reshape(tok_dev, 3 * chunk_width)[place]  16.9 us
    gather x3, local copies, waits for them, and re-layouts, body(): rows_flat = [x[send_order] for x in (query, key, value)]  16 us
    pallas_call x2, Pallas kernels, pack(): pl.pallas_call(functools.partial(pack_kernel, head_count, part_width, chu...  13.9 us
    gather x2, local copies, waits for them, and re-layouts, body(): outgoing = out_tile[local].reshape(devices, share, chunk_width)  13 us
  transfers between devices with their start and end apart: 10, of which 3 were waited for; matrix products, arithmetic and copies ran while one was open for 27% of the time, Pallas kernels for 14%

profile of v5, /device:TPU:0, one launch (start us, length us, event | category | flops | bytes accessed | tf_op | source)
XLA Modules:
  0.0 362.6 jit_solution(1397360212883213828)
XLA Ops:
  0.0 4.6 %sort.17 = (s32[384]{0:T(512)}, s32[384]{0:T(512)S(1)}) sort(s32[384]{0:T(512)} %param.12, s32[384]{0:T(512)S(1)} %iota.15), dimensions={0}, to_apply=%region_0.0 | sort | flops 3456 | bytes 6144 | tf_op jit(solution)/shard_map/jit(argsort)/sort | solution.py:157
  4.6 3.6 gather_fusion.6
  10.2 7.3 %all-to-all-start.1 = ((s32[32,1,48]{2,1,0:T(1,128)}), s32[32,1,48]{2,1,0:T(1,128)S(1)}, u32[]{:S(2)}, u32[]{:S(2)}) async-start(s32[32,1,48]{2,1,0:T(1,128)} %bitcast.5), calls=%async_computation.1 | async-start | bytes 32768 | tf_op jit(solution)/shard_map/all_to_all | solution.py:161
  17.5 3.6 gather_fusion.4
  21.1 8.9 %gather_fusion.3 = bf16[384,3072]{1,0:T(8,128)(2,1)} fusion(bf16[384,3072]{1,0:T(8,128)(2,1)} %param.10, s32[1024]{0:T(1024)S(1)} %pad_clamp_fusion.4), kind=kCustom, calls=%fused_computation.3 | custom fusion | bytes 4720128 | tf_op jit(solution)/shard_map/gather | solution.py:191
  30.0 3.6 gather_fusion.2
  33.5 7.0 %shard_map.93 = bf16[32,48,1152]{2,1,0:T(8,128)(2,1)} custom-call(bf16[384,3072]{1,0:T(8,128)(2,1)} %gather_fusion.2, bf16[384,3072]{1,0:T(8,128)(2,1)} %gather_fusion.3, bf16[384,3072]{1,0:T(8,128)(2,1)} %gather_fusion.4), custom_call_target="tpu_custom_call" | custom-call | bytes 7077888 | tf_op jit(solution)/shard_map/pallas_call | solution.py:92
  40.5 4.7 %gather_fusion.11 = bf16[32,48,1152]{2,1,0:T(8,128)(2,1)} fusion(bf16[32,48,1152]{2,1,0:T(8,128)(2,1)} %shard_map.93, s32[1024]{0:T(1024)S(1)} %pad_clamp_fusion.3), kind=kCustom, calls=%fused_computation.11 | custom fusion | bytes 7078016 | tf_op jit(solution)/shard_map/gather | solution.py:204
  45.8 5.9 %all-to-all-start.3 = ((bf16[32,48,1152]{2,1,0:T(8,128)(2,1)}), bf16[32,48,1152]{2,1,0:T(8,128)(2,1)}, u32[]{:S(2)}, u32[]{:S(2)}) async-start(bf16[32,48,1152]{2,1,0:T(8,128)(2,1)} %gather_fusion.11), calls=%async_computation.3 | async-start | bytes 7077888 | tf_op jit(solution)/shard_map/all_to_all | solution.py:204
  51.8 7.0 %shard_map.91 = bf16[32,48,1152]{2,1,0:T(8,128)(2,1)} custom-call(bf16[384,3072]{1,0:T(8,128)(2,1)} %gather_fusion.2, bf16[384,3072]{1,0:T(8,128)(2,1)} %gather_fusion.3, bf16[384,3072]{1,0:T(8,128)(2,1)} %gather_fusion.4), custom_call_target="tpu_custom_call" | custom-call | bytes 7077888 | tf_op jit(solution)/shard_map/pallas_call | solution.py:92
  58.8 4.7 %gather_fusion.5 = bf16[32,48,1152]{2,1,0:T(8,128)(2,1)} fusion(bf16[32,48,1152]{2,1,0:T(8,128)(2,1)} %shard_map.91, s32[1024]{0:T(1024)S(1)} %pad_clamp_fusion.3), kind=kCustom, calls=%fused_computation.5 | custom fusion | bytes 7078016 | tf_op jit(solution)/shard_map/gather | solution.py:204
  63.4 68.1 %all-to-all-done.3 = bf16[32,48,1152]{2,1,0:T(8,128)(2,1)} async-done(((bf16[32,48,1152]{2,1,0:T(8,128)(2,1)}), bf16[32,48,1152]{2,1,0:T(8,128)(2,1)}, u32[]{:S(2)}, u32[]{:S(2)}) %all-to-all-start.3) | async-done | bytes 3538976 | tf_op jit(solution)/shard_map/all_to_all | solution.py:204
  131.5 4.1 %all-to-all-start = ((bf16[32,48,1152]{2,1,0:T(8,128)(2,1)}), bf16[32,48,1152]{2,1,0:T(8,128)(2,1)S(1)}, u32[]{:S(2)}, u32[]{:S(2)}) async-start(bf16[32,48,1152]{2,1,0:T(8,128)(2,1)} %gather_fusion.5), calls=%async_computation | async-start | bytes 7077888 | tf_op jit(solution)/shard_map/all_to_all | solution.py:204
  140.4 6.3 %scatter_custom_fusion = s32[1536]{0:T(1024)S(1)} fusion(s32[1536]{0:T(1024)S(1)} %fusion, s32[1536]{0:T(1024)} %iota.16, s32[]{:T(128)} %constant.17.clone.1), kind=kCustom, calls=%fused_computation.34 | custom fusion | bytes 6656 | tf_op jit(solution)/shard_map/scatter | solution.py:166
  147.3 10.9 %gather_fusion.12 = bf16[1536,1152]{1,0:T(8,128)(2,1)} fusion(bf16[1536,1152]{1,0:T(8,128)(2,1)} %bitcast.8, s32[2048]{0:T(1024)S(1)} %pad_clamp_fusion.1), kind=kCustom, calls=%fused_computation.12 | custom fusion | bytes 7084032 | tf_op jit(solution)/shard_map/gather | solution.py:205
  158.2 4.1 %fusion.6 = (bf16[1152,768]{1,0:T(8,128)(2,1)}, bf16[1152,768]{1,0:T(8,128)(2,1)}) fusion(bf16[1536,1152]{1,0:T(8,128)(2,1)} %gather_fusion.12), kind=kLoop, calls=%fused_computation.41 | loop fusion | bytes 7077888 | tf_op jit(solution)/shard_map/slice | solution.py:208
  162.3 4.9 %collective-permute-start.3 = (bf16[1152,768]{1,0:T(8,128)(2,1)}, bf16[1152,768]{1,0:T(8,128)(2,1)}, u32[]{:S(2)}, u32[]{:S(2)}) collective-permute-start(bf16[1152,768]{1,0:T(8,128)(2,1)} %get-tuple-element.9), channel_id=1, source_target_pairs={{0,4},{5,1},{2,6},{7,3},{4,12},{1,9},{6,14},{3,11},{12,8},{9,13},{... | collective-permute-start | bytes 5308424 | tf_op jit(solution)/shard_map/ppermute | solution.py:208
  177.1 38.4 %all-to-all-done = bf16[32,48,1152]{2,1,0:T(8,128)(2,1)S(1)} async-done(((bf16[32,48,1152]{2,1,0:T(8,128)(2,1)}), bf16[32,48,1152]{2,1,0:T(8,128)(2,1)S(1)}, u32[]{:S(2)}, u32[]{:S(2)}) %all-to-all-start) | async-done | bytes 3538976 | tf_op jit(solution)/shard_map/all_to_all | solution.py:204
  215.5 6.0 %gather_fusion.8 = bf16[1536,1152]{1,0:T(8,128)(2,1)} fusion(bf16[1536,1152]{1,0:T(8,128)(2,1)S(1)} %bitcast.14, s32[2048]{0:T(1024)S(1)} %copy-done.6), kind=kCustom, calls=%fused_computation.8 | custom fusion | bytes 7084032 | tf_op jit(solution)/shard_map/gather | solution.py:205
  221.5 4.2 %fusion.7 = (bf16[1152,768]{1,0:T(8,128)(2,1)}, bf16[1152,768]{1,0:T(8,128)(2,1)}) fusion(bf16[1536,1152]{1,0:T(8,128)(2,1)} %gather_fusion.8), kind=kLoop, calls=%fused_computation.42 | loop fusion | bytes 7077888 | tf_op jit(solution)/shard_map/slice | solution.py:208
  225.7 4.9 %collective-permute-start.1 = (bf16[1152,768]{1,0:T(8,128)(2,1)}, bf16[1152,768]{1,0:T(8,128)(2,1)}, u32[]{:S(2)}, u32[]{:S(2)}) collective-permute-start(bf16[1152,768]{1,0:T(8,128)(2,1)} %get-tuple-element.11), channel_id=1, source_target_pairs={{0,4},{5,1},{2,6},{7,3},{4,12},{1,9},{6,14},{3,11},{12,8},{9,13},{... | collective-permute-start | bytes 5308424 | tf_op jit(solution)/shard_map/ppermute | solution.py:208
  231.9 5.1 %pad_maximum_fusion.1.refs_0_.refs_1_.refs_2_.refs_3_.refs_4_.refs_5_.refs_6_.refs_7_ = bf16[3840,768]{1,0:T(8,128)(2,1)} fusion(bf16[1152,768]{1,0:T(8,128)(2,1)} %collective-permute-done.4, bf16[1536,768]{1,0:T(8,128)(2,1)S(1)} %slice-done, bf16[1152,768]{1,0:T(8,128)(2,1)} %collective-permute-done.3), kind=kLoop, calls=%fused_computation.19 | loop fusion | flops 17694720 | bytes 11796480 | tf_op jit(solution)/shard_map/concatenate | solution.py:210
  237.1 17.9 %shard_map.94 = bf16[1536,384]{1,0:T(8,128)(2,1)} custom-call(s32[16]{0:T(128)} %reshape.72.win_ref, s32[16]{0:T(128)} %gather_fusion.1, s32[4]{0:T(128)} %slice.31.vco_ref, bf16[1536,384]{1,0:T(8,128)(2,1)} %slice.76.q_ref, bf16[3840,768]{1,0:T(8,128)(2,1)} %pad_maximum_fusion.1.refs_0_.refs_1_.refs_2_.refs_3_.refs_4_.refs_5_.refs_6_.refs_7_, ...), custom_call_target="tpu_custom_call" | custom-call | flops 3623878656 | bytes 11796480 | tf_op jit(solution)/shard_map/pallas_call | solution.py:69
  254.9 6.6 %gather_fusion.13 = bf16[1536,384]{1,0:T(8,128)(2,1)} fusion(bf16[1536,384]{1,0:T(8,128)(2,1)} %shard_map.94, s32[2048]{0:T(1024)S(1)} %pad_clamp_fusion), kind=kCustom, calls=%fused_computation.13 | custom fusion | bytes 2365440 | tf_op jit(solution)/shard_map/gather | solution.py:212
  261.5 16.2 %all-to-all-start.4 = ((bf16[32,48,384]{2,1,0:T(8,128)(2,1)}), bf16[32,48,384]{2,1,0:T(8,128)(2,1)}, u32[]{:S(2)}, u32[]{:S(2)}) async-start(bf16[32,48,384]{2,1,0:T(8,128)(2,1)} %bitcast.15), calls=%async_computation.4 | async-start | bytes 2359296 | tf_op jit(solution)/shard_map/all_to_all | solution.py:213
  280.6 5.1 %pad_maximum_fusion.refs_0_.refs_1_.refs_2_.refs_3_.refs_4_.refs_5_.refs_6_.refs_7_ = bf16[3840,768]{1,0:T(8,128)(2,1)} fusion(bf16[1152,768]{1,0:T(8,128)(2,1)} %collective-permute-done.2, bf16[1536,768]{1,0:T(8,128)(2,1)S(1)} %slice-done.1, bf16[1152,768]{1,0:T(8,128)(2,1)} %collective-permute-done.1), kind=kLoop, calls=%fused_computation.18 | loop fusion | flops 17694720 | bytes 11796480 | tf_op jit(solution)/shard_map/concatenate | solution.py:210
  285.7 17.9 %shard_map.92 = bf16[1536,384]{1,0:T(8,128)(2,1)} custom-call(s32[16]{0:T(128)} %reshape.72.win_ref, s32[16]{0:T(128)} %gather_fusion.1, s32[4]{0:T(128)} %slice.31.vco_ref, bf16[1536,384]{1,0:T(8,128)(2,1)} %slice.72.q_ref, bf16[3840,768]{1,0:T(8,128)(2,1)} %pad_maximum_fusion.refs_0_.refs_1_.refs_2_.refs_3_.refs_4_.refs_5_.refs_6_.refs_7_, ...), custom_call_target="tpu_custom_call" | custom-call | flops 3623878656 | bytes 11796480 | tf_op jit(solution)/shard_map/pallas_call | solution.py:69
  303.6 6.5 %gather_fusion.9 = bf16[1536,384]{1,0:T(8,128)(2,1)} fusion(bf16[1536,384]{1,0:T(8,128)(2,1)} %shard_map.92, s32[2048]{0:T(1024)S(1)} %pad_clamp_fusion), kind=kCustom, calls=%fused_computation.9 | custom fusion | bytes 2365440 | tf_op jit(solution)/shard_map/gather | solution.py:212
  310.0 6.9 %all-to-all-start.2 = ((bf16[32,48,384]{2,1,0:T(8,128)(2,1)}), bf16[32,48,384]{2,1,0:T(8,128)(2,1)S(1)}, u32[]{:S(2)}, u32[]{:S(2)}) async-start(bf16[32,48,384]{2,1,0:T(8,128)(2,1)} %bitcast.7), calls=%async_computation.2 | async-start | bytes 2359296 | tf_op jit(solution)/shard_map/all_to_all | solution.py:213
  323.2 22.8 %all-to-all-done.2 = bf16[32,48,384]{2,1,0:T(8,128)(2,1)S(1)} async-done(((bf16[32,48,384]{2,1,0:T(8,128)(2,1)}), bf16[32,48,384]{2,1,0:T(8,128)(2,1)S(1)}, u32[]{:S(2)}, u32[]{:S(2)}) %all-to-all-start.2) | async-done | bytes 1179680 | tf_op jit(solution)/shard_map/all_to_all | solution.py:213
  347.8 5.9 %shard_map.95 = bf16[384,3072]{1,0:T(8,128)(2,1)} custom-call(bf16[32,48,384]{2,1,0:T(8,128)(2,1)} %gather_fusion.10, bf16[32,48,384]{2,1,0:T(8,128)(2,1)} %gather_fusion.14), custom_call_target="tpu_custom_call" | custom-call | bytes 4718592 | tf_op jit(solution)/shard_map/pallas_call | solution.py:115
  353.7 8.9 %gather_fusion.15 = bf16[384,3072]{1,0:T(8,128)(2,1)} fusion(bf16[384,3072]{1,0:T(8,128)(2,1)} %shard_map.95, s32[1024]{0:T(1024)S(1)} %pad_clamp_fusion.2), kind=kCustom, calls=%fused_computation.15 | custom fusion | bytes 4720128 | tf_op jit(solution)/shard_map/gather | solution.py:224
  (68 shorter events, 28.6 us)
Async XLA Ops:
  0.0 17.5 %copy-start = (bf16[384,3072]{1,0:T(8,128)(2,1)S(1)}, bf16[384,3072]{1,0:T(8,128)(2,1)}, u32[]{:S(2)}) copy-start(bf16[384,3072]{1,0:T(8,128)(2,1)} %param.11) | copy-start | bytes 7077892
  4.6 3.7 %copy-start.10 = (s32[384]{0:T(512)}, s32[384]{0:T(512)S(1)}, u32[]{:S(2)}) copy-start(s32[384]{0:T(512)S(1)} %compare_select_fusion.3) | copy-start | bytes 4612
  9.0 49.8 %copy-start.9 = (s32[1024]{0:T(1024)}, s32[1024]{0:T(1024)S(1)}, u32[]{:S(2)}) copy-start(s32[1024]{0:T(1024)S(1)} %pad_clamp_fusion.3) | copy-start | bytes 12292
  10.2 35.1 %all-to-all-start.1 = ((s32[32,1,48]{2,1,0:T(1,128)}), s32[32,1,48]{2,1,0:T(1,128)S(1)}, u32[]{:S(2)}, u32[]{:S(2)}) async-start(s32[32,1,48]{2,1,0:T(1,128)} %bitcast.5), calls=%async_computation.1 | async-start | bytes 32768 | tf_op jit(solution)/shard_map/all_to_all | solution.py:161
  21.1 8.9 %copy-start.3 = (bf16[384,3072]{1,0:T(8,128)(2,1)S(1)}, bf16[384,3072]{1,0:T(8,128)(2,1)}, u32[]{:S(2)}) copy-start(bf16[384,3072]{1,0:T(8,128)(2,1)} %param.9) | copy-start | bytes 7077892
  45.2 0.6 copy-start.7
  45.8 85.7 %all-to-all-start.3 = ((bf16[32,48,1152]{2,1,0:T(8,128)(2,1)}), bf16[32,48,1152]{2,1,0:T(8,128)(2,1)}, u32[]{:S(2)}, u32[]{:S(2)}) async-start(bf16[32,48,1152]{2,1,0:T(8,128)(2,1)} %gather_fusion.11), calls=%async_computation.3 | async-start | bytes 7077888 | tf_op jit(solution)/shard_map/all_to_all | solution.py:204
  131.5 84.0 %all-to-all-start = ((bf16[32,48,1152]{2,1,0:T(8,128)(2,1)}), bf16[32,48,1152]{2,1,0:T(8,128)(2,1)S(1)}, u32[]{:S(2)}, u32[]{:S(2)}) async-start(bf16[32,48,1152]{2,1,0:T(8,128)(2,1)} %gather_fusion.5), calls=%async_computation | async-start | bytes 7077888 | tf_op jit(solution)/shard_map/all_to_all | solution.py:204
  139.7 7.0 %copy-start.8 = (s32[1536]{0:T(1024)}, s32[1536]{0:T(1024)S(1)}, u32[]{:S(2)}) copy-start(s32[1536]{0:T(1024)S(1)} %fusion) | copy-start | bytes 18436
  146.7 0.6 copy-start.5
  158.2 12.5 %copy-start.2 = (s32[32]{0:T(128)S(1)}, s32[32]{0:T(128)}, u32[]{:S(2)}) copy-start(s32[32]{0:T(128)} %param.14) | copy-start | bytes 388
  162.3 69.6 %collective-permute-start.3 = (bf16[1152,768]{1,0:T(8,128)(2,1)}, bf16[1152,768]{1,0:T(8,128)(2,1)}, u32[]{:S(2)}, u32[]{:S(2)}) collective-permute-start(bf16[1152,768]{1,0:T(8,128)(2,1)} %get-tuple-element.9), channel_id=1, source_target_pairs={{0,4},{5,1},{2,6},{7,3},{4,12},{1,9},{6,14},{3,11},{12,8},{9,13},{... | collective-permute-start | bytes 5308424 | tf_op jit(solution)/shard_map/ppermute | solution.py:208
  167.2 64.7 %collective-permute-start.4 = (bf16[1152,768]{1,0:T(8,128)(2,1)}, bf16[1152,768]{1,0:T(8,128)(2,1)}, u32[]{:S(2)}, u32[]{:S(2)}) collective-permute-start(bf16[1152,768]{1,0:T(8,128)(2,1)} %get-tuple-element.10), channel_id=1, source_target_pairs={{4,0},{1,5},{6,2},{3,7},{12,4},{9,1},{14,6},{11,3},{8,12},{13,9},{... | collective-permute-start | bytes 5308424 | tf_op jit(solution)/shard_map/ppermute | solution.py:209
  168.7 3.3 collective-permute-start
  177.1 38.4 %copy-start.6 = (s32[2048]{0:T(1024)S(1)}, s32[2048]{0:T(1024)}, u32[]{:S(2)}) copy-start(s32[2048]{0:T(1024)} %copy-done.5) | copy-start | bytes 24580
  221.5 10.4 %slice-start = ((bf16[1536,1152]{1,0:T(8,128)(2,1)}), bf16[1536,768]{1,0:T(8,128)(2,1)S(1)}, s32[]{:S(2)}) async-start(bf16[1536,1152]{1,0:T(8,128)(2,1)} %gather_fusion.12), calls=%async_computation.5 | async-start | bytes 4718592 | tf_op jit(solution)/shard_map/slice | solution.py:207
  225.7 53.2 %collective-permute-start.1 = (bf16[1152,768]{1,0:T(8,128)(2,1)}, bf16[1152,768]{1,0:T(8,128)(2,1)}, u32[]{:S(2)}, u32[]{:S(2)}) collective-permute-start(bf16[1152,768]{1,0:T(8,128)(2,1)} %get-tuple-element.11), channel_id=1, source_target_pairs={{0,4},{5,1},{2,6},{7,3},{4,12},{1,9},{6,14},{3,11},{12,8},{9,13},{... | collective-permute-start | bytes 5308424 | tf_op jit(solution)/shard_map/ppermute | solution.py:208
  230.6 48.3 %collective-permute-start.2 = (bf16[1152,768]{1,0:T(8,128)(2,1)}, bf16[1152,768]{1,0:T(8,128)(2,1)}, u32[]{:S(2)}, u32[]{:S(2)}) collective-permute-start(bf16[1152,768]{1,0:T(8,128)(2,1)} %get-tuple-element.12), channel_id=1, source_target_pairs={{4,0},{1,5},{6,2},{3,7},{12,4},{9,1},{14,6},{11,3},{8,12},{13,9},{... | collective-permute-start | bytes 5308424 | tf_op jit(solution)/shard_map/ppermute | solution.py:209
  254.9 22.8 %copy-start.4 = (bf16[1536,1152]{1,0:T(8,128)(2,1)S(1)}, bf16[1536,1152]{1,0:T(8,128)(2,1)}, u32[]{:S(2)}) copy-start(bf16[1536,1152]{1,0:T(8,128)(2,1)} %gather_fusion.8) | copy-start | bytes 10616836
  261.5 48.5 %all-to-all-start.4 = ((bf16[32,48,384]{2,1,0:T(8,128)(2,1)}), bf16[32,48,384]{2,1,0:T(8,128)(2,1)}, u32[]{:S(2)}, u32[]{:S(2)}) async-start(bf16[32,48,384]{2,1,0:T(8,128)(2,1)} %bitcast.15), calls=%async_computation.4 | async-start | bytes 2359296 | tf_op jit(solution)/shard_map/all_to_all | solution.py:213
  278.9 1.7 slice-start.1
  310.0 35.9 %all-to-all-start.2 = ((bf16[32,48,384]{2,1,0:T(8,128)(2,1)}), bf16[32,48,384]{2,1,0:T(8,128)(2,1)S(1)}, u32[]{:S(2)}, u32[]{:S(2)}) async-start(bf16[32,48,384]{2,1,0:T(8,128)(2,1)} %bitcast.7), calls=%async_computation.2 | async-start | bytes 2359296 | tf_op jit(solution)/shard_map/all_to_all | solution.py:213
  353.7 8.9 %copy-start.1 = (bf16[384,3072]{1,0:T(8,128)(2,1)S(1)}, bf16[384,3072]{1,0:T(8,128)(2,1)}, u32[]{:S(2)}) copy-start(bf16[384,3072]{1,0:T(8,128)(2,1)} %param.11) | copy-start | bytes 7077892

commit v6 on v5

--- a/solution.py
+++ b/solution.py
@@ -79,49 +79,75 @@
     )(win_flat, vcw_flat, vc_own, q_tile, *([kv_ext] * (2 * win)))
 
 
-def pack_kernel(head_count, part_width, chunk_width, c, q_ref, k_ref, v_ref, o_ref):
+def pack_kernel(head_count, chunk_width, col0, table_ref, *refs):
+    o_ref = refs[-1]
     for h in range(head_count):
-        base = h * part_width + c * chunk_width
-        for t, x_ref in enumerate((q_ref, k_ref, v_ref)):
-            o_ref[h, :, t * chunk_width : (t + 1) * chunk_width] = x_ref[:, base : base + chunk_width]
-
-
-def pack(xs, c, seq_count, head_count, share, chunk_width):
+        for t in range(3):
+            x_ref = refs[t * head_count + h]
+            o_ref[h, :, t * chunk_width : (t + 1) * chunk_width] = x_ref[:, col0 : col0 + chunk_width]
+
+
+def pack(xs, table, col0, seq_count, head_count, share, chunk_width):
     rows_here, width = xs[0].shape
     part_width = width // head_count
+
+    def in_map(h, d, table_ref):
+        return (table_ref[d * head_count + h], h)
+
+    in_specs = [
+        pl.BlockSpec((share, part_width), functools.partial(in_map, h))
+        for t in range(3)
+        for h in range(head_count)
+    ]
     return pl.pallas_call(
-        functools.partial(pack_kernel, head_count, part_width, chunk_width, c),
+        functools.partial(pack_kernel, head_count, chunk_width, col0),
         out_shape=jax.ShapeDtypeStruct((seq_count * head_count, share, 3 * chunk_width), xs[0].dtype),
-        grid=(seq_count,),
-        in_specs=[pl.BlockSpec((share, width), lambda s: (s, 0))] * 3,
-        out_specs=pl.BlockSpec((head_count, share, 3 * chunk_width), lambda s: (s, 0, 0)),
+        grid_spec=pltpu.PrefetchScalarGridSpec(
+            num_scalar_prefetch=1,
+            grid=(seq_count,),
+            in_specs=in_specs,
+            out_specs=pl.BlockSpec((head_count, share, 3 * chunk_width), lambda d, table_ref: (d, 0, 0)),
+        ),
         cost_estimate=pl.CostEstimate(
             flops=0, transcendentals=0, bytes_accessed=2 * 3 * rows_here * head_count * chunk_width * 2
         ),
-    )(*xs)
-
-
-def unpack_kernel(head_count, part_width, chunk_width, *refs):
+    )(table, *[x for x in xs for h in range(head_count)])
+
+
+def unpack_kernel(head_count, part_width, chunk_widths, table_ref, *refs):
     o_ref = refs[-1]
-    for c, b_ref in enumerate(refs[:-1]):
+    col0 = 0
+    for c, chunk_width in enumerate(chunk_widths):
         for h in range(head_count):
-            base = h * part_width + c * chunk_width
-            o_ref[:, base : base + chunk_width] = b_ref[h]
-
-
-def unpack(backs, seq_count, head_count, share, width):
-    devices, _, chunk_width = backs[0].shape
+            base = h * part_width + col0
+            o_ref[:, base : base + chunk_width] = refs[c * head_count + h][0]
+        col0 += chunk_width
+
+
+def unpack(backs, table, seq_count, head_count, share, width):
     part_width = width // head_count
+
+    def in_map(h, o, table_ref):
+        return (table_ref[o * head_count + h], 0, 0)
+
+    in_specs = [
+        pl.BlockSpec((1, share, b.shape[2]), functools.partial(in_map, h))
+        for b in backs
+        for h in range(head_count)
+    ]
     return pl.pallas_call(
-        functools.partial(unpack_kernel, head_count, part_width, chunk_width),
+        functools.partial(unpack_kernel, head_count, part_width, tuple(b.shape[2] for b in backs)),
         out_shape=jax.ShapeDtypeStruct((seq_count * share, width), backs[0].dtype),
-        grid=(seq_count,),
-        in_specs=[pl.BlockSpec((head_count, share, chunk_width), lambda s: (s, 0, 0))] * len(backs),
-        out_specs=pl.BlockSpec((share, width), lambda s: (s, 0)),
+        grid_spec=pltpu.PrefetchScalarGridSpec(
+            num_scalar_prefetch=1,
+            grid=(seq_count,),
+            in_specs=in_specs,
+            out_specs=pl.BlockSpec((share, width), lambda o, table_ref: (o, 0)),
+        ),
         cost_estimate=pl.CostEstimate(
             flops=0, transcendentals=0, bytes_accessed=2 * seq_count * share * width * 2
         ),
-    )(*backs)
+    )(table, *[b for b in backs for h in range(head_count)])
 
 
 def body(placements, query, key, value, raster_to_tile, window_list, valid_count):
@@ -152,6 +178,9 @@
     pos_of = [placements[h % len(placements)] for h in range(head_count)]
     send_blocks = [owner_at[h][d] * head_count + h for d in range(seq_count) for h in range(head_count)]
     back_blocks = [pos_of[h][o] * head_count + h for o in range(seq_count) for h in range(head_count)]
+    owner_rows = jnp.array(
+        [owner_at[h][d] for d in range(seq_count) for h in range(head_count)], jnp.int32
+    )
     send_blocks = jnp.array(send_blocks, jnp.int32)
     back_blocks = jnp.array(back_blocks, jnp.int32)
     send_order = jnp.argsort(raster_to_tile)
@@ -197,11 +226,11 @@
     arrived = []
     for c in range(chunks):
         if packable:
-            send = pack(rows_flat, c, seq_count, head_count, share, chunk_width)
+            send = pack(rows_flat, owner_rows, c * chunk_width, seq_count, head_count, share, chunk_width)
         else:
             send = jnp.concatenate([x[:, :, :, c, :] for x in rows_sorted], axis=3)
-            send = jnp.swapaxes(send, 1, 2).reshape(devices, share, 3 * chunk_width)
-        got = lax.all_to_all(send[send_blocks], both, split_axis=0, concat_axis=0, tiled=True)
+            send = jnp.swapaxes(send, 1, 2).reshape(devices, share, 3 * chunk_width)[send_blocks]
+        got = lax.all_to_all(send, both, split_axis=0, concat_axis=0, tiled=True)
         got_tile = got.reshape(tok_dev, 3 * chunk_width)[place]
         q_tile = got_tile[:, :chunk_width]
         kv_tile = got_tile[:, chunk_width:]
@@ -211,10 +240,11 @@
         out_tile = attention(q_tile, kv_ext, win_flat, vcw_flat, vc_own, tile, win, chunk_heads)
         outgoing = out_tile[local].reshape(devices, share, chunk_width)
         back = lax.all_to_all(outgoing, ("seq", "head"), split_axis=0, concat_axis=0, tiled=True)
-        arrived.append(back[back_blocks])
+        arrived.append(back)
     if packable:
-        sorted_rows = unpack(arrived, seq_count, head_count, share, width)
+        sorted_rows = unpack(arrived, back_blocks, seq_count, head_count, share, width)
     else:
+        arrived = [b[back_blocks] for b in arrived]
         arrived = [b.reshape(seq_count, head_count, share, 1, chunk_width) for b in arrived]
         arrived = jnp.concatenate(arrived, axis=3)
         sorted_rows = jnp.swapaxes(arrived, 1, 2).reshape(rows_here, width)

time: 364 us -> 361 us (level)
  local copies, waits for them, and re-layouts: 104 us -> 90.8 us
  waiting for transfers between devices: 129 us -> 136 us
    gather x4 -> x0, local copies, waits for them, and re-layouts: 14.4 us -> none  [the longest x2 9.39 us: body(): send[send_blocks]]
    all_to_all x2, waiting for transfers between devices: 106 us -> 110 us  [body(): got = lax.all_to_all(send, both, split_axis=0, concat_axis=0, tiled=True)]
  transfers between devices with their start and end apart: 10 -> 10, of which waited for: 3 -> 3; matrix products, arithmetic and copies ran while one was open for 27% -> 24% of each run, Pallas kernels for 14% -> 14%
where the time goes in v6:
time: 361 us; the launch traced here: 358 us
  waiting for transfers between devices  136 us (38%)
  local copies, waits for them, and re-layouts  90.8 us (25%)
  Pallas kernels  57.7 us (16%)
  starting transfers between devices  54.3 us (15%)
  other arithmetic  17.7 us (5%)
    all_to_all x2, waiting for transfers between devices, body(): got = lax.all_to_all(send, both, split_axis=0, concat_axis=0, tiled=True)  110 us
    pallas_call x2, Pallas kernels, attention(): pl.pallas_call(functools.partial(attn_kernel, win, tile, scale), out_shap...  35.8 us
    all_to_all x2, waiting for transfers between devices, body(): lax.all_to_all(outgoing, ('seq', 'head'), split_axis=0, concat_axis=0, ti...  25.9 us
    all_to_all x2, starting transfers between devices, body(): lax.all_to_all(outgoing, ('seq', 'head'), split_axis=0, concat_axis=0, ti...  23.2 us
    gather x2, local copies, waits for them, and re-layouts, body(): got_tile = got.reshape(tok_dev, 3 * chunk_width)[place]  16.9 us
    gather x3, local copies, waits for them, and re-layouts, body(): rows_flat = [x[send_order] for x in (query, key, value)]  16 us
    pallas_call x2, Pallas kernels, pack(): pl.pallas_call(functools.partial(pack_kernel, head_count, chunk_width, co...  15.7 us
    gather x2, local copies, waits for them, and re-layouts, body(): outgoing = out_tile[local].reshape(devices, share, chunk_width)  13 us
  transfers between devices with their start and end apart: 10, of which 3 were waited for; matrix products, arithmetic and copies ran while one was open for 24% of the time, Pallas kernels for 14%

profile of v6, /device:TPU:0, one launch (start us, length us, event | category | flops | bytes accessed | tf_op | source)
XLA Modules:
  0.0 358.4 jit_solution(5941086139871785905)
XLA Ops:
  0.0 4.6 %sort.17 = (s32[384]{0:T(512)}, s32[384]{0:T(512)S(1)}) sort(s32[384]{0:T(512)} %param.13, s32[384]{0:T(512)S(1)} %iota.15), dimensions={0}, to_apply=%region_0.0 | sort | flops 3456 | bytes 6144 | tf_op jit(solution)/shard_map/jit(argsort)/sort | solution.py:186
  4.6 3.6 %gather_fusion.5 = s32[384]{0:T(512)S(1)} fusion(s32[384]{0:T(512)} %param.13, s32[1024]{0:T(1024)S(1)} %pad_clamp_fusion.4), kind=kCustom, calls=%fused_computation.5 | custom fusion | bytes 4608 | tf_op jit(solution)/shard_map/gather | solution.py:187
  10.2 7.3 %all-to-all-start.1 = ((s32[32,1,48]{2,1,0:T(1,128)}), s32[32,1,48]{2,1,0:T(1,128)S(1)}, u32[]{:S(2)}, u32[]{:S(2)}) async-start(s32[32,1,48]{2,1,0:T(1,128)} %bitcast.5), calls=%async_computation.1 | async-start | bytes 32768 | tf_op jit(solution)/shard_map/all_to_all | solution.py:190
  17.5 3.6 gather_fusion.4
  21.1 8.9 %gather_fusion.3 = bf16[384,3072]{1,0:T(8,128)(2,1)} fusion(bf16[384,3072]{1,0:T(8,128)(2,1)} %param.11, s32[1024]{0:T(1024)S(1)} %pad_clamp_fusion.4), kind=kCustom, calls=%fused_computation.3 | custom fusion | bytes 4720128 | tf_op jit(solution)/shard_map/gather | solution.py:220
  30.0 3.6 gather_fusion.2
  33.5 7.8 %shard_map.100 = bf16[32,48,1152]{2,1,0:T(8,128)(2,1)} custom-call(s32[32]{0:T(128)} %constant.46.clone.table_ref, bf16[384,3072]{1,0:T(8,128)(2,1)} %gather_fusion.2, bf16[384,3072]{1,0:T(8,128)(2,1)} %gather_fusion.2, bf16[384,3072]{1,0:T(8,128)(2,1)} %gather_fusion.2, bf16[384,3072]{1,0:T(8,128)(2,1)} %gather_fusion.2, bf16[384,3072]{1,0:T(8,128)(2,1)} %gather_fusion.3, ...), custom_call_target="tpu_custom_call" | custom-call | bytes 7077888 | tf_op jit(solution)/shard_map/pallas_call | solution.py:102
  42.0 5.9 %all-to-all-start = ((bf16[32,48,1152]{2,1,0:T(8,128)(2,1)}), bf16[32,48,1152]{2,1,0:T(8,128)(2,1)}, u32[]{:S(2)}, u32[]{:S(2)}) async-start(bf16[32,48,1152]{2,1,0:T(8,128)(2,1)} %shard_map.100), calls=%async_computation | async-start | bytes 7077888 | tf_op jit(solution)/shard_map/all_to_all | solution.py:233
  47.9 7.8 %shard_map.102 = bf16[32,48,1152]{2,1,0:T(8,128)(2,1)} custom-call(s32[32]{0:T(128)} %constant.46.clone.table_ref, bf16[384,3072]{1,0:T(8,128)(2,1)} %gather_fusion.2, bf16[384,3072]{1,0:T(8,128)(2,1)} %gather_fusion.2, bf16[384,3072]{1,0:T(8,128)(2,1)} %gather_fusion.2, bf16[384,3072]{1,0:T(8,128)(2,1)} %gather_fusion.2, bf16[384,3072]{1,0:T(8,128)(2,1)} %gather_fusion.3, ...), custom_call_target="tpu_custom_call" | custom-call | bytes 7077888 | tf_op jit(solution)/shard_map/pallas_call | solution.py:102
  55.8 71.9 %all-to-all-done = bf16[32,48,1152]{2,1,0:T(8,128)(2,1)} async-done(((bf16[32,48,1152]{2,1,0:T(8,128)(2,1)}), bf16[32,48,1152]{2,1,0:T(8,128)(2,1)}, u32[]{:S(2)}, u32[]{:S(2)}) %all-to-all-start) | async-done | bytes 3538976 | tf_op jit(solution)/shard_map/all_to_all | solution.py:233
  127.7 4.1 %all-to-all-start.3 = ((bf16[32,48,1152]{2,1,0:T(8,128)(2,1)}), bf16[32,48,1152]{2,1,0:T(8,128)(2,1)S(1)}, u32[]{:S(2)}, u32[]{:S(2)}) async-start(bf16[32,48,1152]{2,1,0:T(8,128)(2,1)} %shard_map.102), calls=%async_computation.3 | async-start | bytes 7077888 | tf_op jit(solution)/shard_map/all_to_all | solution.py:233
  136.5 6.3 %scatter_custom_fusion = s32[1536]{0:T(1024)S(1)} fusion(s32[1536]{0:T(1024)S(1)} %fusion, s32[1536]{0:T(1024)} %iota.16, s32[]{:T(128)} %constant.18.clone.1), kind=kCustom, calls=%fused_computation.30 | custom fusion | bytes 6656 | tf_op jit(solution)/shard_map/scatter | solution.py:195
  143.4 10.9 %gather_fusion.7 = bf16[1536,1152]{1,0:T(8,128)(2,1)} fusion(bf16[1536,1152]{1,0:T(8,128)(2,1)} %bitcast.2, s32[2048]{0:T(1024)S(1)} %pad_clamp_fusion.1), kind=kCustom, calls=%fused_computation.7 | custom fusion | bytes 7084032 | tf_op jit(solution)/shard_map/gather | solution.py:234
  154.3 4.2 %fusion.7 = (bf16[1152,768]{1,0:T(8,128)(2,1)}, bf16[1152,768]{1,0:T(8,128)(2,1)}) fusion(bf16[1536,1152]{1,0:T(8,128)(2,1)} %gather_fusion.7), kind=kLoop, calls=%fused_computation.38 | loop fusion | bytes 7077888 | tf_op jit(solution)/shard_map/slice | solution.py:237
  158.5 4.9 %collective-permute-start.1 = (bf16[1152,768]{1,0:T(8,128)(2,1)}, bf16[1152,768]{1,0:T(8,128)(2,1)}, u32[]{:S(2)}, u32[]{:S(2)}) collective-permute-start(bf16[1152,768]{1,0:T(8,128)(2,1)} %get-tuple-element.11), channel_id=1, source_target_pairs={{0,4},{5,1},{2,6},{7,3},{4,12},{1,9},{6,14},{3,11},{12,8},{9,13},{... | collective-permute-start | bytes 5308424 | tf_op jit(solution)/shard_map/ppermute | solution.py:237
  170.6 2.4 slice.64.q_ref
  173.0 38.6 %all-to-all-done.3 = bf16[32,48,1152]{2,1,0:T(8,128)(2,1)S(1)} async-done(((bf16[32,48,1152]{2,1,0:T(8,128)(2,1)}), bf16[32,48,1152]{2,1,0:T(8,128)(2,1)S(1)}, u32[]{:S(2)}, u32[]{:S(2)}) %all-to-all-start.3) | async-done | bytes 3538976 | tf_op jit(solution)/shard_map/all_to_all | solution.py:233
  211.6 6.0 %gather_fusion.9 = bf16[1536,1152]{1,0:T(8,128)(2,1)} fusion(bf16[1536,1152]{1,0:T(8,128)(2,1)S(1)} %bitcast.14, s32[2048]{0:T(1024)S(1)} %copy-done.7), kind=kCustom, calls=%fused_computation.9 | custom fusion | bytes 7084032 | tf_op jit(solution)/shard_map/gather | solution.py:234
  217.7 4.2 %fusion.6 = (bf16[1152,768]{1,0:T(8,128)(2,1)}, bf16[1152,768]{1,0:T(8,128)(2,1)}) fusion(bf16[1536,1152]{1,0:T(8,128)(2,1)} %gather_fusion.9), kind=kLoop, calls=%fused_computation.37 | loop fusion | bytes 7077888 | tf_op jit(solution)/shard_map/slice | solution.py:237
  221.9 4.9 %collective-permute-start.3 = (bf16[1152,768]{1,0:T(8,128)(2,1)}, bf16[1152,768]{1,0:T(8,128)(2,1)}, u32[]{:S(2)}, u32[]{:S(2)}) collective-permute-start(bf16[1152,768]{1,0:T(8,128)(2,1)} %get-tuple-element.9), channel_id=1, source_target_pairs={{0,4},{5,1},{2,6},{7,3},{4,12},{1,9},{6,14},{3,11},{12,8},{9,13},{... | collective-permute-start | bytes 5308424 | tf_op jit(solution)/shard_map/ppermute | solution.py:237
  228.2 5.1 %pad_maximum_fusion.refs_0_.refs_1_.refs_2_.refs_3_.refs_4_.refs_5_.refs_6_.refs_7_ = bf16[3840,768]{1,0:T(8,128)(2,1)} fusion(bf16[1152,768]{1,0:T(8,128)(2,1)} %collective-permute-done.2, bf16[1536,768]{1,0:T(8,128)(2,1)S(1)} %slice-done, bf16[1152,768]{1,0:T(8,128)(2,1)} %collective-permute-done.1), kind=kLoop, calls=%fused_computation.14 | loop fusion | flops 17694720 | bytes 11796480 | tf_op jit(solution)/shard_map/concatenate | solution.py:239
  233.3 17.9 %shard_map.101 = bf16[1536,384]{1,0:T(8,128)(2,1)} custom-call(s32[16]{0:T(128)} %reshape.72.win_ref, s32[16]{0:T(128)} %gather_fusion.1, s32[4]{0:T(128)} %slice.31.vco_ref, bf16[1536,384]{1,0:T(8,128)(2,1)} %slice.64.q_ref, bf16[3840,768]{1,0:T(8,128)(2,1)} %pad_maximum_fusion.refs_0_.refs_1_.refs_2_.refs_3_.refs_4_.refs_5_.refs_6_.refs_7_, ...), custom_call_target="tpu_custom_call" | custom-call | flops 3623878656 | bytes 11796480 | tf_op jit(solution)/shard_map/pallas_call | solution.py:69
  251.2 6.6 %gather_fusion.8 = bf16[1536,384]{1,0:T(8,128)(2,1)} fusion(bf16[1536,384]{1,0:T(8,128)(2,1)} %shard_map.101, s32[2048]{0:T(1024)S(1)} %pad_clamp_fusion), kind=kCustom, calls=%fused_computation.8 | custom fusion | bytes 2365440 | tf_op jit(solution)/shard_map/gather | solution.py:241
  257.8 16.1 %all-to-all-start.2 = ((bf16[32,48,384]{2,1,0:T(8,128)(2,1)}), bf16[32,48,384]{2,1,0:T(8,128)(2,1)}, u32[]{:S(2)}, u32[]{:S(2)}) async-start(bf16[32,48,384]{2,1,0:T(8,128)(2,1)} %bitcast.15), calls=%async_computation.2 | async-start | bytes 2359296 | tf_op jit(solution)/shard_map/all_to_all | solution.py:242
  276.7 5.1 %pad_maximum_fusion.1.refs_0_.refs_1_.refs_2_.refs_3_.refs_4_.refs_5_.refs_6_.refs_7_ = bf16[3840,768]{1,0:T(8,128)(2,1)} fusion(bf16[1152,768]{1,0:T(8,128)(2,1)} %collective-permute-done.4, bf16[1536,768]{1,0:T(8,128)(2,1)S(1)} %slice-done.1, bf16[1152,768]{1,0:T(8,128)(2,1)} %collective-permute-done.3), kind=kLoop, calls=%fused_computation.15 | loop fusion | flops 17694720 | bytes 11796480 | tf_op jit(solution)/shard_map/concatenate | solution.py:239
  281.8 17.9 %shard_map.103 = bf16[1536,384]{1,0:T(8,128)(2,1)} custom-call(s32[16]{0:T(128)} %reshape.72.win_ref, s32[16]{0:T(128)} %gather_fusion.1, s32[4]{0:T(128)} %slice.31.vco_ref, bf16[1536,384]{1,0:T(8,128)(2,1)} %slice.68.q_ref, bf16[3840,768]{1,0:T(8,128)(2,1)} %pad_maximum_fusion.1.refs_0_.refs_1_.refs_2_.refs_3_.refs_4_.refs_5_.refs_6_.refs_7_, ...), custom_call_target="tpu_custom_call" | custom-call | flops 3623878656 | bytes 11796480 | tf_op jit(solution)/shard_map/pallas_call | solution.py:69
  299.7 6.4 %gather_fusion.10 = bf16[1536,384]{1,0:T(8,128)(2,1)} fusion(bf16[1536,384]{1,0:T(8,128)(2,1)} %shard_map.103, s32[2048]{0:T(1024)S(1)} %pad_clamp_fusion), kind=kCustom, calls=%fused_computation.10 | custom fusion | bytes 2365440 | tf_op jit(solution)/shard_map/gather | solution.py:241
  306.1 7.1 %all-to-all-start.4 = ((bf16[32,48,384]{2,1,0:T(8,128)(2,1)}), bf16[32,48,384]{2,1,0:T(8,128)(2,1)S(1)}, u32[]{:S(2)}, u32[]{:S(2)}) async-start(bf16[32,48,384]{2,1,0:T(8,128)(2,1)} %bitcast.9), calls=%async_computation.4 | async-start | bytes 2359296 | tf_op jit(solution)/shard_map/all_to_all | solution.py:242
  313.3 3.0 scatter_custom_fusion.1
  316.3 25.9 %all-to-all-done.4.refs_4_.refs_5_.refs_6_.refs_7_ = bf16[32,48,384]{2,1,0:T(8,128)(2,1)S(1)} async-done(((bf16[32,48,384]{2,1,0:T(8,128)(2,1)}), bf16[32,48,384]{2,1,0:T(8,128)(2,1)S(1)}, u32[]{:S(2)}, u32[]{:S(2)}) %all-to-all-start.4) | async-done | bytes 1179680 | tf_op jit(solution)/shard_map/all_to_all | solution.py:242
  343.3 6.3 %shard_map.104 = bf16[384,3072]{1,0:T(8,128)(2,1)} custom-call(s32[32]{0:T(128)} %constant.47.clone.table_ref, bf16[32,48,384]{2,1,0:T(8,128)(2,1)} %all-to-all-done.2.refs_0_.refs_1_.refs_2_.refs_3_, bf16[32,48,384]{2,1,0:T(8,128)(2,1)} %all-to-all-done.2.refs_0_.refs_1_.refs_2_.refs_3_, ...), custom_call_target="tpu_custom_call" | custom-call | bytes 4718592 | tf_op jit(solution)/shard_map/pallas_call | solution.py:138
  349.5 8.9 %gather_fusion.11 = bf16[384,3072]{1,0:T(8,128)(2,1)} fusion(bf16[384,3072]{1,0:T(8,128)(2,1)} %shard_map.104, s32[1024]{0:T(1024)S(1)} %pad_clamp_fusion.2), kind=kCustom, calls=%fused_computation.11 | custom fusion | bytes 4720128 | tf_op jit(solution)/shard_map/gather | solution.py:254
  (64 shorter events, 18.9 us)
Async XLA Ops:
  0.0 17.5 %copy-start = (bf16[384,3072]{1,0:T(8,128)(2,1)S(1)}, bf16[384,3072]{1,0:T(8,128)(2,1)}, u32[]{:S(2)}) copy-start(bf16[384,3072]{1,0:T(8,128)(2,1)} %param.12) | copy-start | bytes 7077892
  4.6 3.7 %copy-start.10 = (s32[384]{0:T(512)}, s32[384]{0:T(512)S(1)}, u32[]{:S(2)}) copy-start(s32[384]{0:T(512)S(1)} %compare_select_fusion.3) | copy-start | bytes 4612
  10.2 31.2 %all-to-all-start.1 = ((s32[32,1,48]{2,1,0:T(1,128)}), s32[32,1,48]{2,1,0:T(1,128)S(1)}, u32[]{:S(2)}, u32[]{:S(2)}) async-start(s32[32,1,48]{2,1,0:T(1,128)} %bitcast.5), calls=%async_computation.1 | async-start | bytes 32768 | tf_op jit(solution)/shard_map/all_to_all | solution.py:190
  21.1 8.9 %copy-start.3 = (bf16[384,3072]{1,0:T(8,128)(2,1)S(1)}, bf16[384,3072]{1,0:T(8,128)(2,1)}, u32[]{:S(2)}) copy-start(bf16[384,3072]{1,0:T(8,128)(2,1)} %param.10) | copy-start | bytes 7077892
  41.4 0.6 copy-start.8
  42.0 85.7 %all-to-all-start = ((bf16[32,48,1152]{2,1,0:T(8,128)(2,1)}), bf16[32,48,1152]{2,1,0:T(8,128)(2,1)}, u32[]{:S(2)}, u32[]{:S(2)}) async-start(bf16[32,48,1152]{2,1,0:T(8,128)(2,1)} %shard_map.100), calls=%async_computation | async-start | bytes 7077888 | tf_op jit(solution)/shard_map/all_to_all | solution.py:233
  127.7 84.0 %all-to-all-start.3 = ((bf16[32,48,1152]{2,1,0:T(8,128)(2,1)}), bf16[32,48,1152]{2,1,0:T(8,128)(2,1)S(1)}, u32[]{:S(2)}, u32[]{:S(2)}) async-start(bf16[32,48,1152]{2,1,0:T(8,128)(2,1)} %shard_map.102), calls=%async_computation.3 | async-start | bytes 7077888 | tf_op jit(solution)/shard_map/all_to_all | solution.py:233
  135.8 7.0 %copy-start.9 = (s32[1536]{0:T(1024)}, s32[1536]{0:T(1024)S(1)}, u32[]{:S(2)}) copy-start(s32[1536]{0:T(1024)S(1)} %fusion) | copy-start | bytes 18436
  142.8 0.6 copy-start.6
  154.3 12.4 %copy-start.2 = (s32[32]{0:T(128)S(1)}, s32[32]{0:T(128)}, u32[]{:S(2)}) copy-start(s32[32]{0:T(128)} %param.15) | copy-start | bytes 388
  158.5 69.6 %collective-permute-start.1 = (bf16[1152,768]{1,0:T(8,128)(2,1)}, bf16[1152,768]{1,0:T(8,128)(2,1)}, u32[]{:S(2)}, u32[]{:S(2)}) collective-permute-start(bf16[1152,768]{1,0:T(8,128)(2,1)} %get-tuple-element.11), channel_id=1, source_target_pairs={{0,4},{5,1},{2,6},{7,3},{4,12},{1,9},{6,14},{3,11},{12,8},{9,13},{... | collective-permute-start | bytes 5308424 | tf_op jit(solution)/shard_map/ppermute | solution.py:237
  163.4 64.7 %collective-permute-start.2 = (bf16[1152,768]{1,0:T(8,128)(2,1)}, bf16[1152,768]{1,0:T(8,128)(2,1)}, u32[]{:S(2)}, u32[]{:S(2)}) collective-permute-start(bf16[1152,768]{1,0:T(8,128)(2,1)} %get-tuple-element.12), channel_id=1, source_target_pairs={{4,0},{1,5},{6,2},{3,7},{12,4},{9,1},{14,6},{11,3},{8,12},{13,9},{... | collective-permute-start | bytes 5308424 | tf_op jit(solution)/shard_map/ppermute | solution.py:238
  164.7 3.3 collective-permute-start
  173.0 38.6 %copy-start.7 = (s32[2048]{0:T(1024)S(1)}, s32[2048]{0:T(1024)}, u32[]{:S(2)}) copy-start(s32[2048]{0:T(1024)} %copy-done.6) | copy-start | bytes 24580
  217.7 10.5 %slice-start = ((bf16[1536,1152]{1,0:T(8,128)(2,1)}), bf16[1536,768]{1,0:T(8,128)(2,1)S(1)}, s32[]{:S(2)}) async-start(bf16[1536,1152]{1,0:T(8,128)(2,1)} %gather_fusion.7), calls=%async_computation.5 | async-start | bytes 4718592 | tf_op jit(solution)/shard_map/slice | solution.py:236
  221.9 53.1 %collective-permute-start.3 = (bf16[1152,768]{1,0:T(8,128)(2,1)}, bf16[1152,768]{1,0:T(8,128)(2,1)}, u32[]{:S(2)}, u32[]{:S(2)}) collective-permute-start(bf16[1152,768]{1,0:T(8,128)(2,1)} %get-tuple-element.9), channel_id=1, source_target_pairs={{0,4},{5,1},{2,6},{7,3},{4,12},{1,9},{6,14},{3,11},{12,8},{9,13},{... | collective-permute-start | bytes 5308424 | tf_op jit(solution)/shard_map/ppermute | solution.py:237
  226.8 48.2 %collective-permute-start.4 = (bf16[1152,768]{1,0:T(8,128)(2,1)}, bf16[1152,768]{1,0:T(8,128)(2,1)}, u32[]{:S(2)}, u32[]{:S(2)}) collective-permute-start(bf16[1152,768]{1,0:T(8,128)(2,1)} %get-tuple-element.10), channel_id=1, source_target_pairs={{4,0},{1,5},{6,2},{3,7},{12,4},{9,1},{14,6},{11,3},{8,12},{13,9},{... | collective-permute-start | bytes 5308424 | tf_op jit(solution)/shard_map/ppermute | solution.py:238
  251.2 22.7 %copy-start.4 = (bf16[1536,1152]{1,0:T(8,128)(2,1)S(1)}, bf16[1536,1152]{1,0:T(8,128)(2,1)}, u32[]{:S(2)}) copy-start(bf16[1536,1152]{1,0:T(8,128)(2,1)} %gather_fusion.9) | copy-start | bytes 10616836
  257.8 48.4 %all-to-all-start.2 = ((bf16[32,48,384]{2,1,0:T(8,128)(2,1)}), bf16[32,48,384]{2,1,0:T(8,128)(2,1)}, u32[]{:S(2)}, u32[]{:S(2)}) async-start(bf16[32,48,384]{2,1,0:T(8,128)(2,1)} %bitcast.15), calls=%async_computation.2 | async-start | bytes 2359296 | tf_op jit(solution)/shard_map/all_to_all | solution.py:242
  275.0 1.7 slice-start.1
  306.1 36.1 %all-to-all-start.4 = ((bf16[32,48,384]{2,1,0:T(8,128)(2,1)}), bf16[32,48,384]{2,1,0:T(8,128)(2,1)S(1)}, u32[]{:S(2)}, u32[]{:S(2)}) async-start(bf16[32,48,384]{2,1,0:T(8,128)(2,1)} %bitcast.9), calls=%async_computation.4 | async-start | bytes 2359296 | tf_op jit(solution)/shard_map/all_to_all | solution.py:242
  342.3 1.0 copy-start.5
  349.5 8.9 %copy-start.1 = (bf16[384,3072]{1,0:T(8,128)(2,1)S(1)}, bf16[384,3072]{1,0:T(8,128)(2,1)}, u32[]{:S(2)}) copy-start(bf16[384,3072]{1,0:T(8,128)(2,1)} %param.12) | copy-start | bytes 7077892

commit v7 on v6

--- a/solution.py
+++ b/solution.py
@@ -10,36 +10,40 @@
 HEAD_DIM = 128
 
 
-def attn_kernel(win, tile, scale, win_ref, vcw_ref, vco_ref, q_ref, *refs):
+def attn_kernel(win, tile, scale, heads, win_ref, vcw_ref, vco_ref, q_ref, *refs):
     k_refs = refs[:win]
     v_refs = refs[win : 2 * win]
     o_ref = refs[2 * win]
     i = pl.program_id(0)
-    q = q_ref[...]
     col = lax.broadcasted_iota(jnp.int32, (1, tile), 1)
-    scores = []
-    top = None
-    for w in range(win):
-        s = lax.dot_general(
-            q, k_refs[w][...], (((1,), (1,)), ((), ())), preferred_element_type=jnp.float32
-        )
-        s = s * scale
-        s = jnp.where(col < vcw_ref[i * win + w], s, -jnp.inf)
-        scores.append(s)
-        m = jnp.max(s, axis=1, keepdims=True)
-        top = m if top is None else jnp.maximum(top, m)
-    total = None
-    acc = None
-    for w in range(win):
-        p = jnp.exp(scores[w] - top)
-        part = jnp.sum(p, axis=1, keepdims=True)
-        mix = jnp.dot(p.astype(jnp.bfloat16), v_refs[w][...], preferred_element_type=jnp.float32)
-        total = part if total is None else total + part
-        acc = mix if acc is None else acc + mix
-    out = acc / total
     row = lax.broadcasted_iota(jnp.int32, (tile, 1), 0)
-    out = jnp.where(row < vco_ref[i], out, 0.0)
-    o_ref[...] = out.astype(o_ref.dtype)
+    for hh in range(heads):
+        cols = slice(hh * HEAD_DIM, (hh + 1) * HEAD_DIM)
+        q = q_ref[:, cols]
+        scores = []
+        top = None
+        for w in range(win):
+            s = lax.dot_general(
+                q, k_refs[w][:, cols], (((1,), (1,)), ((), ())), preferred_element_type=jnp.float32
+            )
+            s = s * scale
+            s = jnp.where(col < vcw_ref[i * win + w], s, -jnp.inf)
+            scores.append(s)
+            m = jnp.max(s, axis=1, keepdims=True)
+            top = m if top is None else jnp.maximum(top, m)
+        total = None
+        acc = None
+        for w in range(win):
+            p = jnp.exp(scores[w] - top)
+            part = jnp.sum(p, axis=1, keepdims=True)
+            mix = jnp.dot(
+                p.astype(jnp.bfloat16), v_refs[w][:, cols], preferred_element_type=jnp.float32
+            )
+            total = part if total is None else total + part
+            acc = mix if acc is None else acc + mix
+        out = acc / total
+        out = jnp.where(row < vco_ref[i], out, 0.0)
+        o_ref[:, cols] = out.astype(o_ref.dtype)
 
 
 def attention(q_tile, kv_ext, win_flat, vcw_flat, vc_own, tile, win, heads_here):
@@ -47,16 +51,16 @@
     tile_dev = tok_dev // tile
     scale = HEAD_DIM ** (-0.5)
 
-    def q_map(i, j, w_ref, a_ref, b_ref):
-        return (i, j)
-
-    def k_map(w, i, j, w_ref, a_ref, b_ref):
-        return (w_ref[i * win + w], j)
-
-    def v_map(w, i, j, w_ref, a_ref, b_ref):
-        return (w_ref[i * win + w], heads_here + j)
-
-    blk = (tile, HEAD_DIM)
+    def q_map(i, w_ref, a_ref, b_ref):
+        return (i, 0)
+
+    def k_map(w, i, w_ref, a_ref, b_ref):
+        return (w_ref[i * win + w], 0)
+
+    def v_map(w, i, w_ref, a_ref, b_ref):
+        return (w_ref[i * win + w], 1)
+
+    blk = (tile, pw)
     in_specs = [pl.BlockSpec(blk, q_map)]
     in_specs += [pl.BlockSpec(blk, functools.partial(k_map, w)) for w in range(win)]
     in_specs += [pl.BlockSpec(blk, functools.partial(v_map, w)) for w in range(win)]
@@ -67,11 +71,11 @@
         bytes_accessed=steps * (2 * win + 2) * tile * HEAD_DIM * 2,
     )
     return pl.pallas_call(
-        functools.partial(attn_kernel, win, tile, scale),
+        functools.partial(attn_kernel, win, tile, scale, heads_here),
         out_shape=jax.ShapeDtypeStruct((tok_dev, pw), jnp.bfloat16),
         grid_spec=pltpu.PrefetchScalarGridSpec(
             num_scalar_prefetch=3,
-            grid=(tile_dev, heads_here),
+            grid=(tile_dev,),
             in_specs=in_specs,
             out_specs=pl.BlockSpec(blk, q_map),
         ),

time: 361 us -> 360 us (level)
  Pallas kernels: 57.7 us -> 53.1 us
  starting transfers between devices: 54.3 us -> 58.5 us
    pallas_call x2, Pallas kernels: 35.8 us -> 31.2 us  [attention(): pl.pallas_call(functools.partial(attn_kernel, win, tile, scale, heads_her...]
    all_to_all x2, starting transfers between devices: 23.2 us -> 27.4 us  [body(): lax.all_to_all(outgoing, ('seq', 'head'), split_axis=0, concat_axis=0, ti...]
  transfers between devices with their start and end apart: 10 -> 10, of which waited for: 3 -> 4; matrix products, arithmetic and copies ran while one was open for 24% -> 24% of each run, Pallas kernels for 14% -> 13%
where the time goes in v7:
time: 360 us; the launch traced here: 358 us
  waiting for transfers between devices  137 us (38%)
  local copies, waits for them, and re-layouts  90.3 us (25%)
  starting transfers between devices  58.5 us (16%)
  Pallas kernels  53.1 us (15%)
  other arithmetic  17.7 us (5%)
    all_to_all x2, waiting for transfers between devices, body(): got = lax.all_to_all(send, both, split_axis=0, concat_axis=0, tiled=True)  110 us
    pallas_call x2, Pallas kernels, attention(): pl.pallas_call(functools.partial(attn_kernel, win, tile, scale, heads_her...  31.2 us
    all_to_all x2, starting transfers between devices, body(): lax.all_to_all(outgoing, ('seq', 'head'), split_axis=0, concat_axis=0, ti...  27.4 us
    all_to_all x2, waiting for transfers between devices, body(): lax.all_to_all(outgoing, ('seq', 'head'), split_axis=0, concat_axis=0, ti...  25.7 us
    gather x2, local copies, waits for them, and re-layouts, body(): got_tile = got.reshape(tok_dev, 3 * chunk_width)[place]  16.9 us
    gather x3, local copies, waits for them, and re-layouts, body(): rows_flat = [x[send_order] for x in (query, key, value)]  16 us
    pallas_call x2, Pallas kernels, pack(): pl.pallas_call(functools.partial(pack_kernel, head_count, chunk_width, co...  15.7 us
    gather x2, local copies, waits for them, and re-layouts, body(): outgoing = out_tile[local].reshape(devices, share, chunk_width)  13 us
  transfers between devices with their start and end apart: 10, of which 4 were waited for; matrix products, arithmetic and copies ran while one was open for 24% of the time, Pallas kernels for 13%

profile of v7, /device:TPU:0, one launch (start us, length us, event | category | flops | bytes accessed | tf_op | source)
XLA Modules:
  0.0 358.0 jit_solution(17295736871141568948)
XLA Ops:
  0.0 4.6 %sort.17 = (s32[384]{0:T(512)}, s32[384]{0:T(512)S(1)}) sort(s32[384]{0:T(512)} %param.13, s32[384]{0:T(512)S(1)} %iota.15), dimensions={0}, to_apply=%region_0.0 | sort | flops 3456 | bytes 6144 | tf_op jit(solution)/shard_map/jit(argsort)/sort | solution.py:190
  4.6 3.6 %gather_fusion.5 = s32[384]{0:T(512)S(1)} fusion(s32[384]{0:T(512)} %param.13, s32[1024]{0:T(1024)S(1)} %pad_clamp_fusion.4), kind=kCustom, calls=%fused_computation.5 | custom fusion | bytes 4608 | tf_op jit(solution)/shard_map/gather | solution.py:191
  10.2 7.3 %all-to-all-start.1 = ((s32[32,1,48]{2,1,0:T(1,128)}), s32[32,1,48]{2,1,0:T(1,128)S(1)}, u32[]{:S(2)}, u32[]{:S(2)}) async-start(s32[32,1,48]{2,1,0:T(1,128)} %bitcast.5), calls=%async_computation.1 | async-start | bytes 32768 | tf_op jit(solution)/shard_map/all_to_all | solution.py:194
  17.5 3.6 gather_fusion.4
  21.1 8.9 %gather_fusion.3 = bf16[384,3072]{1,0:T(8,128)(2,1)} fusion(bf16[384,3072]{1,0:T(8,128)(2,1)} %param.11, s32[1024]{0:T(1024)S(1)} %pad_clamp_fusion.4), kind=kCustom, calls=%fused_computation.3 | custom fusion | bytes 4720128 | tf_op jit(solution)/shard_map/gather | solution.py:224
  30.0 3.6 gather_fusion.2
  33.5 7.8 %shard_map.100 = bf16[32,48,1152]{2,1,0:T(8,128)(2,1)} custom-call(s32[32]{0:T(128)} %constant.46.clone.table_ref, bf16[384,3072]{1,0:T(8,128)(2,1)} %gather_fusion.2, bf16[384,3072]{1,0:T(8,128)(2,1)} %gather_fusion.2, bf16[384,3072]{1,0:T(8,128)(2,1)} %gather_fusion.2, bf16[384,3072]{1,0:T(8,128)(2,1)} %gather_fusion.2, bf16[384,3072]{1,0:T(8,128)(2,1)} %gather_fusion.3, ...), custom_call_target="tpu_custom_call" | custom-call | bytes 7077888 | tf_op jit(solution)/shard_map/pallas_call | solution.py:106
  42.0 5.9 %all-to-all-start = ((bf16[32,48,1152]{2,1,0:T(8,128)(2,1)}), bf16[32,48,1152]{2,1,0:T(8,128)(2,1)}, u32[]{:S(2)}, u32[]{:S(2)}) async-start(bf16[32,48,1152]{2,1,0:T(8,128)(2,1)} %shard_map.100), calls=%async_computation | async-start | bytes 7077888 | tf_op jit(solution)/shard_map/all_to_all | solution.py:237
  47.9 7.8 %shard_map.102 = bf16[32,48,1152]{2,1,0:T(8,128)(2,1)} custom-call(s32[32]{0:T(128)} %constant.46.clone.table_ref, bf16[384,3072]{1,0:T(8,128)(2,1)} %gather_fusion.2, bf16[384,3072]{1,0:T(8,128)(2,1)} %gather_fusion.2, bf16[384,3072]{1,0:T(8,128)(2,1)} %gather_fusion.2, bf16[384,3072]{1,0:T(8,128)(2,1)} %gather_fusion.2, bf16[384,3072]{1,0:T(8,128)(2,1)} %gather_fusion.3, ...), custom_call_target="tpu_custom_call" | custom-call | bytes 7077888 | tf_op jit(solution)/shard_map/pallas_call | solution.py:106
  55.8 71.9 %all-to-all-done = bf16[32,48,1152]{2,1,0:T(8,128)(2,1)} async-done(((bf16[32,48,1152]{2,1,0:T(8,128)(2,1)}), bf16[32,48,1152]{2,1,0:T(8,128)(2,1)}, u32[]{:S(2)}, u32[]{:S(2)}) %all-to-all-start) | async-done | bytes 3538976 | tf_op jit(solution)/shard_map/all_to_all | solution.py:237
  127.7 4.1 %all-to-all-start.3 = ((bf16[32,48,1152]{2,1,0:T(8,128)(2,1)}), bf16[32,48,1152]{2,1,0:T(8,128)(2,1)S(1)}, u32[]{:S(2)}, u32[]{:S(2)}) async-start(bf16[32,48,1152]{2,1,0:T(8,128)(2,1)} %shard_map.102), calls=%async_computation.3 | async-start | bytes 7077888 | tf_op jit(solution)/shard_map/all_to_all | solution.py:237
  136.5 6.3 %scatter_custom_fusion = s32[1536]{0:T(1024)S(1)} fusion(s32[1536]{0:T(1024)S(1)} %fusion, s32[1536]{0:T(1024)} %iota.16, s32[]{:T(128)} %constant.18.clone.1), kind=kCustom, calls=%fused_computation.30 | custom fusion | bytes 6656 | tf_op jit(solution)/shard_map/scatter | solution.py:199
  143.4 10.9 %gather_fusion.7 = bf16[1536,1152]{1,0:T(8,128)(2,1)} fusion(bf16[1536,1152]{1,0:T(8,128)(2,1)} %bitcast.2, s32[2048]{0:T(1024)S(1)} %pad_clamp_fusion.1), kind=kCustom, calls=%fused_computation.7 | custom fusion | bytes 7084032 | tf_op jit(solution)/shard_map/gather | solution.py:238
  154.3 4.2 %fusion.7 = (bf16[1152,768]{1,0:T(8,128)(2,1)}, bf16[1152,768]{1,0:T(8,128)(2,1)}) fusion(bf16[1536,1152]{1,0:T(8,128)(2,1)} %gather_fusion.7), kind=kLoop, calls=%fused_computation.38 | loop fusion | bytes 7077888 | tf_op jit(solution)/shard_map/slice | solution.py:241
  158.5 4.9 %collective-permute-start.1 = (bf16[1152,768]{1,0:T(8,128)(2,1)}, bf16[1152,768]{1,0:T(8,128)(2,1)}, u32[]{:S(2)}, u32[]{:S(2)}) collective-permute-start(bf16[1152,768]{1,0:T(8,128)(2,1)} %get-tuple-element.11), channel_id=1, source_target_pairs={{0,4},{5,1},{2,6},{7,3},{4,12},{1,9},{6,14},{3,11},{12,8},{9,13},{... | collective-permute-start | bytes 5308424 | tf_op jit(solution)/shard_map/ppermute | solution.py:241
  170.6 2.4 slice.64.q_ref
  173.0 38.6 %all-to-all-done.3 = bf16[32,48,1152]{2,1,0:T(8,128)(2,1)S(1)} async-done(((bf16[32,48,1152]{2,1,0:T(8,128)(2,1)}), bf16[32,48,1152]{2,1,0:T(8,128)(2,1)S(1)}, u32[]{:S(2)}, u32[]{:S(2)}) %all-to-all-start.3) | async-done | bytes 3538976 | tf_op jit(solution)/shard_map/all_to_all | solution.py:237
  211.6 6.0 %gather_fusion.9 = bf16[1536,1152]{1,0:T(8,128)(2,1)} fusion(bf16[1536,1152]{1,0:T(8,128)(2,1)S(1)} %bitcast.14, s32[2048]{0:T(1024)S(1)} %copy-done.7), kind=kCustom, calls=%fused_computation.9 | custom fusion | bytes 7084032 | tf_op jit(solution)/shard_map/gather | solution.py:238
  217.7 4.2 %fusion.6 = (bf16[1152,768]{1,0:T(8,128)(2,1)}, bf16[1152,768]{1,0:T(8,128)(2,1)}) fusion(bf16[1536,1152]{1,0:T(8,128)(2,1)} %gather_fusion.9), kind=kLoop, calls=%fused_computation.37 | loop fusion | bytes 7077888 | tf_op jit(solution)/shard_map/slice | solution.py:241
  221.9 4.9 %collective-permute-start.3 = (bf16[1152,768]{1,0:T(8,128)(2,1)}, bf16[1152,768]{1,0:T(8,128)(2,1)}, u32[]{:S(2)}, u32[]{:S(2)}) collective-permute-start(bf16[1152,768]{1,0:T(8,128)(2,1)} %get-tuple-element.9), channel_id=1, source_target_pairs={{0,4},{5,1},{2,6},{7,3},{4,12},{1,9},{6,14},{3,11},{12,8},{9,13},{... | collective-permute-start | bytes 5308424 | tf_op jit(solution)/shard_map/ppermute | solution.py:241
  228.2 5.1 %pad_maximum_fusion.refs_0_.refs_1_.refs_2_.refs_3_.refs_4_.refs_5_.refs_6_.refs_7_ = bf16[3840,768]{1,0:T(8,128)(2,1)} fusion(bf16[1152,768]{1,0:T(8,128)(2,1)} %collective-permute-done.2, bf16[1536,768]{1,0:T(8,128)(2,1)S(1)} %slice-done, bf16[1152,768]{1,0:T(8,128)(2,1)} %collective-permute-done.1), kind=kLoop, calls=%fused_computation.14 | loop fusion | flops 17694720 | bytes 11796480 | tf_op jit(solution)/shard_map/concatenate | solution.py:243
  233.3 15.6 %shard_map.101 = bf16[1536,384]{1,0:T(8,128)(2,1)} custom-call(s32[16]{0:T(128)} %reshape.72.win_ref, s32[16]{0:T(128)} %gather_fusion.1, s32[4]{0:T(128)} %slice.31.vco_ref, bf16[1536,384]{1,0:T(8,128)(2,1)} %slice.64.q_ref, bf16[3840,768]{1,0:T(8,128)(2,1)} %pad_maximum_fusion.refs_0_.refs_1_.refs_2_.refs_3_.refs_4_.refs_5_.refs_6_.refs_7_, ...), custom_call_target="tpu_custom_call" | custom-call | flops 3623878656 | bytes 11796480 | tf_op jit(solution)/shard_map/pallas_call | solution.py:73
  248.9 6.6 %gather_fusion.8 = bf16[1536,384]{1,0:T(8,128)(2,1)} fusion(bf16[1536,384]{1,0:T(8,128)(2,1)} %shard_map.101, s32[2048]{0:T(1024)S(1)} %pad_clamp_fusion), kind=kCustom, calls=%fused_computation.8 | custom fusion | bytes 2365440 | tf_op jit(solution)/shard_map/gather | solution.py:245
  255.4 16.1 %all-to-all-start.2 = ((bf16[32,48,384]{2,1,0:T(8,128)(2,1)}), bf16[32,48,384]{2,1,0:T(8,128)(2,1)}, u32[]{:S(2)}, u32[]{:S(2)}) async-start(bf16[32,48,384]{2,1,0:T(8,128)(2,1)} %bitcast.15), calls=%async_computation.2 | async-start | bytes 2359296 | tf_op jit(solution)/shard_map/all_to_all | solution.py:246
  274.4 5.1 %pad_maximum_fusion.1.refs_0_.refs_1_.refs_2_.refs_3_.refs_4_.refs_5_.refs_6_.refs_7_ = bf16[3840,768]{1,0:T(8,128)(2,1)} fusion(bf16[1152,768]{1,0:T(8,128)(2,1)} %collective-permute-done.4, bf16[1536,768]{1,0:T(8,128)(2,1)S(1)} %slice-done.1, bf16[1152,768]{1,0:T(8,128)(2,1)} %collective-permute-done.3), kind=kLoop, calls=%fused_computation.15 | loop fusion | flops 17694720 | bytes 11796480 | tf_op jit(solution)/shard_map/concatenate | solution.py:243
  279.5 15.6 %shard_map.103 = bf16[1536,384]{1,0:T(8,128)(2,1)} custom-call(s32[16]{0:T(128)} %reshape.72.win_ref, s32[16]{0:T(128)} %gather_fusion.1, s32[4]{0:T(128)} %slice.31.vco_ref, bf16[1536,384]{1,0:T(8,128)(2,1)} %slice.68.q_ref, bf16[3840,768]{1,0:T(8,128)(2,1)} %pad_maximum_fusion.1.refs_0_.refs_1_.refs_2_.refs_3_.refs_4_.refs_5_.refs_6_.refs_7_, ...), custom_call_target="tpu_custom_call" | custom-call | flops 3623878656 | bytes 11796480 | tf_op jit(solution)/shard_map/pallas_call | solution.py:73
  295.1 6.4 %gather_fusion.10 = bf16[1536,384]{1,0:T(8,128)(2,1)} fusion(bf16[1536,384]{1,0:T(8,128)(2,1)} %shard_map.103, s32[2048]{0:T(1024)S(1)} %pad_clamp_fusion), kind=kCustom, calls=%fused_computation.10 | custom fusion | bytes 2365440 | tf_op jit(solution)/shard_map/gather | solution.py:245
  301.5 11.3 %all-to-all-start.4 = ((bf16[32,48,384]{2,1,0:T(8,128)(2,1)}), bf16[32,48,384]{2,1,0:T(8,128)(2,1)S(1)}, u32[]{:S(2)}, u32[]{:S(2)}) async-start(bf16[32,48,384]{2,1,0:T(8,128)(2,1)} %bitcast.9), calls=%async_computation.4 | async-start | bytes 2359296 | tf_op jit(solution)/shard_map/all_to_all | solution.py:246
  312.8 3.3 scatter_custom_fusion.1
  316.1 25.7 %all-to-all-done.4.refs_4_.refs_5_.refs_6_.refs_7_ = bf16[32,48,384]{2,1,0:T(8,128)(2,1)S(1)} async-done(((bf16[32,48,384]{2,1,0:T(8,128)(2,1)}), bf16[32,48,384]{2,1,0:T(8,128)(2,1)S(1)}, u32[]{:S(2)}, u32[]{:S(2)}) %all-to-all-start.4) | async-done | bytes 1179680 | tf_op jit(solution)/shard_map/all_to_all | solution.py:246
  342.9 6.3 %shard_map.104 = bf16[384,3072]{1,0:T(8,128)(2,1)} custom-call(s32[32]{0:T(128)} %constant.47.clone.table_ref, bf16[32,48,384]{2,1,0:T(8,128)(2,1)} %all-to-all-done.2.refs_0_.refs_1_.refs_2_.refs_3_, bf16[32,48,384]{2,1,0:T(8,128)(2,1)} %all-to-all-done.2.refs_0_.refs_1_.refs_2_.refs_3_, ...), custom_call_target="tpu_custom_call" | custom-call | bytes 4718592 | tf_op jit(solution)/shard_map/pallas_call | solution.py:142
  349.1 8.9 %gather_fusion.11 = bf16[384,3072]{1,0:T(8,128)(2,1)} fusion(bf16[384,3072]{1,0:T(8,128)(2,1)} %shard_map.104, s32[1024]{0:T(1024)S(1)} %pad_clamp_fusion.2), kind=kCustom, calls=%fused_computation.11 | custom fusion | bytes 4720128 | tf_op jit(solution)/shard_map/gather | solution.py:258
  (64 shorter events, 18.9 us)
Async XLA Ops:
  0.0 17.5 %copy-start = (bf16[384,3072]{1,0:T(8,128)(2,1)S(1)}, bf16[384,3072]{1,0:T(8,128)(2,1)}, u32[]{:S(2)}) copy-start(bf16[384,3072]{1,0:T(8,128)(2,1)} %param.12) | copy-start | bytes 7077892
  4.6 3.7 %copy-start.10 = (s32[384]{0:T(512)}, s32[384]{0:T(512)S(1)}, u32[]{:S(2)}) copy-start(s32[384]{0:T(512)S(1)} %compare_select_fusion.3) | copy-start | bytes 4612
  10.2 31.2 %all-to-all-start.1 = ((s32[32,1,48]{2,1,0:T(1,128)}), s32[32,1,48]{2,1,0:T(1,128)S(1)}, u32[]{:S(2)}, u32[]{:S(2)}) async-start(s32[32,1,48]{2,1,0:T(1,128)} %bitcast.5), calls=%async_computation.1 | async-start | bytes 32768 | tf_op jit(solution)/shard_map/all_to_all | solution.py:194
  21.1 8.9 %copy-start.3 = (bf16[384,3072]{1,0:T(8,128)(2,1)S(1)}, bf16[384,3072]{1,0:T(8,128)(2,1)}, u32[]{:S(2)}) copy-start(bf16[384,3072]{1,0:T(8,128)(2,1)} %param.10) | copy-start | bytes 7077892
  41.4 0.6 copy-start.8
  42.0 85.7 %all-to-all-start = ((bf16[32,48,1152]{2,1,0:T(8,128)(2,1)}), bf16[32,48,1152]{2,1,0:T(8,128)(2,1)}, u32[]{:S(2)}, u32[]{:S(2)}) async-start(bf16[32,48,1152]{2,1,0:T(8,128)(2,1)} %shard_map.100), calls=%async_computation | async-start | bytes 7077888 | tf_op jit(solution)/shard_map/all_to_all | solution.py:237
  127.7 84.0 %all-to-all-start.3 = ((bf16[32,48,1152]{2,1,0:T(8,128)(2,1)}), bf16[32,48,1152]{2,1,0:T(8,128)(2,1)S(1)}, u32[]{:S(2)}, u32[]{:S(2)}) async-start(bf16[32,48,1152]{2,1,0:T(8,128)(2,1)} %shard_map.102), calls=%async_computation.3 | async-start | bytes 7077888 | tf_op jit(solution)/shard_map/all_to_all | solution.py:237
  135.8 7.0 %copy-start.9 = (s32[1536]{0:T(1024)}, s32[1536]{0:T(1024)S(1)}, u32[]{:S(2)}) copy-start(s32[1536]{0:T(1024)S(1)} %fusion) | copy-start | bytes 18436
  142.8 0.6 copy-start.6
  154.3 12.4 %copy-start.2 = (s32[32]{0:T(128)S(1)}, s32[32]{0:T(128)}, u32[]{:S(2)}) copy-start(s32[32]{0:T(128)} %param.15) | copy-start | bytes 388
  158.5 69.6 %collective-permute-start.1 = (bf16[1152,768]{1,0:T(8,128)(2,1)}, bf16[1152,768]{1,0:T(8,128)(2,1)}, u32[]{:S(2)}, u32[]{:S(2)}) collective-permute-start(bf16[1152,768]{1,0:T(8,128)(2,1)} %get-tuple-element.11), channel_id=1, source_target_pairs={{0,4},{5,1},{2,6},{7,3},{4,12},{1,9},{6,14},{3,11},{12,8},{9,13},{... | collective-permute-start | bytes 5308424 | tf_op jit(solution)/shard_map/ppermute | solution.py:241
  163.4 64.7 %collective-permute-start.2 = (bf16[1152,768]{1,0:T(8,128)(2,1)}, bf16[1152,768]{1,0:T(8,128)(2,1)}, u32[]{:S(2)}, u32[]{:S(2)}) collective-permute-start(bf16[1152,768]{1,0:T(8,128)(2,1)} %get-tuple-element.12), channel_id=1, source_target_pairs={{4,0},{1,5},{6,2},{3,7},{12,4},{9,1},{14,6},{11,3},{8,12},{13,9},{... | collective-permute-start | bytes 5308424 | tf_op jit(solution)/shard_map/ppermute | solution.py:242
  164.7 3.3 collective-permute-start
  173.0 38.6 %copy-start.7 = (s32[2048]{0:T(1024)S(1)}, s32[2048]{0:T(1024)}, u32[]{:S(2)}) copy-start(s32[2048]{0:T(1024)} %copy-done.6) | copy-start | bytes 24580
  217.7 10.5 %slice-start = ((bf16[1536,1152]{1,0:T(8,128)(2,1)}), bf16[1536,768]{1,0:T(8,128)(2,1)S(1)}, s32[]{:S(2)}) async-start(bf16[1536,1152]{1,0:T(8,128)(2,1)} %gather_fusion.7), calls=%async_computation.5 | async-start | bytes 4718592 | tf_op jit(solution)/shard_map/slice | solution.py:240
  221.9 50.8 %collective-permute-start.3 = (bf16[1152,768]{1,0:T(8,128)(2,1)}, bf16[1152,768]{1,0:T(8,128)(2,1)}, u32[]{:S(2)}, u32[]{:S(2)}) collective-permute-start(bf16[1152,768]{1,0:T(8,128)(2,1)} %get-tuple-element.9), channel_id=1, source_target_pairs={{0,4},{5,1},{2,6},{7,3},{4,12},{1,9},{6,14},{3,11},{12,8},{9,13},{... | collective-permute-start | bytes 5308424 | tf_op jit(solution)/shard_map/ppermute | solution.py:241
  226.8 46.6 %collective-permute-start.4 = (bf16[1152,768]{1,0:T(8,128)(2,1)}, bf16[1152,768]{1,0:T(8,128)(2,1)}, u32[]{:S(2)}, u32[]{:S(2)}) collective-permute-start(bf16[1152,768]{1,0:T(8,128)(2,1)} %get-tuple-element.10), channel_id=1, source_target_pairs={{4,0},{1,5},{6,2},{3,7},{12,4},{9,1},{14,6},{11,3},{8,12},{13,9},{... | collective-permute-start | bytes 5308424 | tf_op jit(solution)/shard_map/ppermute | solution.py:242
  248.9 22.7 %copy-start.4 = (bf16[1536,1152]{1,0:T(8,128)(2,1)S(1)}, bf16[1536,1152]{1,0:T(8,128)(2,1)}, u32[]{:S(2)}) copy-start(bf16[1536,1152]{1,0:T(8,128)(2,1)} %gather_fusion.9) | copy-start | bytes 10616836
  255.4 46.1 %all-to-all-start.2 = ((bf16[32,48,384]{2,1,0:T(8,128)(2,1)}), bf16[32,48,384]{2,1,0:T(8,128)(2,1)}, u32[]{:S(2)}, u32[]{:S(2)}) async-start(bf16[32,48,384]{2,1,0:T(8,128)(2,1)} %bitcast.15), calls=%async_computation.2 | async-start | bytes 2359296 | tf_op jit(solution)/shard_map/all_to_all | solution.py:246
  272.7 1.7 slice-start.1
  301.5 40.3 %all-to-all-start.4 = ((bf16[32,48,384]{2,1,0:T(8,128)(2,1)}), bf16[32,48,384]{2,1,0:T(8,128)(2,1)S(1)}, u32[]{:S(2)}, u32[]{:S(2)}) async-start(bf16[32,48,384]{2,1,0:T(8,128)(2,1)} %bitcast.9), calls=%async_computation.4 | async-start | bytes 2359296 | tf_op jit(solution)/shard_map/all_to_all | solution.py:246
  341.8 1.0 copy-start.5
  349.1 8.9 %copy-start.1 = (bf16[384,3072]{1,0:T(8,128)(2,1)S(1)}, bf16[384,3072]{1,0:T(8,128)(2,1)}, u32[]{:S(2)}) copy-start(bf16[384,3072]{1,0:T(8,128)(2,1)} %param.12) | copy-start | bytes 7077892

commit v8 on v7

--- a/solution.py
+++ b/solution.py
@@ -221,7 +221,8 @@
 
     packable = share % 16 == 0
     if packable:
-        rows_flat = [x[send_order] for x in (query, key, value)]
+        pick = (send_order[:, None] == jnp.arange(rows_here, dtype=jnp.int32)[None, :]).astype(query.dtype)
+        rows_flat = [jnp.dot(pick, x) for x in (query, key, value)]
     else:
         rows_sorted = [
             x[send_order].reshape(seq_count, share, head_count, chunks, chunk_width)
@@ -255,6 +256,8 @@
     inverse = (
         jnp.zeros((rows_here,), jnp.int32).at[send_order].set(jnp.arange(rows_here, dtype=jnp.int32))
     )
+    if packable:
+        return lax.dot_general(pick, sorted_rows, (((0,), (0,)), ((), ())))
     return sorted_rows[inverse]
 
 

time: 360 us -> 353 us (0.981)
  blocking collectives: 0 us -> 37 us
  local copies, waits for them, and re-layouts: 90.3 us -> 61.3 us
  waiting for transfers between devices: 137 us -> 111 us
  matrix products: 0 us -> 13.1 us
  starting transfers between devices: 58.5 us -> 51.6 us
    all_to_all x0 -> x1, blocking collectives: none -> 37 us  [body(): lax.all_to_all(outgoing, ('seq', 'head'), split_axis=0, concat_axis=0, ti...]
    all_to_all x2 -> x1, waiting for transfers between devices: 25.7 us -> 0.01 us  [body(): lax.all_to_all(outgoing, ('seq', 'head'), split_axis=0, concat_axis=0, ti...]
    gather x4 -> x0, local copies, waits for them, and re-layouts: 24.9 us -> none  [the longest x3 16 us: body(): rows_flat = [x[send_order] for x in (query, key, value)]]
    dot_general x0 -> x4, matrix products: none -> 13.1 us  [the longest x3 8.56 us: body(): rows_flat = [jnp.dot(pick, x) for x in (query, key, value)]]
    all_to_all x2 -> x1, starting transfers between devices: 27.4 us -> 19.8 us  [body(): lax.all_to_all(outgoing, ('seq', 'head'), split_axis=0, concat_axis=0, ti...]
    ppermute x2, waiting for transfers between devices: 0.73 us -> 6.49 us  [body(): from_right = lax.ppermute(kv_tile[:rim], both, to_left)]
    all_to_all x2, waiting for transfers between devices: 110 us -> 105 us  [body(): got = lax.all_to_all(send, both, split_axis=0, concat_axis=0, tiled=True)]
  transfers between devices with their start and end apart: 10 -> 9, of which waited for: 4 -> 3; matrix products, arithmetic and copies ran while one was open for 24% -> 23% of each run, Pallas kernels for 13% -> 13%
where the time goes in v8:
time: 353 us; the launch traced here: 350 us
  waiting for transfers between devices  111 us (31%)
  local copies, waits for them, and re-layouts  61.3 us (17%)
  Pallas kernels  53.4 us (15%)
  starting transfers between devices  51.6 us (15%)
  blocking collectives  37 us (10%)
  other arithmetic  21 us (6%)
  matrix products  13.1 us (4%)
    all_to_all x2, waiting for transfers between devices, body(): got = lax.all_to_all(send, both, split_axis=0, concat_axis=0, tiled=True)  105 us
    all_to_all x1, blocking collectives, body(): lax.all_to_all(outgoing, ('seq', 'head'), split_axis=0, concat_axis=0, ti...  37 us
    pallas_call x2, Pallas kernels, attention(): pl.pallas_call(functools.partial(attn_kernel, win, tile, scale, heads_her...  31.3 us
    all_to_all x1, starting transfers between devices, body(): lax.all_to_all(outgoing, ('seq', 'head'), split_axis=0, concat_axis=0, ti...  19.8 us
    gather x2, local copies, waits for them, and re-layouts, body(): got_tile = got.reshape(tok_dev, 3 * chunk_width)[place]  16.9 us
    pallas_call x2, Pallas kernels, pack(): pl.pallas_call(functools.partial(pack_kernel, head_count, chunk_width, co...  15.7 us
    gather x2, local copies, waits for them, and re-layouts, body(): outgoing = out_tile[local].reshape(devices, share, chunk_width)  12.3 us
    concatenate x2, other arithmetic, body(): kv_ext = jnp.concatenate([from_left, kv_tile, from_right], axis=0)  10.3 us
  transfers between devices with their start and end apart: 9, of which 3 were waited for; matrix products, arithmetic and copies ran while one was open for 23% of the time, Pallas kernels for 13%

profile of v8, /device:TPU:0, one launch (start us, length us, event | category | flops | bytes accessed | tf_op | source)
XLA Modules:
  0.0 350.2 jit_solution(6489069939416723734)
XLA Ops:
  0.0 4.6 %sort.17 = (s32[384]{0:T(512)}, s32[384]{0:T(512)S(1)}) sort(s32[384]{0:T(512)} %param.13, s32[384]{0:T(512)S(1)} %iota.15), dimensions={0}, to_apply=%region_0.0 | sort | flops 3456 | bytes 6144 | tf_op jit(solution)/shard_map/jit(argsort)/sort | solution.py:190
  4.6 3.6 %gather_fusion.2 = s32[384]{0:T(512)S(1)} fusion(s32[384]{0:T(512)} %param.13, s32[1024]{0:T(1024)S(1)} %pad_clamp_fusion.3), kind=kCustom, calls=%fused_computation.2 | custom fusion | bytes 4608 | tf_op jit(solution)/shard_map/gather | solution.py:191
  10.1 7.3 %all-to-all-start.1 = ((s32[32,1,48]{2,1,0:T(1,128)}), s32[32,1,48]{2,1,0:T(1,128)S(1)}, u32[]{:S(2)}, u32[]{:S(2)}) async-start(s32[32,1,48]{2,1,0:T(1,128)} %bitcast.5), calls=%async_computation.1 | async-start | bytes 32768 | tf_op jit(solution)/shard_map/all_to_all | solution.py:194
  17.5 2.9 fusion.2.refs_4_.refs_5_.refs_6_.refs_7_
  20.4 2.8 fusion.1.refs_8_.refs_9_.refs_10_.refs_11_
  23.2 2.9 fusion.3.refs_0_.refs_1_.refs_2_.refs_3_
  26.1 7.8 %shard_map.102 = bf16[32,48,1152]{2,1,0:T(8,128)(2,1)} custom-call(s32[32]{0:T(128)} %constant.46.clone.table_ref, bf16[384,3072]{1,0:T(8,128)(2,1)} %fusion.3.refs_0_.refs_1_.refs_2_.refs_3_, bf16[384,3072]{1,0:T(8,128)(2,1)} %fusion.3.refs_0_.refs_1_.refs_2_.refs_3_, bf16[384,3072]{1,0:T(8,128)(2,1)} %fusion.3.refs_0_.refs_1_.refs_2_.refs_3_, ...), custom_call_target="tpu_custom_call" | custom-call | bytes 7077888 | tf_op jit(solution)/shard_map/pallas_call | solution.py:106
  34.5 5.9 %all-to-all-start.3 = ((bf16[32,48,1152]{2,1,0:T(8,128)(2,1)}), bf16[32,48,1152]{2,1,0:T(8,128)(2,1)}, u32[]{:S(2)}, u32[]{:S(2)}) async-start(bf16[32,48,1152]{2,1,0:T(8,128)(2,1)} %shard_map.102), calls=%async_computation.3 | async-start | bytes 7077888 | tf_op jit(solution)/shard_map/all_to_all | solution.py:238
  40.5 7.8 %shard_map.100 = bf16[32,48,1152]{2,1,0:T(8,128)(2,1)} custom-call(s32[32]{0:T(128)} %constant.46.clone.table_ref, bf16[384,3072]{1,0:T(8,128)(2,1)} %fusion.3.refs_0_.refs_1_.refs_2_.refs_3_, bf16[384,3072]{1,0:T(8,128)(2,1)} %fusion.3.refs_0_.refs_1_.refs_2_.refs_3_, bf16[384,3072]{1,0:T(8,128)(2,1)} %fusion.3.refs_0_.refs_1_.refs_2_.refs_3_, ...), custom_call_target="tpu_custom_call" | custom-call | bytes 7077888 | tf_op jit(solution)/shard_map/pallas_call | solution.py:106
  48.3 71.9 %all-to-all-done.3 = bf16[32,48,1152]{2,1,0:T(8,128)(2,1)} async-done(((bf16[32,48,1152]{2,1,0:T(8,128)(2,1)}), bf16[32,48,1152]{2,1,0:T(8,128)(2,1)}, u32[]{:S(2)}, u32[]{:S(2)}) %all-to-all-start.3) | async-done | bytes 3538976 | tf_op jit(solution)/shard_map/all_to_all | solution.py:238
  120.2 4.1 %all-to-all-start = ((bf16[32,48,1152]{2,1,0:T(8,128)(2,1)}), bf16[32,48,1152]{2,1,0:T(8,128)(2,1)S(1)}, u32[]{:S(2)}, u32[]{:S(2)}) async-start(bf16[32,48,1152]{2,1,0:T(8,128)(2,1)} %shard_map.100), calls=%async_computation | async-start | bytes 7077888 | tf_op jit(solution)/shard_map/all_to_all | solution.py:238
  130.3 6.9 %scatter_custom_fusion = s32[1536]{0:T(1024)} fusion(s32[1536]{0:T(1024)S(1)} %fusion.8, s32[1536]{0:T(1024)} %iota.17, s32[]{:T(128)} %constant.18.clone.1), kind=kCustom, calls=%fused_computation.32 | custom fusion | bytes 6656 | tf_op jit(solution)/shard_map/scatter | solution.py:199
  138.5 10.9 %gather_fusion.6 = bf16[1536,1152]{1,0:T(8,128)(2,1)} fusion(bf16[1536,1152]{1,0:T(8,128)(2,1)} %bitcast.8, s32[2048]{0:T(1024)S(1)} %pad_clamp_fusion.1), kind=kCustom, calls=%fused_computation.6 | custom fusion | bytes 7084032 | tf_op jit(solution)/shard_map/gather | solution.py:239
  149.4 4.1 %fusion.12 = (bf16[1152,768]{1,0:T(8,128)(2,1)}, bf16[1152,768]{1,0:T(8,128)(2,1)}) fusion(bf16[1536,1152]{1,0:T(8,128)(2,1)} %gather_fusion.6), kind=kLoop, calls=%fused_computation.37 | loop fusion | bytes 7077888 | tf_op jit(solution)/shard_map/slice | solution.py:242
  153.5 4.9 %collective-permute-start.3 = (bf16[1152,768]{1,0:T(8,128)(2,1)}, bf16[1152,768]{1,0:T(8,128)(2,1)}, u32[]{:S(2)}, u32[]{:S(2)}) collective-permute-start(bf16[1152,768]{1,0:T(8,128)(2,1)} %get-tuple-element.9), channel_id=1, source_target_pairs={{0,4},{5,1},{2,6},{7,3},{4,12},{1,9},{6,14},{3,11},{12,8},{9,13},{... | collective-permute-start | bytes 5308424 | tf_op jit(solution)/shard_map/ppermute | solution.py:242
  159.7 1.9 collective-permute-start
  168.8 2.4 slice.60.q_ref
  171.2 33.0 %all-to-all-done = bf16[32,48,1152]{2,1,0:T(8,128)(2,1)S(1)} async-done(((bf16[32,48,1152]{2,1,0:T(8,128)(2,1)}), bf16[32,48,1152]{2,1,0:T(8,128)(2,1)S(1)}, u32[]{:S(2)}, u32[]{:S(2)}) %all-to-all-start) | async-done | bytes 3538976 | tf_op jit(solution)/shard_map/all_to_all | solution.py:238
  204.2 6.0 %gather_fusion.4 = bf16[1536,1152]{1,0:T(8,128)(2,1)} fusion(bf16[1536,1152]{1,0:T(8,128)(2,1)S(1)} %bitcast.17, s32[2048]{0:T(1024)S(1)} %copy-done.8), kind=kCustom, calls=%fused_computation.4 | custom fusion | bytes 7084032 | tf_op jit(solution)/shard_map/gather | solution.py:239
  210.2 4.2 %fusion.13 = (bf16[1152,768]{1,0:T(8,128)(2,1)}, bf16[1152,768]{1,0:T(8,128)(2,1)}) fusion(bf16[1536,1152]{1,0:T(8,128)(2,1)} %gather_fusion.4), kind=kLoop, calls=%fused_computation.38 | loop fusion | bytes 7077888 | tf_op jit(solution)/shard_map/slice | solution.py:242
  214.4 4.9 %collective-permute-start.1 = (bf16[1152,768]{1,0:T(8,128)(2,1)}, bf16[1152,768]{1,0:T(8,128)(2,1)}, u32[]{:S(2)}, u32[]{:S(2)}) collective-permute-start(bf16[1152,768]{1,0:T(8,128)(2,1)} %get-tuple-element.11), channel_id=1, source_target_pairs={{0,4},{5,1},{2,6},{7,3},{4,12},{1,9},{6,14},{3,11},{12,8},{9,13},{... | collective-permute-start | bytes 5308424 | tf_op jit(solution)/shard_map/ppermute | solution.py:242
  220.8 5.1 %pad_maximum_fusion.1.refs_0_.refs_1_.refs_2_.refs_3_.refs_4_.refs_5_.refs_6_.refs_7_ = bf16[3840,768]{1,0:T(8,128)(2,1)} fusion(bf16[1152,768]{1,0:T(8,128)(2,1)} %collective-permute-done.4, bf16[1536,768]{1,0:T(8,128)(2,1)S(1)} %slice-done, bf16[1152,768]{1,0:T(8,128)(2,1)} %collective-permute-done.3), kind=kLoop, calls=%fused_computation.10 | loop fusion | flops 17694720 | bytes 11796480 | tf_op jit(solution)/shard_map/concatenate | solution.py:244
  226.0 15.7 %shard_map.103 = bf16[1536,384]{1,0:T(8,128)(2,1)} custom-call(s32[16]{0:T(128)} %reshape.73.win_ref, s32[16]{0:T(128)} %gather_fusion.1, s32[4]{0:T(128)} %slice.31.vco_ref, bf16[1536,384]{1,0:T(8,128)(2,1)} %slice.60.q_ref, bf16[3840,768]{1,0:T(8,128)(2,1)} %pad_maximum_fusion.1.refs_0_.refs_1_.refs_2_.refs_3_.refs_4_.refs_5_.refs_6_.refs_7_, ...), custom_call_target="tpu_custom_call" | custom-call | flops 3623878656 | bytes 11796480 | tf_op jit(solution)/shard_map/pallas_call | solution.py:73
  241.7 6.6 %gather_fusion.7 = bf16[1536,384]{1,0:T(8,128)(2,1)} fusion(bf16[1536,384]{1,0:T(8,128)(2,1)} %shard_map.103, s32[2048]{0:T(1024)S(1)} %copy-done.6), kind=kCustom, calls=%fused_computation.7 | custom fusion | bytes 2365440 | tf_op jit(solution)/shard_map/gather | solution.py:246
  248.3 19.8 %all-to-all-start.4 = ((bf16[32,48,384]{2,1,0:T(8,128)(2,1)}), bf16[32,48,384]{2,1,0:T(8,128)(2,1)}, u32[]{:S(2)}, u32[]{:S(2)}) async-start(bf16[32,48,384]{2,1,0:T(8,128)(2,1)} %bitcast.18), calls=%async_computation.4 | async-start | bytes 2359296 | tf_op jit(solution)/shard_map/all_to_all | solution.py:247
  269.3 6.5 %collective-permute-done.2 = bf16[1152,768]{1,0:T(8,128)(2,1)} collective-permute-done((bf16[1152,768]{1,0:T(8,128)(2,1)}, bf16[1152,768]{1,0:T(8,128)(2,1)}, u32[]{:S(2)}, u32[]{:S(2)}) %collective-permute-start.2) | collective-permute-done | bytes 1769504 | tf_op jit(solution)/shard_map/ppermute | solution.py:243
  275.8 5.1 %pad_maximum_fusion.refs_0_.refs_1_.refs_2_.refs_3_.refs_4_.refs_5_.refs_6_.refs_7_ = bf16[3840,768]{1,0:T(8,128)(2,1)} fusion(bf16[1152,768]{1,0:T(8,128)(2,1)} %collective-permute-done.2, bf16[1536,768]{1,0:T(8,128)(2,1)S(1)} %slice-done.1, bf16[1152,768]{1,0:T(8,128)(2,1)} %collective-permute-done.1), kind=kLoop, calls=%fused_computation.9 | loop fusion | flops 17694720 | bytes 11796480 | tf_op jit(solution)/shard_map/concatenate | solution.py:244
  280.9 15.6 %shard_map.101 = bf16[1536,384]{1,0:T(8,128)(2,1)} custom-call(s32[16]{0:T(128)} %reshape.73.win_ref, s32[16]{0:T(128)} %gather_fusion.1, s32[4]{0:T(128)} %slice.31.vco_ref, bf16[1536,384]{1,0:T(8,128)(2,1)} %slice.56.q_ref, bf16[3840,768]{1,0:T(8,128)(2,1)} %pad_maximum_fusion.refs_0_.refs_1_.refs_2_.refs_3_.refs_4_.refs_5_.refs_6_.refs_7_, ...), custom_call_target="tpu_custom_call" | custom-call | flops 3623878656 | bytes 11796480 | tf_op jit(solution)/shard_map/pallas_call | solution.py:73
  296.5 5.8 %gather_fusion.5 = bf16[1536,384]{1,0:T(8,128)(2,1)S(1)} fusion(bf16[1536,384]{1,0:T(8,128)(2,1)} %shard_map.101, s32[2048]{0:T(1024)S(1)} %copy-done.6), kind=kCustom, calls=%fused_computation.5 | custom fusion | bytes 2365440 | tf_op jit(solution)/shard_map/gather | solution.py:246
  302.3 37.0 %all_to_all.29.refs_0_.refs_1_.refs_2_.refs_3_ = bf16[32,48,384]{2,1,0:T(8,128)(2,1)} all-to-all(bf16[32,48,384]{2,1,0:T(8,128)(2,1)S(1)} %bitcast.19), channel_id=1, replica_groups=mesh['seq'=8,'head'=4] {'seq','head'}, dimensions={0} | all-to-all | bytes 2359296 | tf_op jit(solution)/shard_map/all_to_all | solution.py:247
  339.2 6.4 %shard_map.104 = bf16[384,3072]{1,0:T(8,128)(2,1)} custom-call(s32[32]{0:T(128)} %constant.47.clone.table_ref, bf16[32,48,384]{2,1,0:T(8,128)(2,1)} %all_to_all.29.refs_0_.refs_1_.refs_2_.refs_3_, bf16[32,48,384]{2,1,0:T(8,128)(2,1)} %all_to_all.29.refs_0_.refs_1_.refs_2_.refs_3_, bf16[32,48,384]{2,1,0:T(8,128)(2,1)} %all_to_all.29.refs_0_.refs_1_.refs_2_.refs_3_, ...), custom_call_target="tpu_custom_call" | custom-call | bytes 4718592 | tf_op jit(solution)/shard_map/pallas_call | solution.py:142
  345.6 4.6 %fusion = bf16[384,3072]{1,0:T(8,128)(2,1)} fusion(bf16[384,3072]{1,0:T(8,128)(2,1)} %shard_map.104, s32[384]{0:T(512)S(1)} %get-tuple-element.6), kind=kOutput, calls=%fused_computation.12 | convolution fusion | flops 906117120 | bytes 4720128 | tf_op jit(solution)/shard_map/dot_general | solution.py:260
  (59 shorter events, 19.7 us)
Async XLA Ops:
  0.0 17.5 %copy-start = (bf16[384,3072]{1,0:T(8,128)(2,1)S(1)}, bf16[384,3072]{1,0:T(8,128)(2,1)}, u32[]{:S(2)}) copy-start(bf16[384,3072]{1,0:T(8,128)(2,1)} %param.11) | copy-start | bytes 7077892
  10.1 23.8 %all-to-all-start.1 = ((s32[32,1,48]{2,1,0:T(1,128)}), s32[32,1,48]{2,1,0:T(1,128)S(1)}, u32[]{:S(2)}, u32[]{:S(2)}) async-start(s32[32,1,48]{2,1,0:T(1,128)} %bitcast.5), calls=%async_computation.1 | async-start | bytes 32768 | tf_op jit(solution)/shard_map/all_to_all | solution.py:194
  17.5 2.9 copy-start.4
  20.4 2.8 copy-start.5
  33.9 0.6 copy-start.9
  34.5 85.7 %all-to-all-start.3 = ((bf16[32,48,1152]{2,1,0:T(8,128)(2,1)}), bf16[32,48,1152]{2,1,0:T(8,128)(2,1)}, u32[]{:S(2)}, u32[]{:S(2)}) async-start(bf16[32,48,1152]{2,1,0:T(8,128)(2,1)} %shard_map.102), calls=%async_computation.3 | async-start | bytes 7077888 | tf_op jit(solution)/shard_map/all_to_all | solution.py:238
  120.2 84.0 %all-to-all-start = ((bf16[32,48,1152]{2,1,0:T(8,128)(2,1)}), bf16[32,48,1152]{2,1,0:T(8,128)(2,1)S(1)}, u32[]{:S(2)}, u32[]{:S(2)}) async-start(bf16[32,48,1152]{2,1,0:T(8,128)(2,1)} %shard_map.100), calls=%async_computation | async-start | bytes 7077888 | tf_op jit(solution)/shard_map/all_to_all | solution.py:238
  129.7 7.5 %copy-start.10 = (s32[1536]{0:T(1024)}, s32[1536]{0:T(1024)S(1)}, u32[]{:S(2)}) copy-start(s32[1536]{0:T(1024)S(1)} %fusion.8) | copy-start | bytes 18436
  137.9 0.6 copy-start.7
  149.4 12.9 %copy-start.2 = (s32[32]{0:T(128)S(1)}, s32[32]{0:T(128)}, u32[]{:S(2)}) copy-start(s32[32]{0:T(128)} %param.15) | copy-start | bytes 388
  153.5 67.3 %collective-permute-start.3 = (bf16[1152,768]{1,0:T(8,128)(2,1)}, bf16[1152,768]{1,0:T(8,128)(2,1)}, u32[]{:S(2)}, u32[]{:S(2)}) collective-permute-start(bf16[1152,768]{1,0:T(8,128)(2,1)} %get-tuple-element.9), channel_id=1, source_target_pairs={{0,4},{5,1},{2,6},{7,3},{4,12},{1,9},{6,14},{3,11},{12,8},{9,13},{... | collective-permute-start | bytes 5308424 | tf_op jit(solution)/shard_map/ppermute | solution.py:242
  158.4 62.4 %collective-permute-start.4 = (bf16[1152,768]{1,0:T(8,128)(2,1)}, bf16[1152,768]{1,0:T(8,128)(2,1)}, u32[]{:S(2)}, u32[]{:S(2)}) collective-permute-start(bf16[1152,768]{1,0:T(8,128)(2,1)} %get-tuple-element.10), channel_id=1, source_target_pairs={{4,0},{1,5},{6,2},{3,7},{12,4},{9,1},{14,6},{11,3},{8,12},{13,9},{... | collective-permute-start | bytes 5308424 | tf_op jit(solution)/shard_map/ppermute | solution.py:243
  159.7 3.9 %collective-permute-start = (s32[4,4]{1,0:T(4,128)}, s32[4,4]{1,0:T(4,128)}, u32[]{:S(2)}, u32[]{:S(2)}) collective-permute-start(s32[4,4]{1,0:T(4,128)} %param.14), channel_id=1, source_target_pairs={{0,0},{1,5},{2,2},{3,7},{4,4},{5,1},{6,6},{7,3},{8,12},{9,9},{10,1... | collective-permute-start | bytes 200 | tf_op jit(solution)/shard_map/ppermute | solution.py:202
  171.2 33.0 %copy-start.8 = (s32[2048]{0:T(1024)S(1)}, s32[2048]{0:T(1024)}, u32[]{:S(2)}) copy-start(s32[2048]{0:T(1024)} %copy-done.7) | copy-start | bytes 24580
  210.2 10.6 %slice-start = ((bf16[1536,1152]{1,0:T(8,128)(2,1)}), bf16[1536,768]{1,0:T(8,128)(2,1)S(1)}, s32[]{:S(2)}) async-start(bf16[1536,1152]{1,0:T(8,128)(2,1)} %gather_fusion.6), calls=%async_computation.5 | async-start | bytes 4718592 | tf_op jit(solution)/shard_map/slice | solution.py:241
  214.4 54.9 %collective-permute-start.1 = (bf16[1152,768]{1,0:T(8,128)(2,1)}, bf16[1152,768]{1,0:T(8,128)(2,1)}, u32[]{:S(2)}, u32[]{:S(2)}) collective-permute-start(bf16[1152,768]{1,0:T(8,128)(2,1)} %get-tuple-element.11), channel_id=1, source_target_pairs={{0,4},{5,1},{2,6},{7,3},{4,12},{1,9},{6,14},{3,11},{12,8},{9,13},{... | collective-permute-start | bytes 5308424 | tf_op jit(solution)/shard_map/ppermute | solution.py:242
  219.3 56.5 %collective-permute-start.2 = (bf16[1152,768]{1,0:T(8,128)(2,1)}, bf16[1152,768]{1,0:T(8,128)(2,1)}, u32[]{:S(2)}, u32[]{:S(2)}) collective-permute-start(bf16[1152,768]{1,0:T(8,128)(2,1)} %get-tuple-element.12), channel_id=1, source_target_pairs={{4,0},{1,5},{6,2},{3,7},{12,4},{9,1},{14,6},{11,3},{8,12},{13,9},{... | collective-permute-start | bytes 5308424 | tf_op jit(solution)/shard_map/ppermute | solution.py:243
  226.0 15.7 %copy-start.6 = (s32[2048]{0:T(1024)S(1)}, s32[2048]{0:T(1024)}, u32[]{:S(2)}) copy-start(s32[2048]{0:T(1024)} %pad_clamp_fusion) | copy-start | bytes 24580
  241.7 26.4 %copy-start.3 = (bf16[1536,1152]{1,0:T(8,128)(2,1)S(1)}, bf16[1536,1152]{1,0:T(8,128)(2,1)}, u32[]{:S(2)}) copy-start(bf16[1536,1152]{1,0:T(8,128)(2,1)} %gather_fusion.4) | copy-start | bytes 10616836
  248.3 54.0 %all-to-all-start.4 = ((bf16[32,48,384]{2,1,0:T(8,128)(2,1)}), bf16[32,48,384]{2,1,0:T(8,128)(2,1)}, u32[]{:S(2)}, u32[]{:S(2)}) async-start(bf16[32,48,384]{2,1,0:T(8,128)(2,1)} %bitcast.18), calls=%async_computation.4 | async-start | bytes 2359296 | tf_op jit(solution)/shard_map/all_to_all | solution.py:247
  269.3 6.5 %slice-start.1 = ((bf16[1536,1152]{1,0:T(8,128)(2,1)}), bf16[1536,768]{1,0:T(8,128)(2,1)S(1)}, s32[]{:S(2)}) async-start(bf16[1536,1152]{1,0:T(8,128)(2,1)} %gather_fusion.4), calls=%async_computation.6 | async-start | bytes 4718592 | tf_op jit(solution)/shard_map/slice | solution.py:241
  339.2 11.0 %copy-start.1 = (bf16[384,3072]{1,0:T(8,128)(2,1)S(1)}, bf16[384,3072]{1,0:T(8,128)(2,1)}, u32[]{:S(2)}) copy-start(bf16[384,3072]{1,0:T(8,128)(2,1)} %param.11) | copy-start | bytes 7077892

commit v9 on v8

--- a/solution.py
+++ b/solution.py
@@ -197,6 +197,7 @@
     my_owner = jnp.array(owner_at, jnp.int32)[head_pos, seq_pos]
     local = slot_in - my_owner * tok_dev
     place = jnp.zeros((tok_dev,), jnp.int32).at[local].set(jnp.arange(tok_dev, dtype=jnp.int32))
+    route = (local[:, None] == jnp.arange(tok_dev, dtype=jnp.int32)[None, :]).astype(query.dtype)
 
     both = ("seq", "head")
     window_mine = lax.ppermute(
@@ -243,7 +244,10 @@
         from_right = lax.ppermute(kv_tile[:rim], both, to_left)
         kv_ext = jnp.concatenate([from_left, kv_tile, from_right], axis=0)
         out_tile = attention(q_tile, kv_ext, win_flat, vcw_flat, vc_own, tile, win, chunk_heads)
-        outgoing = out_tile[local].reshape(devices, share, chunk_width)
+        if packable:
+            outgoing = jnp.dot(route, out_tile).reshape(devices, share, chunk_width)
+        else:
+            outgoing = out_tile[local].reshape(devices, share, chunk_width)
         back = lax.all_to_all(outgoing, ("seq", "head"), split_axis=0, concat_axis=0, tiled=True)
         arrived.append(back)
     if packable:

time: 353 us -> 351 us (level)
  local copies, waits for them, and re-layouts: 61.3 us -> 49.6 us
  matrix products: 13.1 us -> 22.2 us
    gather x2 -> x0, local copies, waits for them, and re-layouts: 12.3 us -> none  [body(): outgoing = out_tile[local].reshape(devices, share, chunk_width)]
    dot_general x0 -> x2, matrix products: none -> 9.07 us  [body(): outgoing = jnp.dot(route, out_tile).reshape(devices, share, chunk_width)]
  transfers between devices with their start and end apart: 9 -> 9, of which waited for: 3 -> 3; matrix products, arithmetic and copies ran while one was open for 23% -> 22% of each run, Pallas kernels for 13% -> 13%
where the time goes in v9:
time: 351 us; the launch traced here: 349 us
  waiting for transfers between devices  113 us (32%)
  Pallas kernels  53.4 us (15%)
  starting transfers between devices  51.9 us (15%)
  local copies, waits for them, and re-layouts  49.6 us (14%)
  blocking collectives  37.7 us (11%)
  matrix products  22.2 us (6%)
  other arithmetic  20.1 us (6%)
    all_to_all x2, waiting for transfers between devices, body(): got = lax.all_to_all(send, both, split_axis=0, concat_axis=0, tiled=True)  105 us
    all_to_all x1, blocking collectives, body(): lax.all_to_all(outgoing, ('seq', 'head'), split_axis=0, concat_axis=0, ti...  37.7 us
    pallas_call x2, Pallas kernels, attention(): pl.pallas_call(functools.partial(attn_kernel, win, tile, scale, heads_her...  31.3 us
    all_to_all x1, starting transfers between devices, body(): lax.all_to_all(outgoing, ('seq', 'head'), split_axis=0, concat_axis=0, ti...  20.1 us
    gather x2, local copies, waits for them, and re-layouts, body(): got_tile = got.reshape(tok_dev, 3 * chunk_width)[place]  16.9 us
    pallas_call x2, Pallas kernels, pack(): pl.pallas_call(functools.partial(pack_kernel, head_count, chunk_width, co...  15.7 us
    concatenate x2, other arithmetic, body(): kv_ext = jnp.concatenate([from_left, kv_tile, from_right], axis=0)  10.3 us
    all_to_all x2, starting transfers between devices, body(): got = lax.all_to_all(send, both, split_axis=0, concat_axis=0, tiled=True)  10 us
  transfers between devices with their start and end apart: 9, of which 3 were waited for; matrix products, arithmetic and copies ran while one was open for 22% of the time, Pallas kernels for 13%

profile of v9, /device:TPU:0, one launch (start us, length us, event | category | flops | bytes accessed | tf_op | source)
XLA Modules:
  0.0 349.0 jit_solution(6183795707675018025)
XLA Ops:
  0.0 4.6 %sort.17 = (s32[384]{0:T(512)}, s32[384]{0:T(512)S(1)}) sort(s32[384]{0:T(512)} %param.13, s32[384]{0:T(512)S(1)} %iota.19), dimensions={0}, to_apply=%region_0.0 | sort | flops 3456 | bytes 6144 | tf_op jit(solution)/shard_map/jit(argsort)/sort | solution.py:190
  4.6 3.6 %gather_fusion = s32[384]{0:T(512)S(1)} fusion(s32[384]{0:T(512)} %param.13, s32[1024]{0:T(1024)S(1)} %pad_clamp_fusion.4), kind=kCustom, calls=%fused_computation | custom fusion | bytes 4608 | tf_op jit(solution)/shard_map/gather | solution.py:191
  10.1 7.3 %all-to-all-start = ((s32[32,1,48]{2,1,0:T(1,128)}), s32[32,1,48]{2,1,0:T(1,128)S(1)}, u32[]{:S(2)}, u32[]{:S(2)}) async-start(s32[32,1,48]{2,1,0:T(1,128)} %bitcast.2), calls=%async_computation | async-start | bytes 32768 | tf_op jit(solution)/shard_map/all_to_all | solution.py:194
  17.5 2.9 fusion.6.refs_4_.refs_5_.refs_6_.refs_7_
  20.4 2.8 fusion.5.refs_8_.refs_9_.refs_10_.refs_11_
  23.2 2.9 fusion.7.refs_0_.refs_1_.refs_2_.refs_3_
  26.1 7.8 %shard_map.102 = bf16[32,48,1152]{2,1,0:T(8,128)(2,1)} custom-call(s32[32]{0:T(128)} %constant.46.clone.table_ref, bf16[384,3072]{1,0:T(8,128)(2,1)} %fusion.7.refs_0_.refs_1_.refs_2_.refs_3_, bf16[384,3072]{1,0:T(8,128)(2,1)} %fusion.7.refs_0_.refs_1_.refs_2_.refs_3_, bf16[384,3072]{1,0:T(8,128)(2,1)} %fusion.7.refs_0_.refs_1_.refs_2_.refs_3_, ...), custom_call_target="tpu_custom_call" | custom-call | bytes 7077888 | tf_op jit(solution)/shard_map/pallas_call | solution.py:106
  34.5 5.9 %all-to-all-start.3 = ((bf16[32,48,1152]{2,1,0:T(8,128)(2,1)}), bf16[32,48,1152]{2,1,0:T(8,128)(2,1)}, u32[]{:S(2)}, u32[]{:S(2)}) async-start(bf16[32,48,1152]{2,1,0:T(8,128)(2,1)} %shard_map.102), calls=%async_computation.3 | async-start | bytes 7077888 | tf_op jit(solution)/shard_map/all_to_all | solution.py:239
  40.5 7.8 %shard_map.100 = bf16[32,48,1152]{2,1,0:T(8,128)(2,1)} custom-call(s32[32]{0:T(128)} %constant.46.clone.table_ref, bf16[384,3072]{1,0:T(8,128)(2,1)} %fusion.7.refs_0_.refs_1_.refs_2_.refs_3_, bf16[384,3072]{1,0:T(8,128)(2,1)} %fusion.7.refs_0_.refs_1_.refs_2_.refs_3_, bf16[384,3072]{1,0:T(8,128)(2,1)} %fusion.7.refs_0_.refs_1_.refs_2_.refs_3_, ...), custom_call_target="tpu_custom_call" | custom-call | bytes 7077888 | tf_op jit(solution)/shard_map/pallas_call | solution.py:106
  48.3 71.9 %all-to-all-done.3 = bf16[32,48,1152]{2,1,0:T(8,128)(2,1)} async-done(((bf16[32,48,1152]{2,1,0:T(8,128)(2,1)}), bf16[32,48,1152]{2,1,0:T(8,128)(2,1)}, u32[]{:S(2)}, u32[]{:S(2)}) %all-to-all-start.3) | async-done | bytes 3538976 | tf_op jit(solution)/shard_map/all_to_all | solution.py:239
  120.2 4.1 %all-to-all-start.1 = ((bf16[32,48,1152]{2,1,0:T(8,128)(2,1)}), bf16[32,48,1152]{2,1,0:T(8,128)(2,1)S(1)}, u32[]{:S(2)}, u32[]{:S(2)}) async-start(bf16[32,48,1152]{2,1,0:T(8,128)(2,1)} %shard_map.100), calls=%async_computation.1 | async-start | bytes 7077888 | tf_op jit(solution)/shard_map/all_to_all | solution.py:239
  126.7 2.5 fusion.16
  131.2 6.3 %scatter_custom_fusion = s32[1536]{0:T(1024)S(1)} fusion(s32[1536]{0:T(1024)} %fusion.12, s32[1536]{0:T(1024)} %iota.21, s32[]{:T(128)} %constant.17.clone.1), kind=kCustom, calls=%fused_computation.34 | custom fusion | bytes 6656 | tf_op jit(solution)/shard_map/scatter | solution.py:199
  138.2 10.9 %gather_fusion.5 = bf16[1536,1152]{1,0:T(8,128)(2,1)} fusion(bf16[1536,1152]{1,0:T(8,128)(2,1)} %bitcast.8, s32[2048]{0:T(1024)S(1)} %pad_clamp_fusion), kind=kCustom, calls=%fused_computation.5 | custom fusion | bytes 7084032 | tf_op jit(solution)/shard_map/gather | solution.py:240
  149.1 4.1 %fusion.17 = (bf16[1152,768]{1,0:T(8,128)(2,1)}, bf16[1152,768]{1,0:T(8,128)(2,1)}) fusion(bf16[1536,1152]{1,0:T(8,128)(2,1)} %gather_fusion.5), kind=kLoop, calls=%fused_computation.40 | loop fusion | bytes 7077888 | tf_op jit(solution)/shard_map/slice | solution.py:243
  153.2 4.9 %collective-permute-start.3 = (bf16[1152,768]{1,0:T(8,128)(2,1)}, bf16[1152,768]{1,0:T(8,128)(2,1)}, u32[]{:S(2)}, u32[]{:S(2)}) collective-permute-start(bf16[1152,768]{1,0:T(8,128)(2,1)} %get-tuple-element.11), channel_id=1, source_target_pairs={{0,4},{5,1},{2,6},{7,3},{4,12},{1,9},{6,14},{3,11},{12,8},{9,13},{... | collective-permute-start | bytes 5308424 | tf_op jit(solution)/shard_map/ppermute | solution.py:243
  168.5 2.4 slice.56.q_ref
  170.9 33.2 %all-to-all-done.1 = bf16[32,48,1152]{2,1,0:T(8,128)(2,1)S(1)} async-done(((bf16[32,48,1152]{2,1,0:T(8,128)(2,1)}), bf16[32,48,1152]{2,1,0:T(8,128)(2,1)S(1)}, u32[]{:S(2)}, u32[]{:S(2)}) %all-to-all-start.1) | async-done | bytes 3538976 | tf_op jit(solution)/shard_map/all_to_all | solution.py:239
  204.2 6.0 %gather_fusion.4 = bf16[1536,1152]{1,0:T(8,128)(2,1)} fusion(bf16[1536,1152]{1,0:T(8,128)(2,1)S(1)} %bitcast.20, s32[2048]{0:T(1024)S(1)} %copy-done.7), kind=kCustom, calls=%fused_computation.4 | custom fusion | bytes 7084032 | tf_op jit(solution)/shard_map/gather | solution.py:240
  210.2 4.2 %fusion.18 = (bf16[1152,768]{1,0:T(8,128)(2,1)}, bf16[1152,768]{1,0:T(8,128)(2,1)}) fusion(bf16[1536,1152]{1,0:T(8,128)(2,1)} %gather_fusion.4), kind=kLoop, calls=%fused_computation.41 | loop fusion | bytes 7077888 | tf_op jit(solution)/shard_map/slice | solution.py:243
  214.4 4.9 %collective-permute-start.1 = (bf16[1152,768]{1,0:T(8,128)(2,1)}, bf16[1152,768]{1,0:T(8,128)(2,1)}, u32[]{:S(2)}, u32[]{:S(2)}) collective-permute-start(bf16[1152,768]{1,0:T(8,128)(2,1)} %get-tuple-element.13), channel_id=1, source_target_pairs={{0,4},{5,1},{2,6},{7,3},{4,12},{1,9},{6,14},{3,11},{12,8},{9,13},{... | collective-permute-start | bytes 5308424 | tf_op jit(solution)/shard_map/ppermute | solution.py:243
  220.8 5.1 %pad_maximum_fusion.1.refs_0_.refs_1_.refs_2_.refs_3_.refs_4_.refs_5_.refs_6_.refs_7_ = bf16[3840,768]{1,0:T(8,128)(2,1)} fusion(bf16[1152,768]{1,0:T(8,128)(2,1)} %collective-permute-done.4, bf16[1536,768]{1,0:T(8,128)(2,1)S(1)} %slice-done, bf16[1152,768]{1,0:T(8,128)(2,1)} %collective-permute-done.3), kind=kLoop, calls=%fused_computation.11 | loop fusion | flops 17694720 | bytes 11796480 | tf_op jit(solution)/shard_map/concatenate | solution.py:245
  226.0 15.7 %shard_map.103 = bf16[1536,384]{1,0:T(8,128)(2,1)} custom-call(s32[16]{0:T(128)} %reshape.80.win_ref, s32[16]{0:T(128)} %gather_fusion.3, s32[4]{0:T(128)} %slice.31.vco_ref, bf16[1536,384]{1,0:T(8,128)(2,1)} %slice.56.q_ref, bf16[3840,768]{1,0:T(8,128)(2,1)} %pad_maximum_fusion.1.refs_0_.refs_1_.refs_2_.refs_3_.refs_4_.refs_5_.refs_6_.refs_7_, ...), custom_call_target="tpu_custom_call" | custom-call | flops 3623878656 | bytes 11796480 | tf_op jit(solution)/shard_map/pallas_call | solution.py:73
  241.7 5.1 %fusion = bf16[1536,384]{1,0:T(8,128)(2,1)} fusion(bf16[1536,384]{1,0:T(8,128)(2,1)} %shard_map.103, s32[1536]{0:T(1024)S(1)} %copy-done.9), kind=kOutput, calls=%fused_computation.8 | convolution fusion | flops 1814298624 | bytes 2365440 | tf_op jit(solution)/shard_map/dot_general | solution.py:248
  246.8 20.1 %all-to-all-start.4 = ((bf16[32,48,384]{2,1,0:T(8,128)(2,1)}), bf16[32,48,384]{2,1,0:T(8,128)(2,1)}, u32[]{:S(2)}, u32[]{:S(2)}) async-start(bf16[32,48,384]{2,1,0:T(8,128)(2,1)} %bitcast.22), calls=%async_computation.4 | async-start | bytes 2359296 | tf_op jit(solution)/shard_map/all_to_all | solution.py:251
  268.2 7.5 %collective-permute-done.2 = bf16[1152,768]{1,0:T(8,128)(2,1)} collective-permute-done((bf16[1152,768]{1,0:T(8,128)(2,1)}, bf16[1152,768]{1,0:T(8,128)(2,1)}, u32[]{:S(2)}, u32[]{:S(2)}) %collective-permute-start.2) | collective-permute-done | bytes 1769504 | tf_op jit(solution)/shard_map/ppermute | solution.py:244
  275.7 5.1 %pad_maximum_fusion.refs_0_.refs_1_.refs_2_.refs_3_.refs_4_.refs_5_.refs_6_.refs_7_ = bf16[3840,768]{1,0:T(8,128)(2,1)} fusion(bf16[1152,768]{1,0:T(8,128)(2,1)} %collective-permute-done.2, bf16[1536,768]{1,0:T(8,128)(2,1)S(1)} %slice-done.1, bf16[1152,768]{1,0:T(8,128)(2,1)} %collective-permute-done.1), kind=kLoop, calls=%fused_computation.10 | loop fusion | flops 17694720 | bytes 11796480 | tf_op jit(solution)/shard_map/concatenate | solution.py:245
  280.8 15.6 %shard_map.101 = bf16[1536,384]{1,0:T(8,128)(2,1)} custom-call(s32[16]{0:T(128)} %reshape.80.win_ref, s32[16]{0:T(128)} %gather_fusion.3, s32[4]{0:T(128)} %slice.31.vco_ref, bf16[1536,384]{1,0:T(8,128)(2,1)} %slice.52.q_ref, bf16[3840,768]{1,0:T(8,128)(2,1)} %pad_maximum_fusion.refs_0_.refs_1_.refs_2_.refs_3_.refs_4_.refs_5_.refs_6_.refs_7_, ...), custom_call_target="tpu_custom_call" | custom-call | flops 3623878656 | bytes 11796480 | tf_op jit(solution)/shard_map/pallas_call | solution.py:73
  296.4 3.9 %fusion.1 = bf16[1536,384]{1,0:T(8,128)(2,1)S(1)} fusion(bf16[1536,384]{1,0:T(8,128)(2,1)} %shard_map.101, s32[1536]{0:T(1024)S(1)} %copy-done.9), kind=kOutput, calls=%fused_computation.9 | convolution fusion | flops 1814298624 | bytes 2365440 | tf_op jit(solution)/shard_map/dot_general | solution.py:248
  300.4 37.7 %all_to_all.29.refs_0_.refs_1_.refs_2_.refs_3_ = bf16[32,48,384]{2,1,0:T(8,128)(2,1)} all-to-all(bf16[32,48,384]{2,1,0:T(8,128)(2,1)S(1)} %bitcast.23), channel_id=1, replica_groups=mesh['seq'=8,'head'=4] {'seq','head'}, dimensions={0} | all-to-all | bytes 2359296 | tf_op jit(solution)/shard_map/all_to_all | solution.py:251
  338.1 6.4 %shard_map.104 = bf16[384,3072]{1,0:T(8,128)(2,1)} custom-call(s32[32]{0:T(128)} %constant.47.clone.table_ref, bf16[32,48,384]{2,1,0:T(8,128)(2,1)} %all_to_all.29.refs_0_.refs_1_.refs_2_.refs_3_, bf16[32,48,384]{2,1,0:T(8,128)(2,1)} %all_to_all.29.refs_0_.refs_1_.refs_2_.refs_3_, bf16[32,48,384]{2,1,0:T(8,128)(2,1)} %all_to_all.29.refs_0_.refs_1_.refs_2_.refs_3_, ...), custom_call_target="tpu_custom_call" | custom-call | bytes 4718592 | tf_op jit(solution)/shard_map/pallas_call | solution.py:142
  344.4 4.6 %fusion.4 = bf16[384,3072]{1,0:T(8,128)(2,1)} fusion(bf16[384,3072]{1,0:T(8,128)(2,1)} %shard_map.104, s32[384]{0:T(512)S(1)} %get-tuple-element.6), kind=kOutput, calls=%fused_computation.15 | convolution fusion | flops 906117120 | bytes 4720128 | tf_op jit(solution)/shard_map/dot_general | solution.py:264
  (58 shorter events, 19.4 us)
Async XLA Ops:
  0.0 17.5 %copy-start = (bf16[384,3072]{1,0:T(8,128)(2,1)S(1)}, bf16[384,3072]{1,0:T(8,128)(2,1)}, u32[]{:S(2)}) copy-start(bf16[384,3072]{1,0:T(8,128)(2,1)} %param.11) | copy-start | bytes 7077892
  10.1 23.8 %all-to-all-start = ((s32[32,1,48]{2,1,0:T(1,128)}), s32[32,1,48]{2,1,0:T(1,128)S(1)}, u32[]{:S(2)}, u32[]{:S(2)}) async-start(s32[32,1,48]{2,1,0:T(1,128)} %bitcast.2), calls=%async_computation | async-start | bytes 32768 | tf_op jit(solution)/shard_map/all_to_all | solution.py:194
  17.5 2.9 copy-start.4
  20.4 2.8 copy-start.5
  33.9 0.6 copy-start.8
  34.5 85.7 %all-to-all-start.3 = ((bf16[32,48,1152]{2,1,0:T(8,128)(2,1)}), bf16[32,48,1152]{2,1,0:T(8,128)(2,1)}, u32[]{:S(2)}, u32[]{:S(2)}) async-start(bf16[32,48,1152]{2,1,0:T(8,128)(2,1)} %shard_map.102), calls=%async_computation.3 | async-start | bytes 7077888 | tf_op jit(solution)/shard_map/all_to_all | solution.py:239
  120.2 84.0 %all-to-all-start.1 = ((bf16[32,48,1152]{2,1,0:T(8,128)(2,1)}), bf16[32,48,1152]{2,1,0:T(8,128)(2,1)S(1)}, u32[]{:S(2)}, u32[]{:S(2)}) async-start(bf16[32,48,1152]{2,1,0:T(8,128)(2,1)} %shard_map.100), calls=%async_computation.1 | async-start | bytes 7077888 | tf_op jit(solution)/shard_map/all_to_all | solution.py:239
  137.6 0.6 copy-start.6
  149.1 12.9 %copy-start.2 = (s32[32]{0:T(128)S(1)}, s32[32]{0:T(128)}, u32[]{:S(2)}) copy-start(s32[32]{0:T(128)} %param.15) | copy-start | bytes 388
  153.2 67.6 %collective-permute-start.3 = (bf16[1152,768]{1,0:T(8,128)(2,1)}, bf16[1152,768]{1,0:T(8,128)(2,1)}, u32[]{:S(2)}, u32[]{:S(2)}) collective-permute-start(bf16[1152,768]{1,0:T(8,128)(2,1)} %get-tuple-element.11), channel_id=1, source_target_pairs={{0,4},{5,1},{2,6},{7,3},{4,12},{1,9},{6,14},{3,11},{12,8},{9,13},{... | collective-permute-start | bytes 5308424 | tf_op jit(solution)/shard_map/ppermute | solution.py:243
  158.1 62.7 %collective-permute-start.4 = (bf16[1152,768]{1,0:T(8,128)(2,1)}, bf16[1152,768]{1,0:T(8,128)(2,1)}, u32[]{:S(2)}, u32[]{:S(2)}) collective-permute-start(bf16[1152,768]{1,0:T(8,128)(2,1)} %get-tuple-element.12), channel_id=1, source_target_pairs={{4,0},{1,5},{6,2},{3,7},{12,4},{9,1},{14,6},{11,3},{8,12},{13,9},{... | collective-permute-start | bytes 5308424 | tf_op jit(solution)/shard_map/ppermute | solution.py:244
  159.4 3.9 %collective-permute-start = (s32[4,4]{1,0:T(4,128)}, s32[4,4]{1,0:T(4,128)}, u32[]{:S(2)}, u32[]{:S(2)}) collective-permute-start(s32[4,4]{1,0:T(4,128)} %param.14), channel_id=1, source_target_pairs={{0,0},{1,5},{2,2},{3,7},{4,4},{5,1},{6,6},{7,3},{8,12},{9,9},{10,1... | collective-permute-start | bytes 200 | tf_op jit(solution)/shard_map/ppermute | solution.py:203
  170.9 33.2 %copy-start.7 = (s32[2048]{0:T(1024)S(1)}, s32[2048]{0:T(1024)}, u32[]{:S(2)}) copy-start(s32[2048]{0:T(1024)} %copy-done.6) | copy-start | bytes 24580
  210.2 10.6 %slice-start = ((bf16[1536,1152]{1,0:T(8,128)(2,1)}), bf16[1536,768]{1,0:T(8,128)(2,1)S(1)}, s32[]{:S(2)}) async-start(bf16[1536,1152]{1,0:T(8,128)(2,1)} %gather_fusion.5), calls=%async_computation.5 | async-start | bytes 4718592 | tf_op jit(solution)/shard_map/slice | solution.py:242
  214.4 53.7 %collective-permute-start.1 = (bf16[1152,768]{1,0:T(8,128)(2,1)}, bf16[1152,768]{1,0:T(8,128)(2,1)}, u32[]{:S(2)}, u32[]{:S(2)}) collective-permute-start(bf16[1152,768]{1,0:T(8,128)(2,1)} %get-tuple-element.13), channel_id=1, source_target_pairs={{0,4},{5,1},{2,6},{7,3},{4,12},{1,9},{6,14},{3,11},{12,8},{9,13},{... | collective-permute-start | bytes 5308424 | tf_op jit(solution)/shard_map/ppermute | solution.py:243
  219.3 56.4 %collective-permute-start.2 = (bf16[1152,768]{1,0:T(8,128)(2,1)}, bf16[1152,768]{1,0:T(8,128)(2,1)}, u32[]{:S(2)}, u32[]{:S(2)}) collective-permute-start(bf16[1152,768]{1,0:T(8,128)(2,1)} %get-tuple-element.14), channel_id=1, source_target_pairs={{4,0},{1,5},{6,2},{3,7},{12,4},{9,1},{14,6},{11,3},{8,12},{13,9},{... | collective-permute-start | bytes 5308424 | tf_op jit(solution)/shard_map/ppermute | solution.py:244
  226.0 15.7 %copy-start.9 = (s32[1536]{0:T(1024)S(1)}, s32[1536]{0:T(1024)}, u32[]{:S(2)}) copy-start(s32[1536]{0:T(1024)} %sub.35) | copy-start | bytes 18436
  241.7 25.3 %copy-start.3 = (bf16[1536,1152]{1,0:T(8,128)(2,1)S(1)}, bf16[1536,1152]{1,0:T(8,128)(2,1)}, u32[]{:S(2)}) copy-start(bf16[1536,1152]{1,0:T(8,128)(2,1)} %gather_fusion.4) | copy-start | bytes 10616836
  246.8 53.5 %all-to-all-start.4 = ((bf16[32,48,384]{2,1,0:T(8,128)(2,1)}), bf16[32,48,384]{2,1,0:T(8,128)(2,1)}, u32[]{:S(2)}, u32[]{:S(2)}) async-start(bf16[32,48,384]{2,1,0:T(8,128)(2,1)} %bitcast.22), calls=%async_computation.4 | async-start | bytes 2359296 | tf_op jit(solution)/shard_map/all_to_all | solution.py:251
  268.2 7.5 %slice-start.1 = ((bf16[1536,1152]{1,0:T(8,128)(2,1)}), bf16[1536,768]{1,0:T(8,128)(2,1)S(1)}, s32[]{:S(2)}) async-start(bf16[1536,1152]{1,0:T(8,128)(2,1)} %gather_fusion.4), calls=%async_computation.6 | async-start | bytes 4718592 | tf_op jit(solution)/shard_map/slice | solution.py:242
  338.1 11.0 %copy-start.1 = (bf16[384,3072]{1,0:T(8,128)(2,1)S(1)}, bf16[384,3072]{1,0:T(8,128)(2,1)}, u32[]{:S(2)}) copy-start(bf16[384,3072]{1,0:T(8,128)(2,1)} %param.11) | copy-start | bytes 7077892

commit v10 on v9

--- a/solution.py
+++ b/solution.py
@@ -237,7 +237,12 @@
             send = jnp.concatenate([x[:, :, :, c, :] for x in rows_sorted], axis=3)
             send = jnp.swapaxes(send, 1, 2).reshape(devices, share, 3 * chunk_width)[send_blocks]
         got = lax.all_to_all(send, both, split_axis=0, concat_axis=0, tiled=True)
-        got_tile = got.reshape(tok_dev, 3 * chunk_width)[place]
+        if packable:
+            got_tile = lax.dot_general(
+                route, got.reshape(tok_dev, 3 * chunk_width), (((0,), (0,)), ((), ()))
+            )
+        else:
+            got_tile = got.reshape(tok_dev, 3 * chunk_width)[place]
         q_tile = got_tile[:, :chunk_width]
         kv_tile = got_tile[:, chunk_width:]
         from_left = lax.ppermute(kv_tile[tok_dev - rim :], both, to_right)

time: 351 us -> 340 us (0.969)
  local copies, waits for them, and re-layouts: 49.6 us -> 19.4 us
  waiting for transfers between devices: 113 us -> 136 us
  matrix products: 22.2 us -> 40.4 us
  starting transfers between devices: 51.9 us -> 34.8 us
  other arithmetic: 20.1 us -> 15.7 us
    all_to_all x2, waiting for transfers between devices: 105 us -> 125 us  [body(): got = lax.all_to_all(send, both, split_axis=0, concat_axis=0, tiled=True)]
    dot_general x0 -> x2, matrix products: none -> 18.3 us  [body(): lax.dot_general(route, got.reshape(tok_dev, 3 * chunk_width), (((0,), (0,...]
    gather x2 -> x0, local copies, waits for them, and re-layouts: 16.9 us -> none  [body(): got_tile = got.reshape(tok_dev, 3 * chunk_width)[place]]
    all_to_all x1, starting transfers between devices: 20.1 us -> 4.26 us  [body(): lax.all_to_all(outgoing, ('seq', 'head'), split_axis=0, concat_axis=0, ti...]
    ppermute x2, waiting for transfers between devices: 0.01 us -> 9.05 us  [body(): from_left = lax.ppermute(kv_tile[tok_dev - rim:], both, to_right)]
    ppermute x2, waiting for transfers between devices: 7.54 us -> 1.21 us  [body(): from_right = lax.ppermute(kv_tile[:rim], both, to_left)]
    scatter x1 -> x0, local copies, waits for them, and re-layouts: 6.32 us -> none  [body(): jnp.zeros((tok_dev,), jnp.int32).at[local]]
    slice x2, local copies, waits for them, and re-layouts: 8.28 us -> 4 us  [body(): from_left = lax.ppermute(kv_tile[tok_dev - rim:], both, to_right)]
  transfers between devices with their start and end apart: 9 -> 9, of which waited for: 3 -> 4; matrix products, arithmetic and copies ran while one was open for 22% -> 17% of each run, Pallas kernels for 13% -> 14%
where the time goes in v10:
time: 340 us; the launch traced here: 338 us
  waiting for transfers between devices  136 us (40%)
  Pallas kernels  53.2 us (16%)
  matrix products  40.4 us (12%)
  blocking collectives  37.6 us (11%)
  starting transfers between devices  34.8 us (10%)
  local copies, waits for them, and re-layouts  19.4 us (6%)
  other arithmetic  15.7 us (5%)
    all_to_all x2, waiting for transfers between devices, body(): got = lax.all_to_all(send, both, split_axis=0, concat_axis=0, tiled=True)  125 us
    all_to_all x1, blocking collectives, body(): lax.all_to_all(outgoing, ('seq', 'head'), split_axis=0, concat_axis=0, ti...  37.6 us
    pallas_call x2, Pallas kernels, attention(): pl.pallas_call(functools.partial(attn_kernel, win, tile, scale, heads_her...  31.2 us
    dot_general x2, matrix products, body(): lax.dot_general(route, got.reshape(tok_dev, 3 * chunk_width), (((0,), (0,...  18.3 us
    pallas_call x2, Pallas kernels, pack(): pl.pallas_call(functools.partial(pack_kernel, head_count, chunk_width, co...  15.7 us
    concatenate x2, other arithmetic, body(): kv_ext = jnp.concatenate([from_left, kv_tile, from_right], axis=0)  10.3 us
    all_to_all x2, starting transfers between devices, body(): got = lax.all_to_all(send, both, split_axis=0, concat_axis=0, tiled=True)  10.1 us
    ppermute x2, starting transfers between devices, body(): from_left = lax.ppermute(kv_tile[tok_dev - rim:], both, to_right)  9.73 us
  transfers between devices with their start and end apart: 9, of which 4 were waited for; matrix products, arithmetic and copies ran while one was open for 17% of the time, Pallas kernels for 14%

profile of v10, /device:TPU:0, one launch (start us, length us, event | category | flops | bytes accessed | tf_op | source)
XLA Modules:
  0.0 338.3 jit_solution(14801925434656910596)
XLA Ops:
  0.0 4.6 %sort.17 = (s32[384]{0:T(512)}, s32[384]{0:T(512)S(1)}) sort(s32[384]{0:T(512)} %param.13, s32[384]{0:T(512)S(1)} %iota.16), dimensions={0}, to_apply=%region_0.0 | sort | flops 3456 | bytes 6144 | tf_op jit(solution)/shard_map/jit(argsort)/sort | solution.py:190
  4.6 3.6 %gather_fusion = s32[384]{0:T(512)S(1)} fusion(s32[384]{0:T(512)} %param.13, s32[1024]{0:T(1024)S(1)} %pad_clamp_fusion.3), kind=kCustom, calls=%fused_computation | custom fusion | bytes 4608 | tf_op jit(solution)/shard_map/gather | solution.py:191
  10.1 7.3 %all-to-all-start = ((s32[32,1,48]{2,1,0:T(1,128)}), s32[32,1,48]{2,1,0:T(1,128)S(1)}, u32[]{:S(2)}, u32[]{:S(2)}) async-start(s32[32,1,48]{2,1,0:T(1,128)} %bitcast.2), calls=%async_computation | async-start | bytes 32768 | tf_op jit(solution)/shard_map/all_to_all | solution.py:194
  17.5 2.9 fusion.10.refs_4_.refs_5_.refs_6_.refs_7_
  20.4 2.8 fusion.9.refs_8_.refs_9_.refs_10_.refs_11_
  23.3 2.8 fusion.11.refs_0_.refs_1_.refs_2_.refs_3_
  26.1 7.9 %shard_map.102 = bf16[32,48,1152]{2,1,0:T(8,128)(2,1)} custom-call(s32[32]{0:T(128)} %constant.43.clone.table_ref, bf16[384,3072]{1,0:T(8,128)(2,1)} %fusion.11.refs_0_.refs_1_.refs_2_.refs_3_, bf16[384,3072]{1,0:T(8,128)(2,1)} %fusion.11.refs_0_.refs_1_.refs_2_.refs_3_, bf16[384,3072]{1,0:T(8,128)(2,1)} %fusion.11.refs_0_.refs_1_.refs_2_.refs_3_, ...), custom_call_target="tpu_custom_call" | custom-call | bytes 7077888 | tf_op jit(solution)/shard_map/pallas_call | solution.py:106
  34.0 6.0 %all-to-all-start.3 = ((bf16[32,48,1152]{2,1,0:T(8,128)(2,1)}), bf16[32,48,1152]{2,1,0:T(8,128)(2,1)}, u32[]{:S(2)}, u32[]{:S(2)}) async-start(bf16[32,48,1152]{2,1,0:T(8,128)(2,1)} %shard_map.102), calls=%async_computation.3 | async-start | bytes 7077888 | tf_op jit(solution)/shard_map/all_to_all | solution.py:239
  39.9 7.8 %shard_map.100 = bf16[32,48,1152]{2,1,0:T(8,128)(2,1)} custom-call(s32[32]{0:T(128)} %constant.43.clone.table_ref, bf16[384,3072]{1,0:T(8,128)(2,1)} %fusion.11.refs_0_.refs_1_.refs_2_.refs_3_, bf16[384,3072]{1,0:T(8,128)(2,1)} %fusion.11.refs_0_.refs_1_.refs_2_.refs_3_, bf16[384,3072]{1,0:T(8,128)(2,1)} %fusion.11.refs_0_.refs_1_.refs_2_.refs_3_, ...), custom_call_target="tpu_custom_call" | custom-call | bytes 7077888 | tf_op jit(solution)/shard_map/pallas_call | solution.py:106
  47.8 71.9 %all-to-all-done.3 = bf16[32,48,1152]{2,1,0:T(8,128)(2,1)} async-done(((bf16[32,48,1152]{2,1,0:T(8,128)(2,1)}), bf16[32,48,1152]{2,1,0:T(8,128)(2,1)}, u32[]{:S(2)}, u32[]{:S(2)}) %all-to-all-start.3) | async-done | bytes 3538976 | tf_op jit(solution)/shard_map/all_to_all | solution.py:239
  119.6 4.2 %all-to-all-start.1 = ((bf16[32,48,1152]{2,1,0:T(8,128)(2,1)}), bf16[32,48,1152]{2,1,0:T(8,128)(2,1)}, u32[]{:S(2)}, u32[]{:S(2)}) async-start(bf16[32,48,1152]{2,1,0:T(8,128)(2,1)} %shard_map.100), calls=%async_computation.1 | async-start | bytes 7077888 | tf_op jit(solution)/shard_map/all_to_all | solution.py:239
  130.5 9.1 %fusion.1 = bf16[1536,1152]{1,0:T(8,128)(2,1)S(1)} fusion(bf16[1536,1152]{1,0:T(8,128)(2,1)} %bitcast.8, s32[1536]{0:T(1024)S(1)} %sub.26), kind=kOutput, calls=%fused_computation.6 | convolution fusion | flops 5438177280 | bytes 7084032 | tf_op jit(solution)/shard_map/dot_general | solution.py:241
  142.0 2.0 fusion.17
  144.0 4.8 %collective-permute-start.3 = (bf16[1152,768]{1,0:T(8,128)(2,1)}, bf16[1152,768]{1,0:T(8,128)(2,1)}, u32[]{:S(2)}, u32[]{:S(2)}) collective-permute-start(bf16[1152,768]{1,0:T(8,128)(2,1)} %get-tuple-element.9), channel_id=1, source_target_pairs={{0,4},{5,1},{2,6},{7,3},{4,12},{1,9},{6,14},{3,11},{12,8},{9,13},{... | collective-permute-start | bytes 5308424 | tf_op jit(solution)/shard_map/ppermute | solution.py:248
  148.8 1.5 collective-permute-start.4
  150.3 53.5 %all-to-all-done.1 = bf16[32,48,1152]{2,1,0:T(8,128)(2,1)} async-done(((bf16[32,48,1152]{2,1,0:T(8,128)(2,1)}), bf16[32,48,1152]{2,1,0:T(8,128)(2,1)}, u32[]{:S(2)}, u32[]{:S(2)}) %all-to-all-start.1) | async-done | bytes 3538976 | tf_op jit(solution)/shard_map/all_to_all | solution.py:239
  203.7 9.1 %fusion.3 = bf16[1536,1152]{1,0:T(8,128)(2,1)S(1)} fusion(bf16[1536,1152]{1,0:T(8,128)(2,1)} %bitcast.6, s32[1536]{0:T(1024)S(1)} %sub.26), kind=kOutput, calls=%fused_computation.8 | convolution fusion | flops 5438177280 | bytes 7084032 | tf_op jit(solution)/shard_map/dot_general | solution.py:241
  212.9 2.0 fusion.18
  216.0 4.9 %collective-permute-start.1 = (bf16[1152,768]{1,0:T(8,128)(2,1)}, bf16[1152,768]{1,0:T(8,128)(2,1)}, u32[]{:S(2)}, u32[]{:S(2)}) collective-permute-start(bf16[1152,768]{1,0:T(8,128)(2,1)} %get-tuple-element.11), channel_id=1, source_target_pairs={{0,4},{5,1},{2,6},{7,3},{4,12},{1,9},{6,14},{3,11},{12,8},{9,13},{... | collective-permute-start | bytes 5308424 | tf_op jit(solution)/shard_map/ppermute | solution.py:248
  221.0 1.3 collective-permute-start.2
  222.3 5.1 %pad_maximum_fusion.1.refs_0_.refs_1_.refs_2_.refs_3_.refs_4_.refs_5_.refs_6_.refs_7_ = bf16[3840,768]{1,0:T(8,128)(2,1)} fusion(bf16[1152,768]{1,0:T(8,128)(2,1)} %collective-permute-done.4, bf16[1536,768]{1,0:T(8,128)(2,1)S(1)} %slice-done.1, bf16[1152,768]{1,0:T(8,128)(2,1)} %collective-permute-done.3), kind=kLoop, calls=%fused_computation.10 | loop fusion | flops 17694720 | bytes 11796480 | tf_op jit(solution)/shard_map/concatenate | solution.py:250
  227.4 15.6 %shard_map.103 = bf16[1536,384]{1,0:T(8,128)(2,1)} custom-call(s32[16]{0:T(128)} %reshape.60.win_ref, s32[16]{0:T(128)} %gather_fusion.3, s32[4]{0:T(128)} %slice.31.vco_ref, bf16[1536,384]{1,0:T(8,128)(2,1)} %slice.52.q_ref, bf16[3840,768]{1,0:T(8,128)(2,1)} %pad_maximum_fusion.1.refs_0_.refs_1_.refs_2_.refs_3_.refs_4_.refs_5_.refs_6_.refs_7_, ...), custom_call_target="tpu_custom_call" | custom-call | flops 3623878656 | bytes 11796480 | tf_op jit(solution)/shard_map/pallas_call | solution.py:73
  243.0 5.0 %fusion = bf16[1536,384]{1,0:T(8,128)(2,1)} fusion(bf16[1536,384]{1,0:T(8,128)(2,1)} %shard_map.103, s32[1536]{0:T(1024)S(1)} %sub.26), kind=kOutput, calls=%fused_computation.5 | convolution fusion | flops 1814298624 | bytes 2365440 | tf_op jit(solution)/shard_map/dot_general | solution.py:253
  248.0 4.3 %all-to-all-start.4 = ((bf16[32,48,384]{2,1,0:T(8,128)(2,1)}), bf16[32,48,384]{2,1,0:T(8,128)(2,1)S(1)}, u32[]{:S(2)}, u32[]{:S(2)}) async-start(bf16[32,48,384]{2,1,0:T(8,128)(2,1)} %bitcast.9), calls=%async_computation.4 | async-start | bytes 2359296 | tf_op jit(solution)/shard_map/all_to_all | solution.py:256
  252.2 2.4 slice.48.q_ref
  254.7 9.0 %collective-permute-done.1 = bf16[1152,768]{1,0:T(8,128)(2,1)} collective-permute-done((bf16[1152,768]{1,0:T(8,128)(2,1)}, bf16[1152,768]{1,0:T(8,128)(2,1)}, u32[]{:S(2)}, u32[]{:S(2)}) %collective-permute-start.1) | collective-permute-done | bytes 1769504 | tf_op jit(solution)/shard_map/ppermute | solution.py:248
  264.9 5.2 %pad_maximum_fusion.refs_0_.refs_1_.refs_2_.refs_3_.refs_4_.refs_5_.refs_6_.refs_7_ = bf16[3840,768]{1,0:T(8,128)(2,1)} fusion(bf16[1152,768]{1,0:T(8,128)(2,1)} %collective-permute-done.2, bf16[1536,768]{1,0:T(8,128)(2,1)S(1)} %slice-done, bf16[1152,768]{1,0:T(8,128)(2,1)} %collective-permute-done.1), kind=kLoop, calls=%fused_computation.9 | loop fusion | flops 17694720 | bytes 11796480 | tf_op jit(solution)/shard_map/concatenate | solution.py:250
  270.1 15.6 %shard_map.101 = bf16[1536,384]{1,0:T(8,128)(2,1)} custom-call(s32[16]{0:T(128)} %reshape.60.win_ref, s32[16]{0:T(128)} %gather_fusion.3, s32[4]{0:T(128)} %slice.31.vco_ref, bf16[1536,384]{1,0:T(8,128)(2,1)} %slice.48.q_ref, bf16[3840,768]{1,0:T(8,128)(2,1)} %pad_maximum_fusion.refs_0_.refs_1_.refs_2_.refs_3_.refs_4_.refs_5_.refs_6_.refs_7_, ...), custom_call_target="tpu_custom_call" | custom-call | flops 3623878656 | bytes 11796480 | tf_op jit(solution)/shard_map/pallas_call | solution.py:73
  285.7 4.0 %fusion.2 = bf16[1536,384]{1,0:T(8,128)(2,1)S(1)} fusion(bf16[1536,384]{1,0:T(8,128)(2,1)} %shard_map.101, s32[1536]{0:T(1024)S(1)} %sub.26), kind=kOutput, calls=%fused_computation.7 | convolution fusion | flops 1814298624 | bytes 2365440 | tf_op jit(solution)/shard_map/dot_general | solution.py:253
  289.7 37.6 %all_to_all.29.refs_0_.refs_1_.refs_2_.refs_3_ = bf16[32,48,384]{2,1,0:T(8,128)(2,1)} all-to-all(bf16[32,48,384]{2,1,0:T(8,128)(2,1)S(1)} %bitcast.21), channel_id=1, replica_groups=mesh['seq'=8,'head'=4] {'seq','head'}, dimensions={0} | all-to-all | bytes 2359296 | tf_op jit(solution)/shard_map/all_to_all | solution.py:256
  327.3 6.4 %shard_map.104 = bf16[384,3072]{1,0:T(8,128)(2,1)} custom-call(s32[32]{0:T(128)} %constant.44.clone.table_ref, bf16[32,48,384]{2,1,0:T(8,128)(2,1)} %all_to_all.29.refs_0_.refs_1_.refs_2_.refs_3_, bf16[32,48,384]{2,1,0:T(8,128)(2,1)} %all_to_all.29.refs_0_.refs_1_.refs_2_.refs_3_, bf16[32,48,384]{2,1,0:T(8,128)(2,1)} %all_to_all.29.refs_0_.refs_1_.refs_2_.refs_3_, ...), custom_call_target="tpu_custom_call" | custom-call | bytes 4718592 | tf_op jit(solution)/shard_map/pallas_call | solution.py:142
  333.7 4.6 %fusion.8 = bf16[384,3072]{1,0:T(8,128)(2,1)} fusion(bf16[384,3072]{1,0:T(8,128)(2,1)} %shard_map.104, s32[384]{0:T(512)S(1)} %get-tuple-element.6), kind=kOutput, calls=%fused_computation.16 | convolution fusion | flops 906117120 | bytes 4720128 | tf_op jit(solution)/shard_map/dot_general | solution.py:269
  (49 shorter events, 12.0 us)
Async XLA Ops:
  0.0 17.5 %copy-start = (bf16[384,3072]{1,0:T(8,128)(2,1)S(1)}, bf16[384,3072]{1,0:T(8,128)(2,1)}, u32[]{:S(2)}) copy-start(bf16[384,3072]{1,0:T(8,128)(2,1)} %param.11) | copy-start | bytes 7077892
  10.1 23.8 %all-to-all-start = ((s32[32,1,48]{2,1,0:T(1,128)}), s32[32,1,48]{2,1,0:T(1,128)S(1)}, u32[]{:S(2)}, u32[]{:S(2)}) async-start(s32[32,1,48]{2,1,0:T(1,128)} %bitcast.2), calls=%async_computation | async-start | bytes 32768 | tf_op jit(solution)/shard_map/all_to_all | solution.py:194
  17.5 2.9 copy-start.6
  20.4 2.9 copy-start.7
  34.0 85.7 %all-to-all-start.3 = ((bf16[32,48,1152]{2,1,0:T(8,128)(2,1)}), bf16[32,48,1152]{2,1,0:T(8,128)(2,1)}, u32[]{:S(2)}, u32[]{:S(2)}) async-start(bf16[32,48,1152]{2,1,0:T(8,128)(2,1)} %shard_map.102), calls=%async_computation.3 | async-start | bytes 7077888 | tf_op jit(solution)/shard_map/all_to_all | solution.py:239
  47.7 76.1 %copy-start.8 = (s32[4,4]{1,0:T(4,128)S(1)}, s32[4,4]{1,0:T(4,128)}, u32[]{:S(2)}) copy-start(s32[4,4]{1,0:T(4,128)} %param.14) | copy-start | bytes 196
  47.8 79.4 %copy-start.2 = (s32[32]{0:T(128)S(1)}, s32[32]{0:T(128)}, u32[]{:S(2)}) copy-start(s32[32]{0:T(128)} %param.15) | copy-start | bytes 388
  119.6 84.1 %all-to-all-start.1 = ((bf16[32,48,1152]{2,1,0:T(8,128)(2,1)}), bf16[32,48,1152]{2,1,0:T(8,128)(2,1)}, u32[]{:S(2)}, u32[]{:S(2)}) async-start(bf16[32,48,1152]{2,1,0:T(8,128)(2,1)} %shard_map.100), calls=%async_computation.1 | async-start | bytes 7077888 | tf_op jit(solution)/shard_map/all_to_all | solution.py:239
  123.8 4.5 %collective-permute-start = (s32[4,4]{1,0:T(4,128)S(1)}, s32[4,4]{1,0:T(4,128)S(1)}, u32[]{:S(2)}, u32[]{:S(2)}) collective-permute-start(s32[4,4]{1,0:T(4,128)S(1)} %copy-done.8), channel_id=1, source_target_pairs={{0,0},{1,5},{2,2},{3,7},{4,4},{5,1},{6,6},{7,3},{8,12},{9,9},{10,1... | collective-permute-start | bytes 200 | tf_op jit(solution)/shard_map/ppermute | solution.py:203
  139.7 2.3 copy-start.5
  144.0 78.3 %collective-permute-start.3 = (bf16[1152,768]{1,0:T(8,128)(2,1)}, bf16[1152,768]{1,0:T(8,128)(2,1)}, u32[]{:S(2)}, u32[]{:S(2)}) collective-permute-start(bf16[1152,768]{1,0:T(8,128)(2,1)} %get-tuple-element.9), channel_id=1, source_target_pairs={{0,4},{5,1},{2,6},{7,3},{4,12},{1,9},{6,14},{3,11},{12,8},{9,13},{... | collective-permute-start | bytes 5308424 | tf_op jit(solution)/shard_map/ppermute | solution.py:248
  148.8 73.5 %collective-permute-start.4 = (bf16[1152,768]{1,0:T(8,128)(2,1)}, bf16[1152,768]{1,0:T(8,128)(2,1)}, u32[]{:S(2)}, u32[]{:S(2)}) collective-permute-start(bf16[1152,768]{1,0:T(8,128)(2,1)} %get-tuple-element.10), channel_id=1, source_target_pairs={{4,0},{1,5},{6,2},{3,7},{12,4},{9,1},{14,6},{11,3},{8,12},{13,9},{... | collective-permute-start | bytes 5308424 | tf_op jit(solution)/shard_map/ppermute | solution.py:249
  212.9 3.2 copy-start.4
  212.9 9.4 %slice-start.1 = ((bf16[1536,1152]{1,0:T(8,128)(2,1)}), bf16[1536,768]{1,0:T(8,128)(2,1)S(1)}, s32[]{:S(2)}) async-start(bf16[1536,1152]{1,0:T(8,128)(2,1)} %copy-done.5), calls=%async_computation.6 | async-start | bytes 4718592 | tf_op jit(solution)/shard_map/slice | solution.py:247
  216.0 47.7 %collective-permute-start.1 = (bf16[1152,768]{1,0:T(8,128)(2,1)}, bf16[1152,768]{1,0:T(8,128)(2,1)}, u32[]{:S(2)}, u32[]{:S(2)}) collective-permute-start(bf16[1152,768]{1,0:T(8,128)(2,1)} %get-tuple-element.11), channel_id=1, source_target_pairs={{0,4},{5,1},{2,6},{7,3},{4,12},{1,9},{6,14},{3,11},{12,8},{9,13},{... | collective-permute-start | bytes 5308424 | tf_op jit(solution)/shard_map/ppermute | solution.py:248
  221.0 43.9 %collective-permute-start.2 = (bf16[1152,768]{1,0:T(8,128)(2,1)}, bf16[1152,768]{1,0:T(8,128)(2,1)}, u32[]{:S(2)}, u32[]{:S(2)}) collective-permute-start(bf16[1152,768]{1,0:T(8,128)(2,1)} %get-tuple-element.12), channel_id=1, source_target_pairs={{4,0},{1,5},{6,2},{3,7},{12,4},{9,1},{14,6},{11,3},{8,12},{13,9},{... | collective-permute-start | bytes 5308424 | tf_op jit(solution)/shard_map/ppermute | solution.py:249
  248.0 41.7 %all-to-all-start.4 = ((bf16[32,48,384]{2,1,0:T(8,128)(2,1)}), bf16[32,48,384]{2,1,0:T(8,128)(2,1)S(1)}, u32[]{:S(2)}, u32[]{:S(2)}) async-start(bf16[32,48,384]{2,1,0:T(8,128)(2,1)} %bitcast.9), calls=%async_computation.4 | async-start | bytes 2359296 | tf_op jit(solution)/shard_map/all_to_all | solution.py:256
  254.7 10.3 %slice-start = ((bf16[1536,1152]{1,0:T(8,128)(2,1)}), bf16[1536,768]{1,0:T(8,128)(2,1)S(1)}, s32[]{:S(2)}) async-start(bf16[1536,1152]{1,0:T(8,128)(2,1)} %copy-done.4), calls=%async_computation.5 | async-start | bytes 4718592 | tf_op jit(solution)/shard_map/slice | solution.py:247
  289.7 37.6 %copy-start.3 = (bf16[32,48,384]{2,1,0:T(8,128)(2,1)}, bf16[32,48,384]{2,1,0:T(8,128)(2,1)S(1)}, u32[]{:S(2)}) copy-start(bf16[32,48,384]{2,1,0:T(8,128)(2,1)S(1)} %all-to-all-done.4.refs_4_.refs_5_.refs_6_.refs_7_) | copy-start | bytes 3538948
  327.3 11.0 %copy-start.1 = (bf16[384,3072]{1,0:T(8,128)(2,1)S(1)}, bf16[384,3072]{1,0:T(8,128)(2,1)}, u32[]{:S(2)}) copy-start(bf16[384,3072]{1,0:T(8,128)(2,1)} %param.11) | copy-start | bytes 7077892

commit v11 on v10

--- a/solution.py
+++ b/solution.py
@@ -188,7 +188,9 @@
     send_blocks = jnp.array(send_blocks, jnp.int32)
     back_blocks = jnp.array(back_blocks, jnp.int32)
     send_order = jnp.argsort(raster_to_tile)
-    slots_sorted = raster_to_tile[send_order].reshape(seq_count, share)
+    rank = jnp.sum((raster_to_tile[None, :] < raster_to_tile[:, None]).astype(jnp.int32), axis=1)
+    chosen = rank[None, :] == jnp.arange(rows_here, dtype=jnp.int32)[:, None]
+    slots_sorted = jnp.sum(jnp.where(chosen, raster_to_tile[None, :], 0), axis=1).reshape(seq_count, share)
     slot_send = jnp.broadcast_to(slots_sorted[:, None, :], (seq_count, head_count, share))
     slot_send = slot_send.reshape(devices, share)[send_blocks]
     slot_in = lax.all_to_all(
@@ -222,7 +224,7 @@
 
     packable = share % 16 == 0
     if packable:
-        pick = (send_order[:, None] == jnp.arange(rows_here, dtype=jnp.int32)[None, :]).astype(query.dtype)
+        pick = chosen.astype(query.dtype)
         rows_flat = [jnp.dot(pick, x) for x in (query, key, value)]
     else:
         rows_sorted = [

time: 340 us -> 334 us (0.982)
  local copies, waits for them, and re-layouts: 19.4 us -> 15.6 us
    sort x1 -> x0, other arithmetic: 4.6 us -> none  [body(): send_order = jnp.argsort(raster_to_tile)]
    gather x1 -> x0, local copies, waits for them, and re-layouts: 3.62 us -> none  [body(): slots_sorted = raster_to_tile[send_order].reshape(seq_count, share)]
  transfers between devices with their start and end apart: 9 -> 9, of which waited for: 4 -> 4; matrix products, arithmetic and copies ran while one was open for 17% -> 18% of each run, Pallas kernels for 14% -> 14%
where the time goes in v11:
time: 334 us; the launch traced here: 332 us
  waiting for transfers between devices  136 us (41%)
  Pallas kernels  53.3 us (16%)
  matrix products  40.1 us (12%)
  blocking collectives  37.7 us (11%)
  starting transfers between devices  34.8 us (10%)
  local copies, waits for them, and re-layouts  15.6 us (5%)
  other arithmetic  12.9 us (4%)
    all_to_all x2, waiting for transfers between devices, body(): got = lax.all_to_all(send, both, split_axis=0, concat_axis=0, tiled=True)  125 us
    all_to_all x1, blocking collectives, body(): lax.all_to_all(outgoing, ('seq', 'head'), split_axis=0, concat_axis=0, ti...  37.7 us
    pallas_call x2, Pallas kernels, attention(): pl.pallas_call(functools.partial(attn_kernel, win, tile, scale, heads_her...  31.2 us
    dot_general x2, matrix products, body(): lax.dot_general(route, got.reshape(tok_dev, 3 * chunk_width), (((0,), (0,...  18.3 us
    pallas_call x2, Pallas kernels, pack(): pl.pallas_call(functools.partial(pack_kernel, head_count, chunk_width, co...  15.7 us
    concatenate x2, other arithmetic, body(): kv_ext = jnp.concatenate([from_left, kv_tile, from_right], axis=0)  10.3 us
    all_to_all x2, starting transfers between devices, body(): got = lax.all_to_all(send, both, split_axis=0, concat_axis=0, tiled=True)  10.1 us
    ppermute x2, starting transfers between devices, body(): from_left = lax.ppermute(kv_tile[tok_dev - rim:], both, to_right)  9.74 us
  transfers between devices with their start and end apart: 9, of which 4 were waited for; matrix products, arithmetic and copies ran while one was open for 18% of the time, Pallas kernels for 14%

profile of v11, /device:TPU:0, one launch (start us, length us, event | category | flops | bytes accessed | tf_op | source)
XLA Modules:
  0.0 331.5 jit_solution(80322746923804317)
XLA Ops:
  3.8 7.3 %all-to-all-start = ((s32[32,1,48]{2,1,0:T(1,128)}), s32[32,1,48]{2,1,0:T(1,128)S(1)}, u32[]{:S(2)}, u32[]{:S(2)}) async-start(s32[32,1,48]{2,1,0:T(1,128)} %bitcast.2), calls=%async_computation | async-start | bytes 32768 | tf_op jit(solution)/shard_map/all_to_all | solution.py:196
  11.2 2.8 fusion.9.refs_8_.refs_9_.refs_10_.refs_11_
  14.0 2.8 fusion.10.refs_4_.refs_5_.refs_6_.refs_7_
  16.8 2.8 fusion.11.refs_0_.refs_1_.refs_2_.refs_3_
  19.6 7.9 %shard_map.102 = bf16[32,48,1152]{2,1,0:T(8,128)(2,1)} custom-call(s32[32]{0:T(128)} %constant.40.clone.table_ref, bf16[384,3072]{1,0:T(8,128)(2,1)} %fusion.11.refs_0_.refs_1_.refs_2_.refs_3_, bf16[384,3072]{1,0:T(8,128)(2,1)} %fusion.11.refs_0_.refs_1_.refs_2_.refs_3_, bf16[384,3072]{1,0:T(8,128)(2,1)} %fusion.11.refs_0_.refs_1_.refs_2_.refs_3_, ...), custom_call_target="tpu_custom_call" | custom-call | bytes 7077888 | tf_op jit(solution)/shard_map/pallas_call | solution.py:106
  27.5 6.0 %all-to-all-start.3 = ((bf16[32,48,1152]{2,1,0:T(8,128)(2,1)}), bf16[32,48,1152]{2,1,0:T(8,128)(2,1)}, u32[]{:S(2)}, u32[]{:S(2)}) async-start(bf16[32,48,1152]{2,1,0:T(8,128)(2,1)} %shard_map.102), calls=%async_computation.3 | async-start | bytes 7077888 | tf_op jit(solution)/shard_map/all_to_all | solution.py:241
  33.4 7.9 %shard_map.100 = bf16[32,48,1152]{2,1,0:T(8,128)(2,1)} custom-call(s32[32]{0:T(128)} %constant.40.clone.table_ref, bf16[384,3072]{1,0:T(8,128)(2,1)} %fusion.11.refs_0_.refs_1_.refs_2_.refs_3_, bf16[384,3072]{1,0:T(8,128)(2,1)} %fusion.11.refs_0_.refs_1_.refs_2_.refs_3_, bf16[384,3072]{1,0:T(8,128)(2,1)} %fusion.11.refs_0_.refs_1_.refs_2_.refs_3_, ...), custom_call_target="tpu_custom_call" | custom-call | bytes 7077888 | tf_op jit(solution)/shard_map/pallas_call | solution.py:106
  41.3 71.8 %all-to-all-done.3 = bf16[32,48,1152]{2,1,0:T(8,128)(2,1)} async-done(((bf16[32,48,1152]{2,1,0:T(8,128)(2,1)}), bf16[32,48,1152]{2,1,0:T(8,128)(2,1)}, u32[]{:S(2)}, u32[]{:S(2)}) %all-to-all-start.3) | async-done | bytes 3538976 | tf_op jit(solution)/shard_map/all_to_all | solution.py:241
  113.2 4.2 %all-to-all-start.1 = ((bf16[32,48,1152]{2,1,0:T(8,128)(2,1)}), bf16[32,48,1152]{2,1,0:T(8,128)(2,1)}, u32[]{:S(2)}, u32[]{:S(2)}) async-start(bf16[32,48,1152]{2,1,0:T(8,128)(2,1)} %shard_map.100), calls=%async_computation.1 | async-start | bytes 7077888 | tf_op jit(solution)/shard_map/all_to_all | solution.py:241
  118.0 1.3 dynamic_slice.3
  123.9 9.1 %fusion.1 = bf16[1536,1152]{1,0:T(8,128)(2,1)S(1)} fusion(bf16[1536,1152]{1,0:T(8,128)(2,1)} %bitcast.8, s32[1536]{0:T(1024)S(1)} %sub.26), kind=kOutput, calls=%fused_computation.5 | convolution fusion | flops 5438177280 | bytes 7084032 | tf_op jit(solution)/shard_map/dot_general | solution.py:243
  133.1 1.3 slice.50.q_ref
  135.4 2.0 fusion.17
  137.4 4.8 %collective-permute-start.3 = (bf16[1152,768]{1,0:T(8,128)(2,1)}, bf16[1152,768]{1,0:T(8,128)(2,1)}, u32[]{:S(2)}, u32[]{:S(2)}) collective-permute-start(bf16[1152,768]{1,0:T(8,128)(2,1)} %get-tuple-element.7), channel_id=1, source_target_pairs={{0,4},{5,1},{2,6},{7,3},{4,12},{1,9},{6,14},{3,11},{12,8},{9,13},{... | collective-permute-start | bytes 5308424 | tf_op jit(solution)/shard_map/ppermute | solution.py:250
  142.2 1.5 collective-permute-start.4
  143.7 53.6 %all-to-all-done.1 = bf16[32,48,1152]{2,1,0:T(8,128)(2,1)} async-done(((bf16[32,48,1152]{2,1,0:T(8,128)(2,1)}), bf16[32,48,1152]{2,1,0:T(8,128)(2,1)}, u32[]{:S(2)}, u32[]{:S(2)}) %all-to-all-start.1) | async-done | bytes 3538976 | tf_op jit(solution)/shard_map/all_to_all | solution.py:241
  197.2 9.1 %fusion.3 = bf16[1536,1152]{1,0:T(8,128)(2,1)S(1)} fusion(bf16[1536,1152]{1,0:T(8,128)(2,1)} %bitcast.6, s32[1536]{0:T(1024)S(1)} %sub.26), kind=kOutput, calls=%fused_computation.7 | convolution fusion | flops 5438177280 | bytes 7084032 | tf_op jit(solution)/shard_map/dot_general | solution.py:243
  206.4 2.0 fusion.18
  209.5 4.9 %collective-permute-start.1 = (bf16[1152,768]{1,0:T(8,128)(2,1)}, bf16[1152,768]{1,0:T(8,128)(2,1)}, u32[]{:S(2)}, u32[]{:S(2)}) collective-permute-start(bf16[1152,768]{1,0:T(8,128)(2,1)} %get-tuple-element.9), channel_id=1, source_target_pairs={{0,4},{5,1},{2,6},{7,3},{4,12},{1,9},{6,14},{3,11},{12,8},{9,13},{... | collective-permute-start | bytes 5308424 | tf_op jit(solution)/shard_map/ppermute | solution.py:250
  214.5 1.3 collective-permute-start.2
  215.8 5.2 %pad_maximum_fusion.1.refs_0_.refs_1_.refs_2_.refs_3_.refs_4_.refs_5_.refs_6_.refs_7_ = bf16[3840,768]{1,0:T(8,128)(2,1)} fusion(bf16[1152,768]{1,0:T(8,128)(2,1)} %collective-permute-done.4, bf16[1536,768]{1,0:T(8,128)(2,1)S(1)} %slice-done.1, bf16[1152,768]{1,0:T(8,128)(2,1)} %collective-permute-done.3), kind=kLoop, calls=%fused_computation.9 | loop fusion | flops 17694720 | bytes 11796480 | tf_op jit(solution)/shard_map/concatenate | solution.py:252
  221.0 15.6 %shard_map.103 = bf16[1536,384]{1,0:T(8,128)(2,1)} custom-call(s32[16]{0:T(128)} %reshape.62.win_ref, s32[16]{0:T(128)} %gather_fusion.2, s32[4]{0:T(128)} %slice.31.vco_ref, bf16[1536,384]{1,0:T(8,128)(2,1)} %slice.50.q_ref, bf16[3840,768]{1,0:T(8,128)(2,1)} %pad_maximum_fusion.1.refs_0_.refs_1_.refs_2_.refs_3_.refs_4_.refs_5_.refs_6_.refs_7_, ...), custom_call_target="tpu_custom_call" | custom-call | flops 3623878656 | bytes 11796480 | tf_op jit(solution)/shard_map/pallas_call | solution.py:73
  236.6 5.0 %fusion = bf16[1536,384]{1,0:T(8,128)(2,1)} fusion(bf16[1536,384]{1,0:T(8,128)(2,1)} %shard_map.103, s32[1536]{0:T(1024)S(1)} %sub.26), kind=kOutput, calls=%fused_computation.4 | convolution fusion | flops 1814298624 | bytes 2365440 | tf_op jit(solution)/shard_map/dot_general | solution.py:255
  241.5 4.3 %all-to-all-start.4 = ((bf16[32,48,384]{2,1,0:T(8,128)(2,1)}), bf16[32,48,384]{2,1,0:T(8,128)(2,1)S(1)}, u32[]{:S(2)}, u32[]{:S(2)}) async-start(bf16[32,48,384]{2,1,0:T(8,128)(2,1)} %bitcast.9), calls=%async_computation.4 | async-start | bytes 2359296 | tf_op jit(solution)/shard_map/all_to_all | solution.py:258
  245.8 2.4 slice.46.q_ref
  248.2 8.9 %collective-permute-done.1 = bf16[1152,768]{1,0:T(8,128)(2,1)} collective-permute-done((bf16[1152,768]{1,0:T(8,128)(2,1)}, bf16[1152,768]{1,0:T(8,128)(2,1)}, u32[]{:S(2)}, u32[]{:S(2)}) %collective-permute-start.1) | collective-permute-done | bytes 1769504 | tf_op jit(solution)/shard_map/ppermute | solution.py:250
  258.3 5.1 %pad_maximum_fusion.refs_0_.refs_1_.refs_2_.refs_3_.refs_4_.refs_5_.refs_6_.refs_7_ = bf16[3840,768]{1,0:T(8,128)(2,1)} fusion(bf16[1152,768]{1,0:T(8,128)(2,1)} %collective-permute-done.2, bf16[1536,768]{1,0:T(8,128)(2,1)S(1)} %slice-done, bf16[1152,768]{1,0:T(8,128)(2,1)} %collective-permute-done.1), kind=kLoop, calls=%fused_computation.8 | loop fusion | flops 17694720 | bytes 11796480 | tf_op jit(solution)/shard_map/concatenate | solution.py:252
  263.4 15.6 %shard_map.101 = bf16[1536,384]{1,0:T(8,128)(2,1)} custom-call(s32[16]{0:T(128)} %reshape.62.win_ref, s32[16]{0:T(128)} %gather_fusion.2, s32[4]{0:T(128)} %slice.31.vco_ref, bf16[1536,384]{1,0:T(8,128)(2,1)} %slice.46.q_ref, bf16[3840,768]{1,0:T(8,128)(2,1)} %pad_maximum_fusion.refs_0_.refs_1_.refs_2_.refs_3_.refs_4_.refs_5_.refs_6_.refs_7_, ...), custom_call_target="tpu_custom_call" | custom-call | flops 3623878656 | bytes 11796480 | tf_op jit(solution)/shard_map/pallas_call | solution.py:73
  279.0 4.0 %fusion.2 = bf16[1536,384]{1,0:T(8,128)(2,1)S(1)} fusion(bf16[1536,384]{1,0:T(8,128)(2,1)} %shard_map.101, s32[1536]{0:T(1024)S(1)} %sub.26), kind=kOutput, calls=%fused_computation.6 | convolution fusion | flops 1814298624 | bytes 2365440 | tf_op jit(solution)/shard_map/dot_general | solution.py:255
  283.0 37.7 %all_to_all.29.refs_0_.refs_1_.refs_2_.refs_3_ = bf16[32,48,384]{2,1,0:T(8,128)(2,1)} all-to-all(bf16[32,48,384]{2,1,0:T(8,128)(2,1)S(1)} %bitcast.21), channel_id=1, replica_groups=mesh['seq'=8,'head'=4] {'seq','head'}, dimensions={0} | all-to-all | bytes 2359296 | tf_op jit(solution)/shard_map/all_to_all | solution.py:258
  320.6 6.4 %shard_map.104 = bf16[384,3072]{1,0:T(8,128)(2,1)} custom-call(s32[32]{0:T(128)} %constant.41.clone.table_ref, bf16[32,48,384]{2,1,0:T(8,128)(2,1)} %all_to_all.29.refs_0_.refs_1_.refs_2_.refs_3_, bf16[32,48,384]{2,1,0:T(8,128)(2,1)} %all_to_all.29.refs_0_.refs_1_.refs_2_.refs_3_, bf16[32,48,384]{2,1,0:T(8,128)(2,1)} %all_to_all.29.refs_0_.refs_1_.refs_2_.refs_3_, ...), custom_call_target="tpu_custom_call" | custom-call | bytes 4718592 | tf_op jit(solution)/shard_map/pallas_call | solution.py:142
  327.0 4.5 %fusion.8 = bf16[384,3072]{1,0:T(8,128)(2,1)} fusion(bf16[384,3072]{1,0:T(8,128)(2,1)} %shard_map.104, s32[384]{0:T(512)S(1)} %convert_reduce_fusion), kind=kOutput, calls=%fused_computation.16 | convolution fusion | flops 906117120 | bytes 4720128 | tf_op jit(solution)/shard_map/dot_general | solution.py:271
  (46 shorter events, 11.2 us)
Async XLA Ops:
  0.0 11.2 %copy-start = (bf16[384,3072]{1,0:T(8,128)(2,1)S(1)}, bf16[384,3072]{1,0:T(8,128)(2,1)}, u32[]{:S(2)}) copy-start(bf16[384,3072]{1,0:T(8,128)(2,1)} %param.12) | copy-start | bytes 7077892
  3.8 23.7 %all-to-all-start = ((s32[32,1,48]{2,1,0:T(1,128)}), s32[32,1,48]{2,1,0:T(1,128)S(1)}, u32[]{:S(2)}, u32[]{:S(2)}) async-start(s32[32,1,48]{2,1,0:T(1,128)} %bitcast.2), calls=%async_computation | async-start | bytes 32768 | tf_op jit(solution)/shard_map/all_to_all | solution.py:196
  11.2 2.8 copy-start.6
  14.0 2.9 copy-start.7
  27.5 85.7 %all-to-all-start.3 = ((bf16[32,48,1152]{2,1,0:T(8,128)(2,1)}), bf16[32,48,1152]{2,1,0:T(8,128)(2,1)}, u32[]{:S(2)}, u32[]{:S(2)}) async-start(bf16[32,48,1152]{2,1,0:T(8,128)(2,1)} %shard_map.102), calls=%async_computation.3 | async-start | bytes 7077888 | tf_op jit(solution)/shard_map/all_to_all | solution.py:241
  41.3 76.1 %copy-start.8 = (s32[4,4]{1,0:T(4,128)S(1)}, s32[4,4]{1,0:T(4,128)}, u32[]{:S(2)}) copy-start(s32[4,4]{1,0:T(4,128)} %param.14) | copy-start | bytes 196
  41.3 79.3 %copy-start.2 = (s32[32]{0:T(128)S(1)}, s32[32]{0:T(128)}, u32[]{:S(2)}) copy-start(s32[32]{0:T(128)} %param.15) | copy-start | bytes 388
  113.2 84.1 %all-to-all-start.1 = ((bf16[32,48,1152]{2,1,0:T(8,128)(2,1)}), bf16[32,48,1152]{2,1,0:T(8,128)(2,1)}, u32[]{:S(2)}, u32[]{:S(2)}) async-start(bf16[32,48,1152]{2,1,0:T(8,128)(2,1)} %shard_map.100), calls=%async_computation.1 | async-start | bytes 7077888 | tf_op jit(solution)/shard_map/all_to_all | solution.py:241
  117.4 4.6 %collective-permute-start = (s32[4,4]{1,0:T(4,128)S(1)}, s32[4,4]{1,0:T(4,128)S(1)}, u32[]{:S(2)}, u32[]{:S(2)}) collective-permute-start(s32[4,4]{1,0:T(4,128)S(1)} %copy-done.8), channel_id=1, source_target_pairs={{0,0},{1,5},{2,2},{3,7},{4,4},{5,1},{6,6},{7,3},{8,12},{9,9},{10,1... | collective-permute-start | bytes 200 | tf_op jit(solution)/shard_map/ppermute | solution.py:205
  133.1 2.3 copy-start.5
  137.4 78.4 %collective-permute-start.3 = (bf16[1152,768]{1,0:T(8,128)(2,1)}, bf16[1152,768]{1,0:T(8,128)(2,1)}, u32[]{:S(2)}, u32[]{:S(2)}) collective-permute-start(bf16[1152,768]{1,0:T(8,128)(2,1)} %get-tuple-element.7), channel_id=1, source_target_pairs={{0,4},{5,1},{2,6},{7,3},{4,12},{1,9},{6,14},{3,11},{12,8},{9,13},{... | collective-permute-start | bytes 5308424 | tf_op jit(solution)/shard_map/ppermute | solution.py:250
  142.2 73.6 %collective-permute-start.4 = (bf16[1152,768]{1,0:T(8,128)(2,1)}, bf16[1152,768]{1,0:T(8,128)(2,1)}, u32[]{:S(2)}, u32[]{:S(2)}) collective-permute-start(bf16[1152,768]{1,0:T(8,128)(2,1)} %get-tuple-element.8), channel_id=1, source_target_pairs={{4,0},{1,5},{6,2},{3,7},{12,4},{9,1},{14,6},{11,3},{8,12},{13,9},{... | collective-permute-start | bytes 5308424 | tf_op jit(solution)/shard_map/ppermute | solution.py:251
  206.4 3.2 copy-start.4
  206.4 9.4 %slice-start.1 = ((bf16[1536,1152]{1,0:T(8,128)(2,1)}), bf16[1536,768]{1,0:T(8,128)(2,1)S(1)}, s32[]{:S(2)}) async-start(bf16[1536,1152]{1,0:T(8,128)(2,1)} %copy-done.5), calls=%async_computation.6 | async-start | bytes 4718592 | tf_op jit(solution)/shard_map/slice | solution.py:249
  209.5 47.6 %collective-permute-start.1 = (bf16[1152,768]{1,0:T(8,128)(2,1)}, bf16[1152,768]{1,0:T(8,128)(2,1)}, u32[]{:S(2)}, u32[]{:S(2)}) collective-permute-start(bf16[1152,768]{1,0:T(8,128)(2,1)} %get-tuple-element.9), channel_id=1, source_target_pairs={{0,4},{5,1},{2,6},{7,3},{4,12},{1,9},{6,14},{3,11},{12,8},{9,13},{... | collective-permute-start | bytes 5308424 | tf_op jit(solution)/shard_map/ppermute | solution.py:250
  214.5 43.8 %collective-permute-start.2 = (bf16[1152,768]{1,0:T(8,128)(2,1)}, bf16[1152,768]{1,0:T(8,128)(2,1)}, u32[]{:S(2)}, u32[]{:S(2)}) collective-permute-start(bf16[1152,768]{1,0:T(8,128)(2,1)} %get-tuple-element.10), channel_id=1, source_target_pairs={{4,0},{1,5},{6,2},{3,7},{12,4},{9,1},{14,6},{11,3},{8,12},{13,9},{... | collective-permute-start | bytes 5308424 | tf_op jit(solution)/shard_map/ppermute | solution.py:251
  241.5 41.4 %all-to-all-start.4 = ((bf16[32,48,384]{2,1,0:T(8,128)(2,1)}), bf16[32,48,384]{2,1,0:T(8,128)(2,1)S(1)}, u32[]{:S(2)}, u32[]{:S(2)}) async-start(bf16[32,48,384]{2,1,0:T(8,128)(2,1)} %bitcast.9), calls=%async_computation.4 | async-start | bytes 2359296 | tf_op jit(solution)/shard_map/all_to_all | solution.py:258
  248.2 10.1 %slice-start = ((bf16[1536,1152]{1,0:T(8,128)(2,1)}), bf16[1536,768]{1,0:T(8,128)(2,1)S(1)}, s32[]{:S(2)}) async-start(bf16[1536,1152]{1,0:T(8,128)(2,1)} %copy-done.4), calls=%async_computation.5 | async-start | bytes 4718592 | tf_op jit(solution)/shard_map/slice | solution.py:249
  283.0 37.7 %copy-start.3 = (bf16[32,48,384]{2,1,0:T(8,128)(2,1)}, bf16[32,48,384]{2,1,0:T(8,128)(2,1)S(1)}, u32[]{:S(2)}) copy-start(bf16[32,48,384]{2,1,0:T(8,128)(2,1)S(1)} %all-to-all-done.4.refs_4_.refs_5_.refs_6_.refs_7_) | copy-start | bytes 3538948
  320.6 10.9 %copy-start.1 = (bf16[384,3072]{1,0:T(8,128)(2,1)S(1)}, bf16[384,3072]{1,0:T(8,128)(2,1)}, u32[]{:S(2)}) copy-start(bf16[384,3072]{1,0:T(8,128)(2,1)} %param.12) | copy-start | bytes 7077892
